TPU v7x, 256 devices: a whole 4x4x8 slice. The times are simulated.
256 devices in a mesh: wave: 8 (over z_lo, y), tile: 32 (over x, z_hi, core).
Axes of the slice: x: 4, y: 4, z: 8 (z_hi: 4, z_lo: 2; z = z_hi * 2 + z_lo), core: 2. Of those that a mesh axis runs over, the one named last changes fastest.
Arguments:
- coefficients: bfloat16 [512, 256, 4096], P('tile', 'wave'), may hold values from -2.09375 to 2.09375
- profile_basis: bfloat16 [4096, 512], replicated, may hold values from -0.26367188 to 0.26367188
- point_spread: bfloat16 [17, 17], replicated, may hold values from 0.0009994507 to 0.0099487305
- observed: bfloat16 [512, 512, 256], P(None, 'tile', 'wave'), may hold values from -6 to 6
Outputs:
- coef_grad: bfloat16 [512, 256, 4096], P('tile', 'wave')
All inputs are finite; a program needn't handle non-finite values.
Results may differ from a plain program's by a relative error of at most 0.0058.
Values may be sent and summed in bfloat16 or wider, within the bound.
No kernel may reach another device: no remote copies, remote signals or barrier semaphores. Data moves between devices by JAX's collectives and lax.ppermute only.
A program may use at most 64 MiB of HBM per device.

v0:
```python
import jax
import jax.numpy as jnp
from jax import lax
from jax.sharding import PartitionSpec as P


def send(block, tile_step, wave_step):
    n_tile = lax.axis_size("tile")
    n_wave = lax.axis_size("wave")
    if wave_step == 0:
        pairs = [(t, t + tile_step) for t in range(n_tile) if 0 <= t + tile_step < n_tile]
        return lax.ppermute(block, "tile", pairs)
    if tile_step == 0:
        pairs = [(w, w + wave_step) for w in range(n_wave) if 0 <= w + wave_step < n_wave]
        return lax.ppermute(block, "wave", pairs)
    pairs = []
    for t in range(n_tile):
        for w in range(n_wave):
            t2, w2 = t + tile_step, w + wave_step
            if 0 <= t2 < n_tile and 0 <= w2 < n_wave:
                pairs.append((w * n_tile + t, w2 * n_tile + t2))
    return lax.ppermute(block, ("wave", "tile"), pairs)


def halo(block, h):
    rows, cols = block.shape[0], block.shape[1]
    low, high = block[rows - h :], block[:h]
    pieces = [
        send(low[:, cols - h :], 1, 1),
        send(low, 1, 0),
        send(low[:, :h], 1, -1),
        send(high[:, cols - h :], -1, 1),
        send(high, -1, 0),
        send(high[:, :h], -1, -1),
        send(block[:, cols - h :], 0, 1),
        send(block[:, :h], 0, -1),
    ]
    return jnp.concatenate([p.reshape(-1, p.shape[-1]) for p in pieces], axis=0)


def blur_mats(psf, rows, cols, h):
    k = psf.shape[0]
    win_rows, win_cols = rows + 2 * h, cols + 2 * h
    shape_c = (k, cols, win_cols)
    col_gap = lax.broadcasted_iota(jnp.int32, shape_c, 2) - lax.broadcasted_iota(jnp.int32, shape_c, 1)
    col_hot = (col_gap == lax.broadcasted_iota(jnp.int32, shape_c, 0)).astype(psf.dtype)
    col = jnp.einsum("ab,bxX->axX", psf, col_hot, preferred_element_type=jnp.float32).astype(psf.dtype)
    shape_r = (k, rows, win_rows)
    row_gap = lax.broadcasted_iota(jnp.int32, shape_r, 2) - lax.broadcasted_iota(jnp.int32, shape_r, 1)
    row_hot = (row_gap == lax.broadcasted_iota(jnp.int32, shape_r, 0)).astype(psf.dtype)
    full = jnp.einsum("ayY,axX->yxYX", row_hot, col, preferred_element_type=jnp.float32)
    full = full.astype(psf.dtype).reshape(rows * cols, win_rows, win_cols)
    center = full[:, h : h + rows, h : h + cols].reshape(rows * cols, rows * cols)
    top, bottom, mid = full[:, :h], full[:, h + rows :], full[:, h : h + rows]
    parts = [
        top[:, :, :h],
        top[:, :, h : h + cols],
        top[:, :, h + cols :],
        bottom[:, :, :h],
        bottom[:, :, h : h + cols],
        bottom[:, :, h + cols :],
        mid[:, :, :h],
        mid[:, :, h + cols :],
    ]
    side = jnp.concatenate([p.reshape(rows * cols, -1) for p in parts], axis=1)
    return center, side


def blur(field, mats, h):
    center, side = mats
    rows, cols, waves = field.shape
    flat = field.reshape(rows * cols, waves)
    near = halo(field, h)
    inner = jnp.dot(center, flat, preferred_element_type=jnp.float32)
    return inner + jnp.dot(side, near, preferred_element_type=jnp.float32)


def shards(coefficients, profile_basis, point_spread, observed):
    rows, cols, profiles = coefficients.shape
    waves = profile_basis.shape[1]
    h = point_spread.shape[0] // 2
    opacity = jnp.dot(
        coefficients.reshape(rows * cols, profiles), profile_basis, preferred_element_type=jnp.float32
    )
    spectra = jnp.exp(-opacity).astype(jnp.bfloat16)
    forward = blur_mats(point_spread, rows, cols, h)
    adjoint = blur_mats(point_spread[::-1, ::-1], rows, cols, h)
    blurred = blur(spectra.reshape(rows, cols, waves), forward, h)
    measured = observed.transpose(1, 2, 0).reshape(rows * cols, waves).astype(jnp.float32)
    residual = (blurred - measured).astype(jnp.bfloat16)
    adjoint_field = blur(residual.reshape(rows, cols, waves), adjoint, h)
    tau_grad = (-spectra.astype(jnp.float32) * adjoint_field).astype(jnp.bfloat16)
    coef_grad = lax.dot_general(
        tau_grad, profile_basis, (((1,), (1,)), ((), ())), preferred_element_type=jnp.float32
    )
    return coef_grad.astype(jnp.bfloat16).reshape(rows, cols, profiles)


def solution(mesh):
    placed = (P("tile", "wave", None), P(), P(), P(None, "tile", "wave"))
    return jax.shard_map(
        shards, mesh=mesh, in_specs=placed, out_specs=P("tile", "wave", None), check_vma=False
    )
```

profile of v0, /device:TPU:30, one launch (start us, length us, event | category | flops | bytes accessed | tf_op | source)
XLA Modules:
  0.0 158.3 jit_solution(14425872218366795045)
XLA Ops:
  0.0 5.8 %fusion.3 = bf16[512,512]{1,0:T(8,128)(2,1)S(1)} fusion(bf16[512,4096]{1,0:T(8,128)(2,1)} %bitcast.159, bf16[4096,512]{1,0:T(8,128)(2,1)} %param.5), kind=kOutput, calls=%fused_computation.9 | convolution fusion | flops 2148007936 | bytes 8912896 | tf_op jit(solution)/shard_map/dot_general | solution.py:82
  7.5 1.9 %collective-permute-start.1 = (bf16[8,32,512]{2,1,0:T(8,128)(2,1)}, bf16[8,32,512]{2,1,0:T(8,128)(2,1)}, u32[]{:S(2)}, u32[]{:S(2)}) collective-permute-start(bf16[8,32,512]{2,1,0:T(8,128)(2,1)} %bitcast.22), channel_id=1, source_target_pairs={{0,1},{1,2},{2,3},{3,4},{4,5},{5,6},{6,7},{7,8},{8,9},{9,10},{10,1... | collective-permute-start | bytes 786440 | tf_op jit(solution)/shard_map/ppermute | solution.py:12
  9.5 1.5 fusion.32
  11.0 6.5 %collective-permute-start = (bf16[8,8,512]{2,1,0:T(8,128)(2,1)}, bf16[8,8,512]{2,1,0:T(8,128)(2,1)}, u32[]{:S(2)}, u32[]{:S(2)}) collective-permute-start(bf16[8,8,512]{2,1,0:T(8,128)(2,1)} %get-tuple-element.24), channel_id=1, source_target_pairs={{0,33},{32,65},{64,97},{96,129},{128,161},{160,193},{192,225},{1,3... | collective-permute-start | bytes 196616 | tf_op jit(solution)/shard_map/ppermute | solution.py:22
  17.5 1.9 %collective-permute-start.2 = (bf16[8,8,512]{2,1,0:T(8,128)(2,1)}, bf16[8,8,512]{2,1,0:T(8,128)(2,1)S(1)}, u32[]{:S(2)}, u32[]{:S(2)}) collective-permute-start(bf16[8,8,512]{2,1,0:T(8,128)(2,1)} %get-tuple-element.23), channel_id=1, source_target_pairs={{32,1},{64,33},{96,65},{128,97},{160,129},{192,161},{224,193},{33,... | collective-permute-start | bytes 196616 | tf_op jit(solution)/shard_map/ppermute | solution.py:22
  19.4 6.5 %collective-permute-start.4 = (bf16[8,32,512]{2,1,0:T(8,128)(2,1)}, bf16[8,32,512]{2,1,0:T(8,128)(2,1)}, u32[]{:S(2)}, u32[]{:S(2)}) collective-permute-start(bf16[8,32,512]{2,1,0:T(8,128)(2,1)} %bitcast.26), channel_id=1, source_target_pairs={{1,0},{2,1},{3,2},{4,3},{5,4},{6,5},{7,6},{8,7},{9,8},{10,9},{11,1... | collective-permute-start | bytes 786440 | tf_op jit(solution)/shard_map/ppermute | solution.py:12
  25.9 1.5 fusion.31
  27.5 3.2 %collective-permute-start.3 = (bf16[8,8,512]{2,1,0:T(8,128)(2,1)}, bf16[8,8,512]{2,1,0:T(8,128)(2,1)S(1)}, u32[]{:S(2)}, u32[]{:S(2)}) collective-permute-start(bf16[8,8,512]{2,1,0:T(8,128)(2,1)} %get-tuple-element.22), channel_id=1, source_target_pairs={{1,32},{33,64},{65,96},{97,128},{129,160},{161,192},{193,224},{2,3... | collective-permute-start | bytes 196616 | tf_op jit(solution)/shard_map/ppermute | solution.py:22
  30.8 3.4 %convert_bitcast_fusion = bf16[16,32,32,48]{3,2,0,1:T(8,128)(2,1)} fusion(pred[17,32,48]{2,1,0:T(32,128)(4,1)S(1)} %iota_compare_fusion, bf16[17,17]{1,0:T(8,128)(2,1)S(1)} %copy-done.5), kind=kOutput, calls=%fused_computation.1 | convolution fusion | flops 28456448 | bytes 1599554 | tf_op jit(solution)/shard_map/ayY,axX->yxYX/dot_general | solution.py:51
  34.2 10.5 %copy.6 = bf16[16,32,32,48]{1,0,3,2:T(8,128)(2,1)} copy(bf16[16,32,32,48]{3,2,0,1:T(8,128)(2,1)} %convert_bitcast_fusion) | data formatting | bytes 3145728 | tf_op jit(solution)/shard_map/convert_element_type | solution.py:52
  44.7 8.4 %reshape.130 = bf16[512,32,48]{0,2,1:T(8,128)(2,1)S(1)} reshape(bf16[16,32,32,48]{1,0,3,2:T(8,128)(2,1)} %copy.6) | data formatting | bytes 3145728 | tf_op jit(solution)/shard_map/reshape | solution.py:52
  55.4 3.4 %convert_bitcast_fusion.1 = bf16[16,32,32,48]{3,2,0,1:T(8,128)(2,1)} fusion(pred[17,32,48]{2,1,0:T(32,128)(4,1)S(1)} %iota_compare_fusion, bf16[17,17]{1,0:T(8,128)(2,1)S(1)} %rev.3), kind=kOutput, calls=%fused_computation.2 | convolution fusion | flops 28456448 | bytes 1599554 | tf_op jit(solution)/shard_map/ayY,axX->yxYX/dot_general | solution.py:51
  58.8 10.5 %copy.5 = bf16[16,32,32,48]{1,0,3,2:T(8,128)(2,1)} copy(bf16[16,32,32,48]{3,2,0,1:T(8,128)(2,1)} %convert_bitcast_fusion.1) | data formatting | bytes 3145728 | tf_op jit(solution)/shard_map/convert_element_type | solution.py:52
  69.4 8.4 %reshape.128 = bf16[512,32,48]{0,2,1:T(8,128)(2,1)S(1)} reshape(bf16[16,32,32,48]{1,0,3,2:T(8,128)(2,1)} %copy.5) | data formatting | bytes 3145728 | tf_op jit(solution)/shard_map/reshape | solution.py:52
  78.4 1.7 %constant_dynamic-update-slice_fusion.4 = bf16[512,1024]{0,1:T(8,128)(2,1)} fusion(bf16[512,1024]{0,1:T(8,128)(2,1)} %constant_dynamic-update-slice_fusion.5, bf16[512,256]{0,1:T(8,128)(2,1)} %bitcast.152), kind=kLoop, calls=%fused_computation.37 | loop fusion | bytes 524288
  84.0 1.0 fusion.27
  85.0 1.7 %fusion.33 = f32[512,512]{1,0:T(8,128)S(1)} fusion(bf16[512,512]{0,1:T(8,128)(2,1)} %bitcast.148, bf16[512,512]{1,0:T(8,128)(2,1)} %copy-done), kind=kOutput, calls=%fused_computation.77 | convolution fusion | flops 268435456 | bytes 2097152 | tf_op jit(solution)/shard_map/dot_general | solution.py:74
  91.6 2.7 %collective-permute-start.5 = (bf16[8,8,512]{2,1,0:T(8,128)(2,1)S(1)}, bf16[8,8,512]{2,1,0:T(8,128)(2,1)S(1)}, u32[]{:S(2)}, u32[]{:S(2)}) collective-permute-start(bf16[8,8,512]{2,1,0:T(8,128)(2,1)S(1)} %copy-done.4), channel_id=1, source_target_pairs={{33,0},{65,32},{97,64},{129,96},{161,128},{193,160},{225,192},{34,... | collective-permute-start | bytes 196616 | tf_op jit(solution)/shard_map/ppermute | solution.py:22
  95.1 5.9 %collective-permute-start.6 = (bf16[16,8,512]{2,1,0:T(8,128)(2,1)S(1)}, bf16[16,8,512]{2,1,0:T(8,128)(2,1)S(1)}, u32[]{:S(2)}, u32[]{:S(2)}) collective-permute-start(bf16[16,8,512]{2,1,0:T(8,128)(2,1)S(1)} %get-tuple-element.14), channel_id=1, source_target_pairs={{0,32},{32,64},{64,96},{96,128},{128,160},{160,192},{192,224},{1,3... | collective-permute-start | bytes 393224 | tf_op jit(solution)/shard_map/ppermute | solution.py:15
  101.0 1.0 constant_dynamic-update-slice_fusion.10
  102.0 1.9 %collective-permute-start.7 = (bf16[16,8,512]{2,1,0:T(8,128)(2,1)S(1)}, bf16[16,8,512]{2,1,0:T(8,128)(2,1)S(1)}, u32[]{:S(2)}, u32[]{:S(2)}) collective-permute-start(bf16[16,8,512]{2,1,0:T(8,128)(2,1)S(1)} %get-tuple-element.13), channel_id=1, source_target_pairs={{32,0},{64,32},{96,64},{128,96},{160,128},{192,160},{224,192},{33,... | collective-permute-start | bytes 393224 | tf_op jit(solution)/shard_map/ppermute | solution.py:15
  105.0 6.0 %collective-permute-done.7 = bf16[16,8,512]{2,1,0:T(8,128)(2,1)S(1)} collective-permute-done((bf16[16,8,512]{2,1,0:T(8,128)(2,1)S(1)}, bf16[16,8,512]{2,1,0:T(8,128)(2,1)S(1)}, u32[]{:S(2)}, u32[]{:S(2)}) %collective-permute-start.7) | collective-permute-done | bytes 131104 | tf_op jit(solution)/shard_map/ppermute | solution.py:15
  111.8 2.1 %collective-permute-start.9 = (bf16[8,32,512]{2,1,0:T(8,128)(2,1)S(1)}, bf16[8,32,512]{2,1,0:T(8,128)(2,1)S(1)}, u32[]{:S(2)}, u32[]{:S(2)}) collective-permute-start(bf16[8,32,512]{2,1,0:T(8,128)(2,1)S(1)} %bitcast.156), channel_id=1, source_target_pairs={{0,1},{1,2},{2,3},{3,4},{4,5},{5,6},{6,7},{7,8},{8,9},{9,10},{10,1... | collective-permute-start | bytes 786440 | tf_op jit(solution)/shard_map/ppermute | solution.py:12
  113.9 6.7 %collective-permute-start.12 = (bf16[8,32,512]{2,1,0:T(8,128)(2,1)S(1)}, bf16[8,32,512]{2,1,0:T(8,128)(2,1)S(1)}, u32[]{:S(2)}, u32[]{:S(2)}) collective-permute-start(bf16[8,32,512]{2,1,0:T(8,128)(2,1)S(1)} %bitcast.154), channel_id=1, source_target_pairs={{1,0},{2,1},{3,2},{4,3},{5,4},{6,5},{7,6},{8,7},{9,8},{10,9},{11,1... | collective-permute-start | bytes 786440 | tf_op jit(solution)/shard_map/ppermute | solution.py:12
  120.5 1.9 %collective-permute-start.8 = (bf16[8,8,512]{2,1,0:T(8,128)(2,1)S(1)}, bf16[8,8,512]{2,1,0:T(8,128)(2,1)S(1)}, u32[]{:S(2)}, u32[]{:S(2)}) collective-permute-start(bf16[8,8,512]{2,1,0:T(8,128)(2,1)S(1)} %get-tuple-element.20), channel_id=1, source_target_pairs={{0,33},{32,65},{64,97},{96,129},{128,161},{160,193},{192,225},{1,3... | collective-permute-start | bytes 196616 | tf_op jit(solution)/shard_map/ppermute | solution.py:22
  122.5 3.9 %collective-permute-start.10 = (bf16[8,8,512]{2,1,0:T(8,128)(2,1)S(1)}, bf16[8,8,512]{2,1,0:T(8,128)(2,1)S(1)}, u32[]{:S(2)}, u32[]{:S(2)}) collective-permute-start(bf16[8,8,512]{2,1,0:T(8,128)(2,1)S(1)} %get-tuple-element.19), channel_id=1, source_target_pairs={{32,1},{64,33},{96,65},{128,97},{160,129},{192,161},{224,193},{33,... | collective-permute-start | bytes 196616 | tf_op jit(solution)/shard_map/ppermute | solution.py:22
  126.4 5.9 %collective-permute-start.11 = (bf16[8,8,512]{2,1,0:T(8,128)(2,1)S(1)}, bf16[8,8,512]{2,1,0:T(8,128)(2,1)S(1)}, u32[]{:S(2)}, u32[]{:S(2)}) collective-permute-start(bf16[8,8,512]{2,1,0:T(8,128)(2,1)S(1)} %get-tuple-element.18), channel_id=1, source_target_pairs={{1,32},{33,64},{65,96},{97,128},{129,160},{161,192},{193,224},{2,3... | collective-permute-start | bytes 196616 | tf_op jit(solution)/shard_map/ppermute | solution.py:22
  132.8 3.3 %collective-permute-start.13 = (bf16[8,8,512]{2,1,0:T(8,128)(2,1)S(1)}, bf16[8,8,512]{2,1,0:T(8,128)(2,1)S(1)}, u32[]{:S(2)}, u32[]{:S(2)}) collective-permute-start(bf16[8,8,512]{2,1,0:T(8,128)(2,1)S(1)} %get-tuple-element.17), channel_id=1, source_target_pairs={{33,0},{65,32},{97,64},{129,96},{161,128},{193,160},{225,192},{34,... | collective-permute-start | bytes 196616 | tf_op jit(solution)/shard_map/ppermute | solution.py:22
  136.1 5.7 %collective-permute-start.14 = (bf16[16,8,512]{2,1,0:T(8,128)(2,1)S(1)}, bf16[16,8,512]{2,1,0:T(8,128)(2,1)S(1)}, u32[]{:S(2)}, u32[]{:S(2)}) collective-permute-start(bf16[16,8,512]{2,1,0:T(8,128)(2,1)S(1)} %get-tuple-element.10), channel_id=1, source_target_pairs={{0,32},{32,64},{64,96},{96,128},{128,160},{160,192},{192,224},{1,3... | collective-permute-start | bytes 393224 | tf_op jit(solution)/shard_map/ppermute | solution.py:15
  141.9 2.1 %collective-permute-start.15 = (bf16[16,8,512]{2,1,0:T(8,128)(2,1)S(1)}, bf16[16,8,512]{2,1,0:T(8,128)(2,1)S(1)}, u32[]{:S(2)}, u32[]{:S(2)}) collective-permute-start(bf16[16,8,512]{2,1,0:T(8,128)(2,1)S(1)} %get-tuple-element.9), channel_id=1, source_target_pairs={{32,0},{64,32},{96,64},{128,96},{160,128},{192,160},{224,192},{33,... | collective-permute-start | bytes 393224 | tf_op jit(solution)/shard_map/ppermute | solution.py:15
  144.4 6.5 %collective-permute-done.15 = bf16[16,8,512]{2,1,0:T(8,128)(2,1)S(1)} collective-permute-done((bf16[16,8,512]{2,1,0:T(8,128)(2,1)S(1)}, bf16[16,8,512]{2,1,0:T(8,128)(2,1)S(1)}, u32[]{:S(2)}, u32[]{:S(2)}) %collective-permute-start.15) | collective-permute-done | bytes 131104 | tf_op jit(solution)/shard_map/ppermute | solution.py:15
  150.9 7.4 %convolution_convert_fusion = bf16[512,4096]{1,0:T(8,128)(2,1)} fusion(bf16[4096,512]{1,0:T(8,128)(2,1)} %param.5, f32[512,512]{1,0:T(8,128)S(1)} %fusion.34, bf16[512,1024]{0,1:T(8,128)(2,1)} %fusion.15, bf16[1024,512]{1,0:T(8,128)(2,1)S(1)} %bitcast_dynamic-update-slice_fusion, bf16[512,512]{1,0:T(8,128)(2,1)S(1)} %copy-done.1), kind=kOutput, calls=%fused_computation | convolution fusion | flops 2687762432 | bytes 12058624 | tf_op jit(solution)/shard_map/dot_general | solution.py:93
  (70 shorter events, 17.0 us)
Async XLA Ops:
  0.0 30.8 %copy-start.5 = (bf16[17,17]{1,0:T(8,128)(2,1)S(1)}, bf16[17,17]{1,0:T(8,128)(2,1)}, u32[]{:S(2)}) copy-start(bf16[17,17]{1,0:T(8,128)(2,1)} %param.6) | copy-start | bytes 1738
  5.8 0.8 copy-start
  7.5 87.6 %collective-permute-start.1 = (bf16[8,32,512]{2,1,0:T(8,128)(2,1)}, bf16[8,32,512]{2,1,0:T(8,128)(2,1)}, u32[]{:S(2)}, u32[]{:S(2)}) collective-permute-start(bf16[8,32,512]{2,1,0:T(8,128)(2,1)} %bitcast.22), channel_id=1, source_target_pairs={{0,1},{1,2},{2,3},{3,4},{4,5},{5,6},{6,7},{7,8},{8,9},{9,10},{10,1... | collective-permute-start | bytes 786440 | tf_op jit(solution)/shard_map/ppermute | solution.py:12
  11.0 80.6 %collective-permute-start = (bf16[8,8,512]{2,1,0:T(8,128)(2,1)}, bf16[8,8,512]{2,1,0:T(8,128)(2,1)}, u32[]{:S(2)}, u32[]{:S(2)}) collective-permute-start(bf16[8,8,512]{2,1,0:T(8,128)(2,1)} %get-tuple-element.24), channel_id=1, source_target_pairs={{0,33},{32,65},{64,97},{96,129},{128,161},{160,193},{192,225},{1,3... | collective-permute-start | bytes 196616 | tf_op jit(solution)/shard_map/ppermute | solution.py:22
  17.5 84.5 %collective-permute-start.2 = (bf16[8,8,512]{2,1,0:T(8,128)(2,1)}, bf16[8,8,512]{2,1,0:T(8,128)(2,1)S(1)}, u32[]{:S(2)}, u32[]{:S(2)}) collective-permute-start(bf16[8,8,512]{2,1,0:T(8,128)(2,1)} %get-tuple-element.23), channel_id=1, source_target_pairs={{32,1},{64,33},{96,65},{128,97},{160,129},{192,161},{224,193},{33,... | collective-permute-start | bytes 196616 | tf_op jit(solution)/shard_map/ppermute | solution.py:22
  19.4 84.6 %collective-permute-start.4 = (bf16[8,32,512]{2,1,0:T(8,128)(2,1)}, bf16[8,32,512]{2,1,0:T(8,128)(2,1)}, u32[]{:S(2)}, u32[]{:S(2)}) collective-permute-start(bf16[8,32,512]{2,1,0:T(8,128)(2,1)} %bitcast.26), channel_id=1, source_target_pairs={{1,0},{2,1},{3,2},{4,3},{5,4},{6,5},{7,6},{8,7},{9,8},{10,9},{11,1... | collective-permute-start | bytes 786440 | tf_op jit(solution)/shard_map/ppermute | solution.py:12
  27.5 76.5 %collective-permute-start.3 = (bf16[8,8,512]{2,1,0:T(8,128)(2,1)}, bf16[8,8,512]{2,1,0:T(8,128)(2,1)S(1)}, u32[]{:S(2)}, u32[]{:S(2)}) collective-permute-start(bf16[8,8,512]{2,1,0:T(8,128)(2,1)} %get-tuple-element.22), channel_id=1, source_target_pairs={{1,32},{33,64},{65,96},{97,128},{129,160},{161,192},{193,224},{2,3... | collective-permute-start | bytes 196616 | tf_op jit(solution)/shard_map/ppermute | solution.py:22
  77.8 13.7 %copy-start.3 = (bf16[512,16,32]{0,2,1:T(8,128)(2,1)S(1)}, bf16[512,16,32]{0,2,1:T(8,128)(2,1)}, u32[]{:S(2)}) copy-start(bf16[512,16,32]{0,2,1:T(8,128)(2,1)} %param.7) | copy-start | bytes 1572868
  81.4 10.2 %copy-start.4 = (bf16[8,8,512]{2,1,0:T(8,128)(2,1)S(1)}, bf16[8,8,512]{2,1,0:T(8,128)(2,1)}, u32[]{:S(2)}) copy-start(bf16[8,8,512]{2,1,0:T(8,128)(2,1)} %get-tuple-element.21) | copy-start | bytes 196612
  85.0 26.0 %copy-start.2 = (bf16[512,1024]{0,1:T(8,128)(2,1)S(1)}, bf16[512,1024]{0,1:T(8,128)(2,1)}, u32[]{:S(2)}) copy-start(bf16[512,1024]{0,1:T(8,128)(2,1)} %fusion.17) | copy-start | bytes 3145732
  91.6 13.4 %collective-permute-start.5 = (bf16[8,8,512]{2,1,0:T(8,128)(2,1)S(1)}, bf16[8,8,512]{2,1,0:T(8,128)(2,1)S(1)}, u32[]{:S(2)}, u32[]{:S(2)}) collective-permute-start(bf16[8,8,512]{2,1,0:T(8,128)(2,1)S(1)} %copy-done.4), channel_id=1, source_target_pairs={{33,0},{65,32},{97,64},{129,96},{161,128},{193,160},{225,192},{34,... | collective-permute-start | bytes 196616 | tf_op jit(solution)/shard_map/ppermute | solution.py:22
  95.1 9.9 %collective-permute-start.6 = (bf16[16,8,512]{2,1,0:T(8,128)(2,1)S(1)}, bf16[16,8,512]{2,1,0:T(8,128)(2,1)S(1)}, u32[]{:S(2)}, u32[]{:S(2)}) collective-permute-start(bf16[16,8,512]{2,1,0:T(8,128)(2,1)S(1)} %get-tuple-element.14), channel_id=1, source_target_pairs={{0,32},{32,64},{64,96},{96,128},{128,160},{160,192},{192,224},{1,3... | collective-permute-start | bytes 393224 | tf_op jit(solution)/shard_map/ppermute | solution.py:15
  102.0 9.0 %collective-permute-start.7 = (bf16[16,8,512]{2,1,0:T(8,128)(2,1)S(1)}, bf16[16,8,512]{2,1,0:T(8,128)(2,1)S(1)}, u32[]{:S(2)}, u32[]{:S(2)}) collective-permute-start(bf16[16,8,512]{2,1,0:T(8,128)(2,1)S(1)} %get-tuple-element.13), channel_id=1, source_target_pairs={{32,0},{64,32},{96,64},{128,96},{160,128},{192,160},{224,192},{33,... | collective-permute-start | bytes 393224 | tf_op jit(solution)/shard_map/ppermute | solution.py:15
  111.7 39.1 %copy-start.1 = (bf16[512,512]{1,0:T(8,128)(2,1)S(1)}, bf16[512,512]{1,0:T(8,128)(2,1)}, u32[]{:S(2)}) copy-start(bf16[512,512]{1,0:T(8,128)(2,1)} %copy-done) | copy-start | bytes 1572868
  111.8 24.3 %collective-permute-start.9 = (bf16[8,32,512]{2,1,0:T(8,128)(2,1)S(1)}, bf16[8,32,512]{2,1,0:T(8,128)(2,1)S(1)}, u32[]{:S(2)}, u32[]{:S(2)}) collective-permute-start(bf16[8,32,512]{2,1,0:T(8,128)(2,1)S(1)} %bitcast.156), channel_id=1, source_target_pairs={{0,1},{1,2},{2,3},{3,4},{4,5},{5,6},{6,7},{7,8},{8,9},{9,10},{10,1... | collective-permute-start | bytes 786440 | tf_op jit(solution)/shard_map/ppermute | solution.py:12
  113.9 30.2 %collective-permute-start.12 = (bf16[8,32,512]{2,1,0:T(8,128)(2,1)S(1)}, bf16[8,32,512]{2,1,0:T(8,128)(2,1)S(1)}, u32[]{:S(2)}, u32[]{:S(2)}) collective-permute-start(bf16[8,32,512]{2,1,0:T(8,128)(2,1)S(1)} %bitcast.154), channel_id=1, source_target_pairs={{1,0},{2,1},{3,2},{4,3},{5,4},{6,5},{7,6},{8,7},{9,8},{10,9},{11,1... | collective-permute-start | bytes 786440 | tf_op jit(solution)/shard_map/ppermute | solution.py:12
  120.5 12.2 %collective-permute-start.8 = (bf16[8,8,512]{2,1,0:T(8,128)(2,1)S(1)}, bf16[8,8,512]{2,1,0:T(8,128)(2,1)S(1)}, u32[]{:S(2)}, u32[]{:S(2)}) collective-permute-start(bf16[8,8,512]{2,1,0:T(8,128)(2,1)S(1)} %get-tuple-element.20), channel_id=1, source_target_pairs={{0,33},{32,65},{64,97},{96,129},{128,161},{160,193},{192,225},{1,3... | collective-permute-start | bytes 196616 | tf_op jit(solution)/shard_map/ppermute | solution.py:22
  122.5 19.4 %collective-permute-start.10 = (bf16[8,8,512]{2,1,0:T(8,128)(2,1)S(1)}, bf16[8,8,512]{2,1,0:T(8,128)(2,1)S(1)}, u32[]{:S(2)}, u32[]{:S(2)}) collective-permute-start(bf16[8,8,512]{2,1,0:T(8,128)(2,1)S(1)} %get-tuple-element.19), channel_id=1, source_target_pairs={{32,1},{64,33},{96,65},{128,97},{160,129},{192,161},{224,193},{33,... | collective-permute-start | bytes 196616 | tf_op jit(solution)/shard_map/ppermute | solution.py:22
  126.4 17.7 %collective-permute-start.11 = (bf16[8,8,512]{2,1,0:T(8,128)(2,1)S(1)}, bf16[8,8,512]{2,1,0:T(8,128)(2,1)S(1)}, u32[]{:S(2)}, u32[]{:S(2)}) collective-permute-start(bf16[8,8,512]{2,1,0:T(8,128)(2,1)S(1)} %get-tuple-element.18), channel_id=1, source_target_pairs={{1,32},{33,64},{65,96},{97,128},{129,160},{161,192},{193,224},{2,3... | collective-permute-start | bytes 196616 | tf_op jit(solution)/shard_map/ppermute | solution.py:22
  132.8 11.3 %collective-permute-start.13 = (bf16[8,8,512]{2,1,0:T(8,128)(2,1)S(1)}, bf16[8,8,512]{2,1,0:T(8,128)(2,1)S(1)}, u32[]{:S(2)}, u32[]{:S(2)}) collective-permute-start(bf16[8,8,512]{2,1,0:T(8,128)(2,1)S(1)} %get-tuple-element.17), channel_id=1, source_target_pairs={{33,0},{65,32},{97,64},{129,96},{161,128},{193,160},{225,192},{34,... | collective-permute-start | bytes 196616 | tf_op jit(solution)/shard_map/ppermute | solution.py:22
  136.1 8.2 %collective-permute-start.14 = (bf16[16,8,512]{2,1,0:T(8,128)(2,1)S(1)}, bf16[16,8,512]{2,1,0:T(8,128)(2,1)S(1)}, u32[]{:S(2)}, u32[]{:S(2)}) collective-permute-start(bf16[16,8,512]{2,1,0:T(8,128)(2,1)S(1)} %get-tuple-element.10), channel_id=1, source_target_pairs={{0,32},{32,64},{64,96},{96,128},{128,160},{160,192},{192,224},{1,3... | collective-permute-start | bytes 393224 | tf_op jit(solution)/shard_map/ppermute | solution.py:15
  141.9 9.0 %collective-permute-start.15 = (bf16[16,8,512]{2,1,0:T(8,128)(2,1)S(1)}, bf16[16,8,512]{2,1,0:T(8,128)(2,1)S(1)}, u32[]{:S(2)}, u32[]{:S(2)}) collective-permute-start(bf16[16,8,512]{2,1,0:T(8,128)(2,1)S(1)} %get-tuple-element.9), channel_id=1, source_target_pairs={{32,0},{64,32},{96,64},{128,96},{160,128},{192,160},{224,192},{33,... | collective-permute-start | bytes 393224 | tf_op jit(solution)/shard_map/ppermute | solution.py:15
where the time goes:
time: 160 us; the launch traced here: 158 us
  starting transfers between devices  62.1 us (39%)
  local copies, waits for them, and re-layouts  59.9 us (37%)
  matrix products  23 us (14%)
  waiting for transfers between devices  12.7 us (8%)
    ppermute x8, starting transfers between devices, send(): return lax.ppermute(block, ('wave', 'tile'), pairs)  29.3 us
    convert_element_type x2, local copies, waits for them, and re-layouts, blur_mats(): full = full.astype(psf.dtype).reshape(rows * cols, win_rows, win_cols)  21.1 us
    ppermute x4, starting transfers between devices, send(): return lax.ppermute(block, 'tile', pairs)  17.2 us
    reshape x2, local copies, waits for them, and re-layouts, blur_mats(): full = full.astype(psf.dtype).reshape(rows * cols, win_rows, win_cols)  16.7 us
    ppermute x4, starting transfers between devices, send(): return lax.ppermute(block, 'wave', pairs)  15.6 us
    unnamed x40, local copies, waits for them, and re-layouts  13.8 us
    ppermute x4, waiting for transfers between devices, send(): return lax.ppermute(block, 'wave', pairs)  12.7 us
    dot_general x1, matrix products, shards(): lax.dot_general(tau_grad, profile_basis, (((1,), (1,)), ((), ())), prefer...  7.45 us
  transfers between devices with their start and end apart: 16, of which 3 were waited for; matrix products, arithmetic and copies ran while one was open for 42% of the time, Pallas kernels for 0%

commit v1 on v0

v1 whole, which is shorter than its diff:
```python
import jax
import jax.numpy as jnp
from jax import lax
from jax.sharding import PartitionSpec as P


def send(block, axis, step):
    count = lax.axis_size(axis)
    pairs = [(i, i + step) for i in range(count) if 0 <= i + step < count]
    return lax.ppermute(block, axis, pairs)


def window(block, h):
    rows, cols = block.shape[0], block.shape[1]
    left = send(block[:, cols - h :], "wave", 1)
    right = send(block[:, :h], "wave", -1)
    band = jnp.concatenate([left, block, right], axis=1)
    top = send(band[rows - h :], "tile", 1)
    bottom = send(band[:h], "tile", -1)
    full = jnp.concatenate([top, band, bottom], axis=0)
    return full.reshape(-1, full.shape[-1])


def blur_mat(psf, rows, cols, h):
    k = psf.shape[0]
    win_cols = cols + 2 * h
    shape_c = (cols, k, win_cols)
    col_gap = lax.broadcasted_iota(jnp.int32, shape_c, 2) - lax.broadcasted_iota(jnp.int32, shape_c, 0)
    taps = jnp.broadcast_to(psf[None], (cols, k, k))
    strip = jnp.zeros(shape_c, psf.dtype)
    for b in range(k):
        strip = jnp.where(col_gap == b, taps[:, :, b : b + 1], strip)
    strip = strip.reshape(cols, k * win_cols)
    total = (rows + 2 * h) * win_cols
    blocks = [
        jnp.pad(strip, ((0, 0), (y * win_cols, total - y * win_cols - k * win_cols)))
        for y in range(rows)
    ]
    return jnp.concatenate(blocks, axis=0)


def blur(field, mat, h):
    near = window(field, h)
    return jnp.dot(mat, near, preferred_element_type=jnp.float32)


def shards(coefficients, profile_basis, point_spread, observed):
    rows, cols, profiles = coefficients.shape
    waves = profile_basis.shape[1]
    h = point_spread.shape[0] // 2
    opacity = jnp.dot(
        coefficients.reshape(rows * cols, profiles), profile_basis, preferred_element_type=jnp.float32
    )
    spectra = jnp.exp(-opacity).astype(jnp.bfloat16)
    forward = blur_mat(point_spread, rows, cols, h)
    adjoint = blur_mat(point_spread[::-1, ::-1], rows, cols, h)
    blurred = blur(spectra.reshape(rows, cols, waves), forward, h)
    measured = observed.transpose(1, 2, 0).reshape(rows * cols, waves).astype(jnp.float32)
    residual = (blurred - measured).astype(jnp.bfloat16)
    adjoint_field = blur(residual.reshape(rows, cols, waves), adjoint, h)
    tau_grad = (-spectra.astype(jnp.float32) * adjoint_field).astype(jnp.bfloat16)
    coef_grad = lax.dot_general(
        tau_grad, profile_basis, (((1,), (1,)), ((), ())), preferred_element_type=jnp.float32
    )
    return coef_grad.astype(jnp.bfloat16).reshape(rows, cols, profiles)


def solution(mesh):
    placed = (P("tile", "wave", None), P(), P(), P(None, "tile", "wave"))
    return jax.shard_map(
        shards, mesh=mesh, in_specs=placed, out_specs=P("tile", "wave", None), check_vma=False
    )
```

time: 160 us -> 96.2 us (0.60)
  the two profiles are of different devices: /device:TPU:30 before, /device:TPU:71 now
where the time goes in v1:
time: 96.2 us; the launch traced here: 95.9 us
  waiting for transfers between devices  31 us (32%)
  starting transfers between devices  24.7 us (26%)
  local copies, waits for them, and re-layouts  20.9 us (22%)
  matrix products  16 us (17%)
  other arithmetic  2.86 us (3%)
    ppermute x8, waiting for transfers between devices, send(): return lax.ppermute(block, axis, pairs)  31 us
    ppermute x8, starting transfers between devices, send(): return lax.ppermute(block, axis, pairs)  24.7 us
    unnamed x36, local copies, waits for them, and re-layouts  11.9 us
    dot_general x1, matrix products, shards(): lax.dot_general(tau_grad, profile_basis, (((1,), (1,)), ((), ())), prefer...  7.84 us
    dot_general x1, matrix products, shards(): jnp.dot(coefficients.reshape(rows * cols, profiles), profile_basis, prefe...  5.81 us
    broadcast_in_dim x68, local copies, waits for them, and re-layouts, blur_mat(): strip = jnp.where(col_gap == b, taps[:, :, b:b + 1], strip)  5.57 us
    dot_general x1, matrix products, blur(): return jnp.dot(mat, near, preferred_element_type=jnp.float32)  2.39 us
    slice x19, local copies, waits for them, and re-layouts, blur_mat(): strip = jnp.where(col_gap == b, taps[:, :, b:b + 1], strip)  2.32 us
  transfers between devices with their start and end apart: 8, of which 6 were waited for; matrix products, arithmetic and copies ran while one was open for 24% of the time, Pallas kernels for 0%

profile of v1, /device:TPU:71, one launch (start us, length us, event | category | flops | bytes accessed | tf_op | source)
XLA Modules:
  0.0 95.9 jit_solution(14268208455390067880)
XLA Ops:
  0.0 5.8 %fusion.2 = bf16[512,512]{1,0:T(8,128)(2,1)S(1)} fusion(bf16[512,4096]{1,0:T(8,128)(2,1)} %bitcast.25, bf16[4096,512]{1,0:T(8,128)(2,1)} %param.5), kind=kOutput, calls=%fused_computation.8 | convolution fusion | flops 2148007936 | bytes 8912896 | tf_op jit(solution)/shard_map/dot_general | solution.py:51
  5.8 3.2 %collective-permute-start = (bf16[16,8,512]{2,1,0:T(8,128)(2,1)S(1)}, bf16[16,8,512]{2,1,0:T(8,128)(2,1)S(1)}, u32[]{:S(2)}, u32[]{:S(2)}) collective-permute-start(bf16[16,8,512]{2,1,0:T(8,128)(2,1)S(1)} %get-tuple-element.28), channel_id=1, source_target_pairs={{0,32},{32,64},{64,96},{96,128},{128,160},{160,192},{192,224},{1,3... | collective-permute-start | bytes 393224 | tf_op jit(solution)/shard_map/ppermute | solution.py:10
  9.1 1.3 %collective-permute-start.1 = (bf16[16,8,512]{2,1,0:T(8,128)(2,1)S(1)}, bf16[16,8,512]{2,1,0:T(8,128)(2,1)S(1)}, u32[]{:S(2)}, u32[]{:S(2)}) collective-permute-start(bf16[16,8,512]{2,1,0:T(8,128)(2,1)S(1)} %get-tuple-element.29), channel_id=1, source_target_pairs={{32,0},{64,32},{96,64},{128,96},{160,128},{192,160},{224,192},{33,... | collective-permute-start | bytes 393224 | tf_op jit(solution)/shard_map/ppermute | solution.py:10
  13.9 0.6 pad_dynamic-update-slice_fusion.15
  14.6 0.7 pad_dynamic-update-slice_fusion.14
  15.3 0.7 pad_dynamic-update-slice_fusion.13
  16.1 0.7 pad_dynamic-update-slice_fusion.12
  16.8 0.7 pad_dynamic-update-slice_fusion.11
  17.5 0.7 pad_dynamic-update-slice_fusion.10
  18.2 0.7 pad_dynamic-update-slice_fusion.9
  19.0 0.7 pad_dynamic-update-slice_fusion.8
  19.7 0.6 pad_dynamic-update-slice_fusion.7
  20.3 0.7 pad_dynamic-update-slice_fusion.6
  21.1 0.7 pad_dynamic-update-slice_fusion.5
  21.8 0.7 pad_dynamic-update-slice_fusion.4
  22.5 0.7 pad_dynamic-update-slice_fusion.3
  23.3 0.7 pad_dynamic-update-slice_fusion.2
  24.0 0.7 pad_dynamic-update-slice_fusion.1
  24.7 0.7 pad_dynamic-update-slice_fusion
  33.5 7.0 %collective-permute-start.2 = (bf16[8,48,512]{2,1,0:T(8,128)(2,1)S(1)}, bf16[8,48,512]{2,1,0:T(8,128)(2,1)S(1)}, u32[]{:S(2)}, u32[]{:S(2)}) collective-permute-start(bf16[8,48,512]{2,1,0:T(8,128)(2,1)S(1)} %get-tuple-element.24), channel_id=1, source_target_pairs={{0,1},{1,2},{2,3},{3,4},{4,5},{5,6},{6,7},{7,8},{8,9},{9,10},{10,1... | collective-permute-start | bytes 1179656 | tf_op jit(solution)/shard_map/ppermute | solution.py:10
  40.5 1.9 %collective-permute-start.3 = (bf16[8,48,512]{2,1,0:T(8,128)(2,1)S(1)}, bf16[8,48,512]{2,1,0:T(8,128)(2,1)S(1)}, u32[]{:S(2)}, u32[]{:S(2)}) collective-permute-start(bf16[8,48,512]{2,1,0:T(8,128)(2,1)S(1)} %get-tuple-element.25), channel_id=1, source_target_pairs={{1,0},{2,1},{3,2},{4,3},{5,4},{6,5},{7,6},{8,7},{9,8},{10,9},{11,1... | collective-permute-start | bytes 1179656 | tf_op jit(solution)/shard_map/ppermute | solution.py:10
  42.6 6.8 %collective-permute-done.2 = bf16[8,48,512]{2,1,0:T(8,128)(2,1)S(1)} collective-permute-done((bf16[8,48,512]{2,1,0:T(8,128)(2,1)S(1)}, bf16[8,48,512]{2,1,0:T(8,128)(2,1)S(1)}, u32[]{:S(2)}, u32[]{:S(2)}) %collective-permute-start.2) | collective-permute-done | bytes 393248 | tf_op jit(solution)/shard_map/ppermute | solution.py:10
  49.4 6.5 %collective-permute-done.3 = bf16[8,48,512]{2,1,0:T(8,128)(2,1)S(1)} collective-permute-done((bf16[8,48,512]{2,1,0:T(8,128)(2,1)S(1)}, bf16[8,48,512]{2,1,0:T(8,128)(2,1)S(1)}, u32[]{:S(2)}, u32[]{:S(2)}) %collective-permute-start.3) | collective-permute-done | bytes 393248 | tf_op jit(solution)/shard_map/ppermute | solution.py:10
  56.1 2.4 %fusion.1 = bf16[512,512]{1,0:T(8,128)(2,1)S(1)} fusion(f32[512,512]{1,0:T(8,128)S(1)} %bitcast.24, bf16[512,1536]{1,0:T(8,128)(2,1)} %pad_dynamic-update-slice_fusion, bf16[1536,512]{1,0:T(8,128)(2,1)S(1)} %bitcast.23), kind=kOutput, calls=%fused_computation.7 | convolution fusion | flops 805830656 | bytes 4718592 | tf_op jit(solution)/shard_map/dot_general | solution.py:44
  58.5 4.2 %collective-permute-start.4 = (bf16[16,8,512]{2,1,0:T(8,128)(2,1)S(1)}, bf16[16,8,512]{2,1,0:T(8,128)(2,1)S(1)}, u32[]{:S(2)}, u32[]{:S(2)}) collective-permute-start(bf16[16,8,512]{2,1,0:T(8,128)(2,1)S(1)} %get-tuple-element.26), channel_id=1, source_target_pairs={{0,32},{32,64},{64,96},{96,128},{128,160},{160,192},{192,224},{1,3... | collective-permute-start | bytes 393224 | tf_op jit(solution)/shard_map/ppermute | solution.py:10
  62.7 1.3 %collective-permute-start.5 = (bf16[16,8,512]{2,1,0:T(8,128)(2,1)S(1)}, bf16[16,8,512]{2,1,0:T(8,128)(2,1)S(1)}, u32[]{:S(2)}, u32[]{:S(2)}) collective-permute-start(bf16[16,8,512]{2,1,0:T(8,128)(2,1)S(1)} %get-tuple-element.27), channel_id=1, source_target_pairs={{32,0},{64,32},{96,64},{128,96},{160,128},{192,160},{224,192},{33,... | collective-permute-start | bytes 393224 | tf_op jit(solution)/shard_map/ppermute | solution.py:10
  64.6 3.8 %collective-permute-done.5 = bf16[16,8,512]{2,1,0:T(8,128)(2,1)S(1)} collective-permute-done((bf16[16,8,512]{2,1,0:T(8,128)(2,1)S(1)}, bf16[16,8,512]{2,1,0:T(8,128)(2,1)S(1)}, u32[]{:S(2)}, u32[]{:S(2)}) %collective-permute-start.5) | collective-permute-done | bytes 131104 | tf_op jit(solution)/shard_map/ppermute | solution.py:10
  68.6 3.9 %collective-permute-start.6 = (bf16[8,48,512]{2,1,0:T(8,128)(2,1)S(1)}, bf16[8,48,512]{2,1,0:T(8,128)(2,1)S(1)}, u32[]{:S(2)}, u32[]{:S(2)}) collective-permute-start(bf16[8,48,512]{2,1,0:T(8,128)(2,1)S(1)} %get-tuple-element.22), channel_id=1, source_target_pairs={{0,1},{1,2},{2,3},{3,4},{4,5},{5,6},{6,7},{7,8},{8,9},{9,10},{10,1... | collective-permute-start | bytes 1179656 | tf_op jit(solution)/shard_map/ppermute | solution.py:10
  72.5 1.9 %collective-permute-start.7 = (bf16[8,48,512]{2,1,0:T(8,128)(2,1)S(1)}, bf16[8,48,512]{2,1,0:T(8,128)(2,1)S(1)}, u32[]{:S(2)}, u32[]{:S(2)}) collective-permute-start(bf16[8,48,512]{2,1,0:T(8,128)(2,1)S(1)} %get-tuple-element.23), channel_id=1, source_target_pairs={{1,0},{2,1},{3,2},{4,3},{5,4},{6,5},{7,6},{8,7},{9,8},{10,9},{11,1... | collective-permute-start | bytes 1179656 | tf_op jit(solution)/shard_map/ppermute | solution.py:10
  74.6 6.7 %collective-permute-done.6 = bf16[8,48,512]{2,1,0:T(8,128)(2,1)S(1)} collective-permute-done((bf16[8,48,512]{2,1,0:T(8,128)(2,1)S(1)}, bf16[8,48,512]{2,1,0:T(8,128)(2,1)S(1)}, u32[]{:S(2)}, u32[]{:S(2)}) %collective-permute-start.6) | collective-permute-done | bytes 393248 | tf_op jit(solution)/shard_map/ppermute | solution.py:10
  81.3 6.6 %collective-permute-done.7 = bf16[8,48,512]{2,1,0:T(8,128)(2,1)S(1)} collective-permute-done((bf16[8,48,512]{2,1,0:T(8,128)(2,1)S(1)}, bf16[8,48,512]{2,1,0:T(8,128)(2,1)S(1)}, u32[]{:S(2)}, u32[]{:S(2)}) %collective-permute-start.7) | collective-permute-done | bytes 393248 | tf_op jit(solution)/shard_map/ppermute | solution.py:10
  88.0 7.8 %convolution_convert_fusion = bf16[512,4096]{1,0:T(8,128)(2,1)} fusion(bf16[4096,512]{1,0:T(8,128)(2,1)} %param.5, bf16[512,1536]{1,0:T(8,128)(2,1)} %copy-done.2, bf16[1536,512]{1,0:T(8,128)(2,1)S(1)} %bitcast.22, bf16[512,512]{1,0:T(8,128)(2,1)S(1)} %fusion.2), kind=kOutput, calls=%fused_computation | convolution fusion | flops 2955935744 | bytes 12058624 | tf_op jit(solution)/shard_map/dot_general | solution.py:62
  (142 shorter events, 12.8 us)
Async XLA Ops:
  0.0 10.4 %copy-start = (bf16[17,17]{1,0:T(8,128)(2,1)S(1)}, bf16[17,17]{1,0:T(8,128)(2,1)}, u32[]{:S(2)}) copy-start(bf16[17,17]{1,0:T(8,128)(2,1)} %param.6) | copy-start | bytes 1738
  5.8 27.5 %collective-permute-start = (bf16[16,8,512]{2,1,0:T(8,128)(2,1)S(1)}, bf16[16,8,512]{2,1,0:T(8,128)(2,1)S(1)}, u32[]{:S(2)}, u32[]{:S(2)}) collective-permute-start(bf16[16,8,512]{2,1,0:T(8,128)(2,1)S(1)} %get-tuple-element.28), channel_id=1, source_target_pairs={{0,32},{32,64},{64,96},{96,128},{128,160},{160,192},{192,224},{1,3... | collective-permute-start | bytes 393224 | tf_op jit(solution)/shard_map/ppermute | solution.py:10
  9.1 24.3 %collective-permute-start.1 = (bf16[16,8,512]{2,1,0:T(8,128)(2,1)S(1)}, bf16[16,8,512]{2,1,0:T(8,128)(2,1)S(1)}, u32[]{:S(2)}, u32[]{:S(2)}) collective-permute-start(bf16[16,8,512]{2,1,0:T(8,128)(2,1)S(1)} %get-tuple-element.29), channel_id=1, source_target_pairs={{32,0},{64,32},{96,64},{128,96},{160,128},{192,160},{224,192},{33,... | collective-permute-start | bytes 393224 | tf_op jit(solution)/shard_map/ppermute | solution.py:10
  10.7 14.7 %copy-start.1 = (bf16[512,16,32]{0,2,1:T(8,128)(2,1)S(1)}, bf16[512,16,32]{0,2,1:T(8,128)(2,1)}, u32[]{:S(2)}) copy-start(bf16[512,16,32]{0,2,1:T(8,128)(2,1)} %param.7) | copy-start | bytes 1572868
  33.5 15.9 %collective-permute-start.2 = (bf16[8,48,512]{2,1,0:T(8,128)(2,1)S(1)}, bf16[8,48,512]{2,1,0:T(8,128)(2,1)S(1)}, u32[]{:S(2)}, u32[]{:S(2)}) collective-permute-start(bf16[8,48,512]{2,1,0:T(8,128)(2,1)S(1)} %get-tuple-element.24), channel_id=1, source_target_pairs={{0,1},{1,2},{2,3},{3,4},{4,5},{5,6},{6,7},{7,8},{8,9},{9,10},{10,1... | collective-permute-start | bytes 1179656 | tf_op jit(solution)/shard_map/ppermute | solution.py:10
  40.5 15.5 %collective-permute-start.3 = (bf16[8,48,512]{2,1,0:T(8,128)(2,1)S(1)}, bf16[8,48,512]{2,1,0:T(8,128)(2,1)S(1)}, u32[]{:S(2)}, u32[]{:S(2)}) collective-permute-start(bf16[8,48,512]{2,1,0:T(8,128)(2,1)S(1)} %get-tuple-element.25), channel_id=1, source_target_pairs={{1,0},{2,1},{3,2},{4,3},{5,4},{6,5},{7,6},{8,7},{9,8},{10,9},{11,1... | collective-permute-start | bytes 1179656 | tf_op jit(solution)/shard_map/ppermute | solution.py:10
  58.5 6.2 %collective-permute-start.4 = (bf16[16,8,512]{2,1,0:T(8,128)(2,1)S(1)}, bf16[16,8,512]{2,1,0:T(8,128)(2,1)S(1)}, u32[]{:S(2)}, u32[]{:S(2)}) collective-permute-start(bf16[16,8,512]{2,1,0:T(8,128)(2,1)S(1)} %get-tuple-element.26), channel_id=1, source_target_pairs={{0,32},{32,64},{64,96},{96,128},{128,160},{160,192},{192,224},{1,3... | collective-permute-start | bytes 393224 | tf_op jit(solution)/shard_map/ppermute | solution.py:10
  62.7 5.7 %collective-permute-start.5 = (bf16[16,8,512]{2,1,0:T(8,128)(2,1)S(1)}, bf16[16,8,512]{2,1,0:T(8,128)(2,1)S(1)}, u32[]{:S(2)}, u32[]{:S(2)}) collective-permute-start(bf16[16,8,512]{2,1,0:T(8,128)(2,1)S(1)} %get-tuple-element.27), channel_id=1, source_target_pairs={{32,0},{64,32},{96,64},{128,96},{160,128},{192,160},{224,192},{33,... | collective-permute-start | bytes 393224 | tf_op jit(solution)/shard_map/ppermute | solution.py:10
  68.6 12.7 %collective-permute-start.6 = (bf16[8,48,512]{2,1,0:T(8,128)(2,1)S(1)}, bf16[8,48,512]{2,1,0:T(8,128)(2,1)S(1)}, u32[]{:S(2)}, u32[]{:S(2)}) collective-permute-start(bf16[8,48,512]{2,1,0:T(8,128)(2,1)S(1)} %get-tuple-element.22), channel_id=1, source_target_pairs={{0,1},{1,2},{2,3},{3,4},{4,5},{5,6},{6,7},{7,8},{8,9},{9,10},{10,1... | collective-permute-start | bytes 1179656 | tf_op jit(solution)/shard_map/ppermute | solution.py:10
  72.5 15.4 %collective-permute-start.7 = (bf16[8,48,512]{2,1,0:T(8,128)(2,1)S(1)}, bf16[8,48,512]{2,1,0:T(8,128)(2,1)S(1)}, u32[]{:S(2)}, u32[]{:S(2)}) collective-permute-start(bf16[8,48,512]{2,1,0:T(8,128)(2,1)S(1)} %get-tuple-element.23), channel_id=1, source_target_pairs={{1,0},{2,1},{3,2},{4,3},{5,4},{6,5},{7,6},{8,7},{9,8},{10,9},{11,1... | collective-permute-start | bytes 1179656 | tf_op jit(solution)/shard_map/ppermute | solution.py:10
  74.6 13.4 %copy-start.2 = (bf16[512,1536]{1,0:T(8,128)(2,1)}, bf16[512,1536]{1,0:T(8,128)(2,1)S(1)}, u32[]{:S(2)}) copy-start(bf16[512,1536]{1,0:T(8,128)(2,1)S(1)} %pad_dynamic-update-slice_fusion.16) | copy-start | bytes 4718596

commit v2 on v1

v2 whole, which is shorter than its diff:
```python
import jax
import jax.numpy as jnp
from jax import lax
from jax.sharding import PartitionSpec as P


def send(block, axis, step):
    count = lax.axis_size(axis)
    pairs = [(i, i + step) for i in range(count) if 0 <= i + step < count]
    return lax.ppermute(block, axis, pairs)


def window(block, h):
    rows, cols = block.shape[0], block.shape[1]
    top = send(block[rows - h :], "tile", 1)
    bottom = send(block[:h], "tile", -1)
    band = jnp.concatenate([top, block, bottom], axis=0)
    left = send(band[:, cols - h :], "wave", 1)
    right = send(band[:, :h], "wave", -1)
    return jnp.concatenate([left, band, right], axis=1)


def blur_mat(psf, group, cols, h):
    k = psf.shape[0]
    win_cols = cols + 2 * h
    shape_c = (cols, k, win_cols)
    col_gap = lax.broadcasted_iota(jnp.int32, shape_c, 2) - lax.broadcasted_iota(jnp.int32, shape_c, 0)
    hot = (col_gap == lax.broadcasted_iota(jnp.int32, shape_c, 1)).astype(psf.dtype)
    strip = jnp.einsum("ab,xbX->xaX", psf, hot, preferred_element_type=jnp.float32)
    strip = strip.astype(psf.dtype).reshape(cols, k * win_cols)
    total = (group + 2 * h) * win_cols
    blocks = [
        jnp.pad(strip, ((0, 0), (y * win_cols, total - y * win_cols - k * win_cols)))
        for y in range(group)
    ]
    return jnp.concatenate(blocks, axis=0)


def blur(field, mat, group, h):
    rows, cols, waves = field.shape
    near = window(field, h)
    win_cols = cols + 2 * h
    flat = near.reshape(-1, waves)
    span = (group + 2 * h) * win_cols
    outs = [
        jnp.dot(mat, flat[g * win_cols : g * win_cols + span], preferred_element_type=jnp.float32)
        for g in range(0, rows, group)
    ]
    return jnp.concatenate(outs, axis=0)


def shards(coefficients, profile_basis, point_spread, observed):
    rows, cols, profiles = coefficients.shape
    waves = profile_basis.shape[1]
    h = point_spread.shape[0] // 2
    opacity = jnp.dot(
        coefficients.reshape(rows * cols, profiles), profile_basis, preferred_element_type=jnp.float32
    )
    spectra = jnp.exp(-opacity).astype(jnp.bfloat16)
    group = 4 if rows % 4 == 0 else rows
    forward = blur_mat(point_spread, group, cols, h)
    adjoint = blur_mat(point_spread[::-1, ::-1], group, cols, h)
    blurred = blur(spectra.reshape(rows, cols, waves), forward, group, h)
    measured = observed.transpose(1, 2, 0).reshape(rows * cols, waves).astype(jnp.float32)
    residual = (blurred - measured).astype(jnp.bfloat16)
    adjoint_field = blur(residual.reshape(rows, cols, waves), adjoint, group, h)
    tau_grad = (-spectra.astype(jnp.float32) * adjoint_field).astype(jnp.bfloat16)
    coef_grad = lax.dot_general(
        tau_grad, profile_basis, (((1,), (1,)), ((), ())), preferred_element_type=jnp.float32
    )
    return coef_grad.astype(jnp.bfloat16).reshape(rows, cols, profiles)


def solution(mesh):
    placed = (P("tile", "wave", None), P(), P(), P(None, "tile", "wave"))
    return jax.shard_map(
        shards, mesh=mesh, in_specs=placed, out_specs=P("tile", "wave", None), check_vma=False
    )
```

time: 96.2 us -> 76.1 us (0.79)
  the two profiles are of different devices: /device:TPU:71 before, /device:TPU:89 now
where the time goes in v2:
time: 76.1 us; the launch traced here: 75.8 us
  waiting for transfers between devices  30.6 us (40%)
  starting transfers between devices  27.3 us (36%)
  matrix products  13.4 us (18%)
  local copies, waits for them, and re-layouts  3.39 us (4%)
  other arithmetic  0.77 us (1%)
    ppermute x8, waiting for transfers between devices, send(): return lax.ppermute(block, axis, pairs)  30.6 us
    ppermute x8, starting transfers between devices, send(): return lax.ppermute(block, axis, pairs)  27.3 us
    dot_general x1, matrix products, shards(): jnp.dot(coefficients.reshape(rows * cols, profiles), profile_basis, prefe...  5.81 us
    dot_general x1, matrix products, shards(): lax.dot_general(tau_grad, profile_basis, (((1,), (1,)), ((), ())), prefer...  4.41 us
    dot_general x8, matrix products, blur(): jnp.dot(mat, flat[g * win_cols:g * win_cols + span], preferred_element_ty...  2.76 us
    unnamed x6, local copies, waits for them, and re-layouts  1.82 us
  transfers between devices with their start and end apart: 8, of which 8 were waited for; matrix products, arithmetic and copies ran while one was open for 1% of the time, Pallas kernels for 0%

profile of v2, /device:TPU:89, one launch (start us, length us, event | category | flops | bytes accessed | tf_op | source)
XLA Modules:
  0.0 75.8 jit_solution(1603973891662543909)
XLA Ops:
  0.0 5.8 %fusion.1 = bf16[512,512]{1,0:T(8,128)(2,1)S(1)} fusion(bf16[512,4096]{1,0:T(8,128)(2,1)} %bitcast.61, bf16[4096,512]{1,0:T(8,128)(2,1)} %param.5), kind=kOutput, calls=%fused_computation.5 | convolution fusion | flops 2148007936 | bytes 8912896 | tf_op jit(solution)/shard_map/dot_general | solution.py:56
  5.9 6.7 %collective-permute-start = (bf16[8,32,512]{2,1,0:T(8,128)(2,1)S(1)}, bf16[8,32,512]{2,1,0:T(8,128)(2,1)S(1)}, u32[]{:S(2)}, u32[]{:S(2)}) collective-permute-start(bf16[8,32,512]{2,1,0:T(8,128)(2,1)S(1)} %bitcast.60), channel_id=1, source_target_pairs={{0,1},{1,2},{2,3},{3,4},{4,5},{5,6},{6,7},{7,8},{8,9},{9,10},{10,1... | collective-permute-start | bytes 786440 | tf_op jit(solution)/shard_map/ppermute | solution.py:10
  12.5 1.9 %collective-permute-start.1 = (bf16[8,32,512]{2,1,0:T(8,128)(2,1)S(1)}, bf16[8,32,512]{2,1,0:T(8,128)(2,1)S(1)}, u32[]{:S(2)}, u32[]{:S(2)}) collective-permute-start(bf16[8,32,512]{2,1,0:T(8,128)(2,1)S(1)} %bitcast.59), channel_id=1, source_target_pairs={{1,0},{2,1},{3,2},{4,3},{5,4},{6,5},{7,6},{8,7},{9,8},{10,9},{11,1... | collective-permute-start | bytes 786440 | tf_op jit(solution)/shard_map/ppermute | solution.py:10
  14.5 3.9 %collective-permute-done = bf16[8,32,512]{2,1,0:T(8,128)(2,1)S(1)} collective-permute-done((bf16[8,32,512]{2,1,0:T(8,128)(2,1)S(1)}, bf16[8,32,512]{2,1,0:T(8,128)(2,1)S(1)}, u32[]{:S(2)}, u32[]{:S(2)}) %collective-permute-start) | collective-permute-done | bytes 262176 | tf_op jit(solution)/shard_map/ppermute | solution.py:10
  18.4 6.6 %collective-permute-done.1 = bf16[8,32,512]{2,1,0:T(8,128)(2,1)S(1)} collective-permute-done((bf16[8,32,512]{2,1,0:T(8,128)(2,1)S(1)}, bf16[8,32,512]{2,1,0:T(8,128)(2,1)S(1)}, u32[]{:S(2)}, u32[]{:S(2)}) %collective-permute-start.1) | collective-permute-done | bytes 262176 | tf_op jit(solution)/shard_map/ppermute | solution.py:10
  25.1 2.0 %collective-permute-start.2 = (bf16[32,8,512]{2,1,0:T(8,128)(2,1)S(1)}, bf16[32,8,512]{2,1,0:T(8,128)(2,1)S(1)}, u32[]{:S(2)}, u32[]{:S(2)}) collective-permute-start(bf16[32,8,512]{2,1,0:T(8,128)(2,1)S(1)} %get-tuple-element.17), channel_id=1, source_target_pairs={{0,32},{32,64},{64,96},{96,128},{128,160},{160,192},{192,224},{1,3... | collective-permute-start | bytes 786440 | tf_op jit(solution)/shard_map/ppermute | solution.py:10
  27.1 3.3 %collective-permute-start.3 = (bf16[32,8,512]{2,1,0:T(8,128)(2,1)S(1)}, bf16[32,8,512]{2,1,0:T(8,128)(2,1)S(1)}, u32[]{:S(2)}, u32[]{:S(2)}) collective-permute-start(bf16[32,8,512]{2,1,0:T(8,128)(2,1)S(1)} %get-tuple-element.18), channel_id=1, source_target_pairs={{32,0},{64,32},{96,64},{128,96},{160,128},{192,160},{224,192},{33,... | collective-permute-start | bytes 786440 | tf_op jit(solution)/shard_map/ppermute | solution.py:10
  30.4 0.2 fusion.3
  30.7 1.4 %collective-permute-done.2 = bf16[32,8,512]{2,1,0:T(8,128)(2,1)S(1)} collective-permute-done((bf16[32,8,512]{2,1,0:T(8,128)(2,1)S(1)}, bf16[32,8,512]{2,1,0:T(8,128)(2,1)S(1)}, u32[]{:S(2)}, u32[]{:S(2)}) %collective-permute-start.2) | collective-permute-done | bytes 262176 | tf_op jit(solution)/shard_map/ppermute | solution.py:10
  32.2 4.1 %collective-permute-done.3 = bf16[32,8,512]{2,1,0:T(8,128)(2,1)S(1)} collective-permute-done((bf16[32,8,512]{2,1,0:T(8,128)(2,1)S(1)}, bf16[32,8,512]{2,1,0:T(8,128)(2,1)S(1)}, u32[]{:S(2)}, u32[]{:S(2)}) %collective-permute-start.3) | collective-permute-done | bytes 262176 | tf_op jit(solution)/shard_map/ppermute | solution.py:10
  36.4 0.5 fusion.44
  37.0 0.3 fusion.27
  37.4 0.3 fusion.29
  37.7 0.3 fusion.31
  38.1 0.3 fusion.33
  38.4 0.3 copy-done
  39.0 5.4 %collective-permute-start.4 = (bf16[8,32,512]{2,1,0:T(8,128)(2,1)S(1)}, bf16[8,32,512]{2,1,0:T(8,128)(2,1)S(1)}, u32[]{:S(2)}, u32[]{:S(2)}) collective-permute-start(bf16[8,32,512]{2,1,0:T(8,128)(2,1)S(1)} %bitcast.58), channel_id=1, source_target_pairs={{0,1},{1,2},{2,3},{3,4},{4,5},{5,6},{6,7},{7,8},{8,9},{9,10},{10,1... | collective-permute-start | bytes 786440 | tf_op jit(solution)/shard_map/ppermute | solution.py:10
  44.5 1.9 %collective-permute-start.5 = (bf16[8,32,512]{2,1,0:T(8,128)(2,1)S(1)}, bf16[8,32,512]{2,1,0:T(8,128)(2,1)S(1)}, u32[]{:S(2)}, u32[]{:S(2)}) collective-permute-start(bf16[8,32,512]{2,1,0:T(8,128)(2,1)S(1)} %bitcast.57), channel_id=1, source_target_pairs={{1,0},{2,1},{3,2},{4,3},{5,4},{6,5},{7,6},{8,7},{9,8},{10,9},{11,1... | collective-permute-start | bytes 786440 | tf_op jit(solution)/shard_map/ppermute | solution.py:10
  46.6 1.2 %collective-permute-done.4 = bf16[8,32,512]{2,1,0:T(8,128)(2,1)S(1)} collective-permute-done((bf16[8,32,512]{2,1,0:T(8,128)(2,1)S(1)}, bf16[8,32,512]{2,1,0:T(8,128)(2,1)S(1)}, u32[]{:S(2)}, u32[]{:S(2)}) %collective-permute-start.4) | collective-permute-done | bytes 262176 | tf_op jit(solution)/shard_map/ppermute | solution.py:10
  47.8 6.5 %collective-permute-done.5 = bf16[8,32,512]{2,1,0:T(8,128)(2,1)S(1)} collective-permute-done((bf16[8,32,512]{2,1,0:T(8,128)(2,1)S(1)}, bf16[8,32,512]{2,1,0:T(8,128)(2,1)S(1)}, u32[]{:S(2)}, u32[]{:S(2)}) %collective-permute-start.5) | collective-permute-done | bytes 262176 | tf_op jit(solution)/shard_map/ppermute | solution.py:10
  54.3 4.2 %collective-permute-start.6 = (bf16[32,8,512]{2,1,0:T(8,128)(2,1)S(1)}, bf16[32,8,512]{2,1,0:T(8,128)(2,1)S(1)}, u32[]{:S(2)}, u32[]{:S(2)}) collective-permute-start(bf16[32,8,512]{2,1,0:T(8,128)(2,1)S(1)} %get-tuple-element.13), channel_id=1, source_target_pairs={{0,32},{32,64},{64,96},{96,128},{128,160},{160,192},{192,224},{1,3... | collective-permute-start | bytes 786440 | tf_op jit(solution)/shard_map/ppermute | solution.py:10
  58.5 1.9 %collective-permute-start.7 = (bf16[32,8,512]{2,1,0:T(8,128)(2,1)S(1)}, bf16[32,8,512]{2,1,0:T(8,128)(2,1)S(1)}, u32[]{:S(2)}, u32[]{:S(2)}) collective-permute-start(bf16[32,8,512]{2,1,0:T(8,128)(2,1)S(1)} %get-tuple-element.14), channel_id=1, source_target_pairs={{32,0},{64,32},{96,64},{128,96},{160,128},{192,160},{224,192},{33,... | collective-permute-start | bytes 786440 | tf_op jit(solution)/shard_map/ppermute | solution.py:10
  60.5 0.2 fusion.2
  60.9 0.9 %collective-permute-done.6 = bf16[32,8,512]{2,1,0:T(8,128)(2,1)S(1)} collective-permute-done((bf16[32,8,512]{2,1,0:T(8,128)(2,1)S(1)}, bf16[32,8,512]{2,1,0:T(8,128)(2,1)S(1)}, u32[]{:S(2)}, u32[]{:S(2)}) %collective-permute-start.6) | collective-permute-done | bytes 262176 | tf_op jit(solution)/shard_map/ppermute | solution.py:10
  61.8 5.9 %collective-permute-done.7 = bf16[32,8,512]{2,1,0:T(8,128)(2,1)S(1)} collective-permute-done((bf16[32,8,512]{2,1,0:T(8,128)(2,1)S(1)}, bf16[32,8,512]{2,1,0:T(8,128)(2,1)S(1)}, u32[]{:S(2)}, u32[]{:S(2)}) %collective-permute-start.7) | collective-permute-done | bytes 262176 | tf_op jit(solution)/shard_map/ppermute | solution.py:10
  67.9 0.5 fusion.43
  68.5 0.3 fusion.35
  68.8 0.3 fusion.37
  69.2 0.3 fusion.39
  69.5 0.3 fusion.41
  69.9 1.5 %copy-done.2 = bf16[4096,512]{1,0:T(8,128)(2,1)S(1)} copy-done((bf16[4096,512]{1,0:T(8,128)(2,1)S(1)}, bf16[4096,512]{1,0:T(8,128)(2,1)}, u32[]{:S(2)}) %copy-start.2) | copy-done | bytes 4194328
  71.3 4.4 %convolution_convert_fusion = bf16[512,4096]{1,0:T(8,128)(2,1)} fusion(bf16[4096,512]{1,0:T(8,128)(2,1)S(1)} %copy-done.2, f32[128,512]{1,0:T(8,128)S(1)} %fusion.35, f32[128,512]{1,0:T(8,128)S(1)} %fusion.37, f32[128,512]{1,0:T(8,128)S(1)} %fusion.39, f32[128,512]{1,0:T(8,128)S(1)} %fusion.41, bf16[512,512]{1,0:T(8,128)(2,1)S(1)} %fusion.1), kind=kOutput, calls=%fused_computation | convolution fusion | flops 2151415808 | bytes 9961472 | tf_op jit(solution)/shard_map/dot_general | solution.py:68
  (15 shorter events, 1.3 us)
Async XLA Ops:
  0.0 30.4 %copy-start.1 = (bf16[17,17]{1,0:T(8,128)(2,1)S(1)}, bf16[17,17]{1,0:T(8,128)(2,1)}, u32[]{:S(2)}) copy-start(bf16[17,17]{1,0:T(8,128)(2,1)} %param.6) | copy-start | bytes 1738
  5.9 12.5 %collective-permute-start = (bf16[8,32,512]{2,1,0:T(8,128)(2,1)S(1)}, bf16[8,32,512]{2,1,0:T(8,128)(2,1)S(1)}, u32[]{:S(2)}, u32[]{:S(2)}) collective-permute-start(bf16[8,32,512]{2,1,0:T(8,128)(2,1)S(1)} %bitcast.60), channel_id=1, source_target_pairs={{0,1},{1,2},{2,3},{3,4},{4,5},{5,6},{6,7},{7,8},{8,9},{9,10},{10,1... | collective-permute-start | bytes 786440 | tf_op jit(solution)/shard_map/ppermute | solution.py:10
  12.5 12.5 %collective-permute-start.1 = (bf16[8,32,512]{2,1,0:T(8,128)(2,1)S(1)}, bf16[8,32,512]{2,1,0:T(8,128)(2,1)S(1)}, u32[]{:S(2)}, u32[]{:S(2)}) collective-permute-start(bf16[8,32,512]{2,1,0:T(8,128)(2,1)S(1)} %bitcast.59), channel_id=1, source_target_pairs={{1,0},{2,1},{3,2},{4,3},{5,4},{6,5},{7,6},{8,7},{9,8},{10,9},{11,1... | collective-permute-start | bytes 786440 | tf_op jit(solution)/shard_map/ppermute | solution.py:10
  25.1 7.1 %collective-permute-start.2 = (bf16[32,8,512]{2,1,0:T(8,128)(2,1)S(1)}, bf16[32,8,512]{2,1,0:T(8,128)(2,1)S(1)}, u32[]{:S(2)}, u32[]{:S(2)}) collective-permute-start(bf16[32,8,512]{2,1,0:T(8,128)(2,1)S(1)} %get-tuple-element.17), channel_id=1, source_target_pairs={{0,32},{32,64},{64,96},{96,128},{128,160},{160,192},{192,224},{1,3... | collective-permute-start | bytes 786440 | tf_op jit(solution)/shard_map/ppermute | solution.py:10
  27.1 9.2 %collective-permute-start.3 = (bf16[32,8,512]{2,1,0:T(8,128)(2,1)S(1)}, bf16[32,8,512]{2,1,0:T(8,128)(2,1)S(1)}, u32[]{:S(2)}, u32[]{:S(2)}) collective-permute-start(bf16[32,8,512]{2,1,0:T(8,128)(2,1)S(1)} %get-tuple-element.18), channel_id=1, source_target_pairs={{32,0},{64,32},{96,64},{128,96},{160,128},{192,160},{224,192},{33,... | collective-permute-start | bytes 786440 | tf_op jit(solution)/shard_map/ppermute | solution.py:10
  37.7 1.0 %copy-start = (bf16[512,16,32]{0,2,1:T(8,128)(2,1)S(1)}, bf16[512,16,32]{0,2,1:T(8,128)(2,1)}, u32[]{:S(2)}) copy-start(bf16[512,16,32]{0,2,1:T(8,128)(2,1)} %param.7) | copy-start | bytes 1572868
  39.0 8.8 %collective-permute-start.4 = (bf16[8,32,512]{2,1,0:T(8,128)(2,1)S(1)}, bf16[8,32,512]{2,1,0:T(8,128)(2,1)S(1)}, u32[]{:S(2)}, u32[]{:S(2)}) collective-permute-start(bf16[8,32,512]{2,1,0:T(8,128)(2,1)S(1)} %bitcast.58), channel_id=1, source_target_pairs={{0,1},{1,2},{2,3},{3,4},{4,5},{5,6},{6,7},{7,8},{8,9},{9,10},{10,1... | collective-permute-start | bytes 786440 | tf_op jit(solution)/shard_map/ppermute | solution.py:10
  44.5 9.8 %collective-permute-start.5 = (bf16[8,32,512]{2,1,0:T(8,128)(2,1)S(1)}, bf16[8,32,512]{2,1,0:T(8,128)(2,1)S(1)}, u32[]{:S(2)}, u32[]{:S(2)}) collective-permute-start(bf16[8,32,512]{2,1,0:T(8,128)(2,1)S(1)} %bitcast.57), channel_id=1, source_target_pairs={{1,0},{2,1},{3,2},{4,3},{5,4},{6,5},{7,6},{8,7},{9,8},{10,9},{11,1... | collective-permute-start | bytes 786440 | tf_op jit(solution)/shard_map/ppermute | solution.py:10
  54.3 7.5 %collective-permute-start.6 = (bf16[32,8,512]{2,1,0:T(8,128)(2,1)S(1)}, bf16[32,8,512]{2,1,0:T(8,128)(2,1)S(1)}, u32[]{:S(2)}, u32[]{:S(2)}) collective-permute-start(bf16[32,8,512]{2,1,0:T(8,128)(2,1)S(1)} %get-tuple-element.13), channel_id=1, source_target_pairs={{0,32},{32,64},{64,96},{96,128},{128,160},{160,192},{192,224},{1,3... | collective-permute-start | bytes 786440 | tf_op jit(solution)/shard_map/ppermute | solution.py:10
  58.5 9.2 %collective-permute-start.7 = (bf16[32,8,512]{2,1,0:T(8,128)(2,1)S(1)}, bf16[32,8,512]{2,1,0:T(8,128)(2,1)S(1)}, u32[]{:S(2)}, u32[]{:S(2)}) collective-permute-start(bf16[32,8,512]{2,1,0:T(8,128)(2,1)S(1)} %get-tuple-element.14), channel_id=1, source_target_pairs={{32,0},{64,32},{96,64},{128,96},{160,128},{192,160},{224,192},{33,... | collective-permute-start | bytes 786440 | tf_op jit(solution)/shard_map/ppermute | solution.py:10
  69.2 2.2 %copy-start.2 = (bf16[4096,512]{1,0:T(8,128)(2,1)S(1)}, bf16[4096,512]{1,0:T(8,128)(2,1)}, u32[]{:S(2)}) copy-start(bf16[4096,512]{1,0:T(8,128)(2,1)} %param.5) | copy-start | bytes 12582916

commit v3 on v2

--- a/solution.py
+++ b/solution.py
@@ -36,34 +36,47 @@
     return jnp.concatenate(blocks, axis=0)
 
 
-def blur(field, mat, group, h):
-    rows, cols, waves = field.shape
-    near = window(field, h)
-    win_cols = cols + 2 * h
+def blur(near, mat, group, out_rows, out_cols, h):
+    waves = near.shape[-1]
+    win_cols = out_cols + 2 * h
     flat = near.reshape(-1, waves)
     span = (group + 2 * h) * win_cols
     outs = [
         jnp.dot(mat, flat[g * win_cols : g * win_cols + span], preferred_element_type=jnp.float32)
-        for g in range(0, rows, group)
+        for g in range(0, out_rows, group)
     ]
     return jnp.concatenate(outs, axis=0)
+
+
+def inside(rows, cols, h):
+    top = lax.axis_index("tile") * rows - h
+    left = lax.axis_index("wave") * cols - h
+    shape = (rows + 2 * h, cols + 2 * h, 1)
+    r = lax.broadcasted_iota(jnp.int32, shape, 0) + top
+    c = lax.broadcasted_iota(jnp.int32, shape, 1) + left
+    total_r = lax.axis_size("tile") * rows
+    total_c = lax.axis_size("wave") * cols
+    return (r >= 0) & (r < total_r) & (c >= 0) & (c < total_c)
 
 
 def shards(coefficients, profile_basis, point_spread, observed):
     rows, cols, profiles = coefficients.shape
     waves = profile_basis.shape[1]
     h = point_spread.shape[0] // 2
+    measured = window(observed.transpose(1, 2, 0), h)
     opacity = jnp.dot(
         coefficients.reshape(rows * cols, profiles), profile_basis, preferred_element_type=jnp.float32
     )
     spectra = jnp.exp(-opacity).astype(jnp.bfloat16)
     group = 4 if rows % 4 == 0 else rows
-    forward = blur_mat(point_spread, group, cols, h)
+    forward = blur_mat(point_spread, group, cols + 2 * h, h)
     adjoint = blur_mat(point_spread[::-1, ::-1], group, cols, h)
-    blurred = blur(spectra.reshape(rows, cols, waves), forward, group, h)
-    measured = observed.transpose(1, 2, 0).reshape(rows * cols, waves).astype(jnp.float32)
-    residual = (blurred - measured).astype(jnp.bfloat16)
-    adjoint_field = blur(residual.reshape(rows, cols, waves), adjoint, group, h)
+    near = window(spectra.reshape(rows, cols, waves), 2 * h)
+    blurred = blur(near, forward, group, rows + 2 * h, cols + 2 * h, h)
+    blurred = blurred.reshape(rows + 2 * h, cols + 2 * h, waves)
+    residual = (blurred - measured.astype(jnp.float32)).astype(jnp.bfloat16)
+    residual = jnp.where(inside(rows, cols, h), residual, jnp.zeros_like(residual))
+    adjoint_field = blur(residual, adjoint, group, rows, cols, h)
     tau_grad = (-spectra.astype(jnp.float32) * adjoint_field).astype(jnp.bfloat16)
     coef_grad = lax.dot_general(
         tau_grad, profile_basis, (((1,), (1,)), ((), ())), preferred_element_type=jnp.float32

time: 76.1 us -> 74.7 us (0.982)
  the two profiles are of different devices: /device:TPU:89 before, /device:TPU:29 now
where the time goes in v3:
time: 74.7 us; the launch traced here: 74.3 us
  starting transfers between devices  25.3 us (34%)
  waiting for transfers between devices  20.2 us (27%)
  matrix products  17.1 us (23%)
  local copies, waits for them, and re-layouts  8.79 us (12%)
  other arithmetic  2.7 us (4%)
    ppermute x8, starting transfers between devices, send(): return lax.ppermute(block, axis, pairs)  25.3 us
    ppermute x8, waiting for transfers between devices, send(): return lax.ppermute(block, axis, pairs)  20.2 us
    dot_general x1, matrix products, shards(): jnp.dot(coefficients.reshape(rows * cols, profiles), profile_basis, prefe...  5.84 us
    dot_general x12, matrix products, blur(): jnp.dot(mat, flat[g * win_cols:g * win_cols + span], preferred_element_ty...  4.99 us
    dot_general x1, matrix products, shards(): lax.dot_general(tau_grad, profile_basis, (((1,), (1,)), ((), ())), prefer...  4.41 us
    reshape x2, local copies, waits for them, and re-layouts, blur_mat(): strip = strip.astype(psf.dtype).reshape(cols, k * win_cols)  2.87 us
    slice x2, local copies, waits for them, and re-layouts, blur(): flat[g * win_cols:g * win_cols + span]  1.93 us
    dot_general x2, matrix products, blur_mat(): jnp.einsum('ab,xbX->xaX', psf, hot, preferred_element_type=jnp.float32)  1.85 us
  transfers between devices with their start and end apart: 8, of which 3 were waited for; matrix products, arithmetic and copies ran while one was open for 18% of the time, Pallas kernels for 0%

profile of v3, /device:TPU:29, one launch (start us, length us, event | category | flops | bytes accessed | tf_op | source)
XLA Modules:
  0.0 74.3 jit_solution(10323702928005272042)
XLA Ops:
  0.0 5.8 %fusion.2 = bf16[512,512]{1,0:T(8,128)(2,1)S(1)} fusion(bf16[512,4096]{1,0:T(8,128)(2,1)} %bitcast.62, bf16[4096,512]{1,0:T(8,128)(2,1)} %param.5), kind=kOutput, calls=%fused_computation.11 | convolution fusion | flops 2148007936 | bytes 8912896 | tf_op jit(solution)/shard_map/dot_general | solution.py:67
  5.9 5.5 %collective-permute-start = (bf16[16,32,512]{2,1,0:T(8,128)(2,1)S(1)}, bf16[16,32,512]{2,1,0:T(8,128)(2,1)S(1)}, u32[]{:S(2)}, u32[]{:S(2)}) collective-permute-start(bf16[16,32,512]{2,1,0:T(8,128)(2,1)S(1)} %bitcast.46), channel_id=1, source_target_pairs={{0,1},{1,2},{2,3},{3,4},{4,5},{5,6},{6,7},{7,8},{8,9},{9,10},{10,1... | collective-permute-start | bytes 1572872 | tf_op jit(solution)/shard_map/ppermute | solution.py:10
  11.3 1.9 %collective-permute-start.1 = (bf16[16,32,512]{2,1,0:T(8,128)(2,1)S(1)}, bf16[16,32,512]{2,1,0:T(8,128)(2,1)S(1)}, u32[]{:S(2)}, u32[]{:S(2)}) collective-permute-start(bf16[16,32,512]{2,1,0:T(8,128)(2,1)S(1)} %bitcast.47), channel_id=1, source_target_pairs={{1,0},{2,1},{3,2},{4,3},{5,4},{6,5},{7,6},{8,7},{9,8},{10,9},{11,1... | collective-permute-start | bytes 1572872 | tf_op jit(solution)/shard_map/ppermute | solution.py:10
  13.3 0.8 %fusion.49 = (bf16[8,32,512]{2,1,0:T(8,128)(2,1)}, bf16[8,32,512]{2,1,0:T(8,128)(2,1)}) fusion(bf16[16,32,512]{2,1,0:T(8,128)(2,1)S(1)} %bitcast.42), kind=kLoop, calls=%fused_computation.72 | loop fusion | bytes 1048576 | tf_op jit(solution)/shard_map/slice | solution.py:15
  14.1 4.5 %collective-permute-start.4 = (bf16[8,32,512]{2,1,0:T(8,128)(2,1)}, bf16[8,32,512]{2,1,0:T(8,128)(2,1)S(1)}, u32[]{:S(2)}, u32[]{:S(2)}) collective-permute-start(bf16[8,32,512]{2,1,0:T(8,128)(2,1)} %get-tuple-element.21), channel_id=1, source_target_pairs={{0,1},{1,2},{2,3},{3,4},{4,5},{5,6},{6,7},{7,8},{8,9},{9,10},{10,1... | collective-permute-start | bytes 786440 | tf_op jit(solution)/shard_map/ppermute | solution.py:10
  18.6 2.1 %collective-permute-start.5 = (bf16[8,32,512]{2,1,0:T(8,128)(2,1)}, bf16[8,32,512]{2,1,0:T(8,128)(2,1)S(1)}, u32[]{:S(2)}, u32[]{:S(2)}) collective-permute-start(bf16[8,32,512]{2,1,0:T(8,128)(2,1)} %get-tuple-element.22), channel_id=1, source_target_pairs={{1,0},{2,1},{3,2},{4,3},{5,4},{6,5},{7,6},{8,7},{9,8},{10,9},{11,1... | collective-permute-start | bytes 786440 | tf_op jit(solution)/shard_map/ppermute | solution.py:10
  20.9 0.9 %fusion.4 = bf16[32,17,48]{2,1,0:T(8,128)(2,1)} fusion(bf16[17,17]{1,0:T(8,128)(2,1)S(1)} %rev.3), kind=kOutput, calls=%fused_computation.23 | convolution fusion | flops 966144 | bytes 52802 | tf_op jit(solution)/shard_map/ab,xbX->xaX/dot_general | solution.py:29
  21.8 9.7 %collective-permute-done.1 = bf16[16,32,512]{2,1,0:T(8,128)(2,1)S(1)} collective-permute-done((bf16[16,32,512]{2,1,0:T(8,128)(2,1)S(1)}, bf16[16,32,512]{2,1,0:T(8,128)(2,1)S(1)}, u32[]{:S(2)}, u32[]{:S(2)}) %collective-permute-start.1) | collective-permute-done | bytes 524320 | tf_op jit(solution)/shard_map/ppermute | solution.py:10
  31.7 1.3 %fusion.48 = (bf16[48,16,512]{2,1,0:T(8,128)(2,1)}, bf16[48,16,512]{2,1,0:T(8,128)(2,1)}) fusion(bf16[48,32,512]{2,1,0:T(8,128)(2,1)S(1)} %pad_maximum_fusion.1), kind=kLoop, calls=%fused_computation.71 | loop fusion | bytes 3145728 | tf_op jit(solution)/shard_map/slice | solution.py:18
  33.0 1.9 %collective-permute-start.2 = (bf16[48,16,512]{2,1,0:T(8,128)(2,1)}, bf16[48,16,512]{2,1,0:T(8,128)(2,1)S(1)}, u32[]{:S(2)}, u32[]{:S(2)}) collective-permute-start(bf16[48,16,512]{2,1,0:T(8,128)(2,1)} %get-tuple-element.17), channel_id=1, source_target_pairs={{0,32},{32,64},{64,96},{96,128},{128,160},{160,192},{192,224},{1,3... | collective-permute-start | bytes 2359304 | tf_op jit(solution)/shard_map/ppermute | solution.py:10
  34.9 3.4 %collective-permute-start.3 = (bf16[48,16,512]{2,1,0:T(8,128)(2,1)}, bf16[48,16,512]{2,1,0:T(8,128)(2,1)}, u32[]{:S(2)}, u32[]{:S(2)}) collective-permute-start(bf16[48,16,512]{2,1,0:T(8,128)(2,1)} %get-tuple-element.18), channel_id=1, source_target_pairs={{32,0},{64,32},{96,64},{128,96},{160,128},{192,160},{224,192},{33,... | collective-permute-start | bytes 2359304 | tf_op jit(solution)/shard_map/ppermute | solution.py:10
  38.3 1.0 %fusion.3 = bf16[48,17,64]{2,1,0:T(8,128)(2,1)} fusion(bf16[17,17]{1,0:T(8,128)(2,1)S(1)} %copy-done.2), kind=kOutput, calls=%fused_computation.21 | convolution fusion | flops 1932288 | bytes 105026 | tf_op jit(solution)/shard_map/ab,xbX->xaX/dot_general | solution.py:29
  39.2 1.2 %reshape.75 = bf16[48,1088]{1,0:T(8,128)(2,1)S(1)} reshape(bf16[48,17,64]{2,1,0:T(8,128)(2,1)} %fusion.3) | data formatting | bytes 208896 | tf_op jit(solution)/shard_map/reshape | solution.py:30
  40.4 1.7 %reshape.74 = bf16[32,816]{1,0:T(8,128)(2,1)} reshape(bf16[32,17,48]{2,1,0:T(8,128)(2,1)} %fusion.4) | data formatting | bytes 104448 | tf_op jit(solution)/shard_map/reshape | solution.py:30
  42.2 4.0 %collective-permute-start.6 = (bf16[32,8,512]{2,1,0:T(8,128)(2,1)S(1)}, bf16[32,8,512]{2,1,0:T(8,128)(2,1)S(1)}, u32[]{:S(2)}, u32[]{:S(2)}) collective-permute-start(bf16[32,8,512]{2,1,0:T(8,128)(2,1)S(1)} %get-tuple-element.19), channel_id=1, source_target_pairs={{0,32},{32,64},{64,96},{96,128},{128,160},{160,192},{192,224},{1,3... | collective-permute-start | bytes 786440 | tf_op jit(solution)/shard_map/ppermute | solution.py:10
  46.3 1.9 %collective-permute-start.7 = (bf16[32,8,512]{2,1,0:T(8,128)(2,1)S(1)}, bf16[32,8,512]{2,1,0:T(8,128)(2,1)S(1)}, u32[]{:S(2)}, u32[]{:S(2)}) collective-permute-start(bf16[32,8,512]{2,1,0:T(8,128)(2,1)S(1)} %get-tuple-element.20), channel_id=1, source_target_pairs={{32,0},{64,32},{96,64},{128,96},{160,128},{192,160},{224,192},{33,... | collective-permute-start | bytes 786440 | tf_op jit(solution)/shard_map/ppermute | solution.py:10
  48.2 6.5 %collective-permute-done.2 = bf16[48,16,512]{2,1,0:T(8,128)(2,1)S(1)} collective-permute-done((bf16[48,16,512]{2,1,0:T(8,128)(2,1)}, bf16[48,16,512]{2,1,0:T(8,128)(2,1)S(1)}, u32[]{:S(2)}, u32[]{:S(2)}) %collective-permute-start.2) | collective-permute-done | bytes 786464 | tf_op jit(solution)/shard_map/ppermute | solution.py:10
  54.7 3.9 %collective-permute-done.3 = bf16[48,16,512]{2,1,0:T(8,128)(2,1)} collective-permute-done((bf16[48,16,512]{2,1,0:T(8,128)(2,1)}, bf16[48,16,512]{2,1,0:T(8,128)(2,1)}, u32[]{:S(2)}, u32[]{:S(2)}) %collective-permute-start.3) | collective-permute-done | bytes 786464 | tf_op jit(solution)/shard_map/ppermute | solution.py:10
  58.6 1.4 %pad_maximum_fusion = bf16[48,64,512]{2,1,0:T(8,128)(2,1)S(1)} fusion(bf16[48,16,512]{2,1,0:T(8,128)(2,1)} %collective-permute-done.3, bf16[16,32,512]{2,1,0:T(8,128)(2,1)S(1)} %collective-permute-done.1, bf16[16,32,512]{2,1,0:T(8,128)(2,1)S(1)} %bitcast.49, bf16[16,32,512]{2,1,0:T(8,128)(2,1)S(1)} %collective-permute-done, ...), kind=kLoop, calls=%fused_computation.1 | loop fusion | flops 15728640 | bytes 6291456 | tf_op jit(solution)/shard_map/concatenate | solution.py:20
  60.0 1.4 %fusion.46 = (bf16[20,64,512]{2,1,0:T(8,128)(2,1)S(1)}, bf16[20,64,512]{2,1,0:T(8,128)(2,1)S(1)}, bf16[20,64,512]{2,1,0:T(8,128)(2,1)S(1)}, bf16[20,64,512]{2,1,...) fusion(bf16[48,64,512]{2,1,0:T(8,128)(2,1)S(1)} %pad_maximum_fusion), kind=kLoop, calls=%fused_computation.69 | loop fusion | bytes 20971520 | tf_op jit(solution)/shard_map/slice | solution.py:45
  61.4 0.5 convolution_dynamic-update-slice_fusion.7
  61.9 0.5 convolution_dynamic-update-slice_fusion.6
  62.3 0.5 convolution_dynamic-update-slice_fusion.5
  62.8 0.5 convolution_dynamic-update-slice_fusion.4
  63.3 0.4 convolution_dynamic-update-slice_fusion.3
  63.7 0.4 convolution_dynamic-update-slice_fusion.2
  64.2 0.4 convolution_dynamic-update-slice_fusion.1
  64.6 0.4 convolution_dynamic-update-slice_fusion
  65.1 1.0 %fusion = bf16[32,48,512]{2,1,0:T(8,128)(2,1)S(1)} fusion(f32[32,48,512]{2,1,0:T(8,128)S(1)} %bitcast.45, bf16[32,8,512]{2,1,0:T(8,128)(2,1)S(1)} %collective-permute-done.7, bf16[8,32,512]{2,1,0:T(8,128)(2,1)S(1)} %collective-permute-done.5, bf16[16,32,512]{2,1,0:T(8,128)(2,1)S(1)} %bitcast.44, bf16[8,32,512]{2,1,0:T(8,128)(2,1)S(1)} %collective-permute-done.4, ...), kind=kLoop, calls=%fused_computation.3 | loop fusion | flops 10223616 | bytes 6292992 | tf_op jit(solution)/shard_map/jit(_where)/select_n | solution.py:78
  66.2 0.5 fusion.47
  68.4 1.5 %copy-done.3 = bf16[4096,512]{1,0:T(8,128)(2,1)S(1)} copy-done((bf16[4096,512]{1,0:T(8,128)(2,1)S(1)}, bf16[4096,512]{1,0:T(8,128)(2,1)}, u32[]{:S(2)}) %copy-start.3) | copy-done | bytes 4194328
  69.9 4.4 %convolution_convert_fusion = bf16[512,4096]{1,0:T(8,128)(2,1)} fusion(bf16[4096,512]{1,0:T(8,128)(2,1)S(1)} %copy-done.3, f32[128,512]{1,0:T(8,128)S(1)} %fusion.30, f32[128,512]{1,0:T(8,128)S(1)} %fusion.32, f32[128,512]{1,0:T(8,128)S(1)} %fusion.34, f32[128,512]{1,0:T(8,128)S(1)} %fusion.36, bf16[512,512]{1,0:T(8,128)(2,1)S(1)} %fusion.2), kind=kOutput, calls=%fused_computation | convolution fusion | flops 2151415808 | bytes 9961472 | tf_op jit(solution)/shard_map/dot_general | solution.py:81
  (22 shorter events, 2.1 us)
Async XLA Ops:
  0.0 13.3 %copy-start = (bf16[512,16,32]{0,2,1:T(8,128)(2,1)S(1)}, bf16[512,16,32]{0,2,1:T(8,128)(2,1)}, u32[]{:S(2)}) copy-start(bf16[512,16,32]{0,2,1:T(8,128)(2,1)} %param.7) | copy-start | bytes 1572868
  0.0 20.8 %copy-start.2 = (bf16[17,17]{1,0:T(8,128)(2,1)S(1)}, bf16[17,17]{1,0:T(8,128)(2,1)}, u32[]{:S(2)}) copy-start(bf16[17,17]{1,0:T(8,128)(2,1)} %param.6) | copy-start | bytes 1738
  5.9 15.9 %collective-permute-start = (bf16[16,32,512]{2,1,0:T(8,128)(2,1)S(1)}, bf16[16,32,512]{2,1,0:T(8,128)(2,1)S(1)}, u32[]{:S(2)}, u32[]{:S(2)}) collective-permute-start(bf16[16,32,512]{2,1,0:T(8,128)(2,1)S(1)} %bitcast.46), channel_id=1, source_target_pairs={{0,1},{1,2},{2,3},{3,4},{4,5},{5,6},{6,7},{7,8},{8,9},{9,10},{10,1... | collective-permute-start | bytes 1572872 | tf_op jit(solution)/shard_map/ppermute | solution.py:10
  11.3 20.2 %collective-permute-start.1 = (bf16[16,32,512]{2,1,0:T(8,128)(2,1)S(1)}, bf16[16,32,512]{2,1,0:T(8,128)(2,1)S(1)}, u32[]{:S(2)}, u32[]{:S(2)}) collective-permute-start(bf16[16,32,512]{2,1,0:T(8,128)(2,1)S(1)} %bitcast.47), channel_id=1, source_target_pairs={{1,0},{2,1},{3,2},{4,3},{5,4},{6,5},{7,6},{8,7},{9,8},{10,9},{11,1... | collective-permute-start | bytes 1572872 | tf_op jit(solution)/shard_map/ppermute | solution.py:10
  14.1 28.1 %collective-permute-start.4 = (bf16[8,32,512]{2,1,0:T(8,128)(2,1)}, bf16[8,32,512]{2,1,0:T(8,128)(2,1)S(1)}, u32[]{:S(2)}, u32[]{:S(2)}) collective-permute-start(bf16[8,32,512]{2,1,0:T(8,128)(2,1)} %get-tuple-element.21), channel_id=1, source_target_pairs={{0,1},{1,2},{2,3},{3,4},{4,5},{5,6},{6,7},{7,8},{8,9},{9,10},{10,1... | collective-permute-start | bytes 786440 | tf_op jit(solution)/shard_map/ppermute | solution.py:10
  18.6 23.5 %collective-permute-start.5 = (bf16[8,32,512]{2,1,0:T(8,128)(2,1)}, bf16[8,32,512]{2,1,0:T(8,128)(2,1)S(1)}, u32[]{:S(2)}, u32[]{:S(2)}) collective-permute-start(bf16[8,32,512]{2,1,0:T(8,128)(2,1)} %get-tuple-element.22), channel_id=1, source_target_pairs={{1,0},{2,1},{3,2},{4,3},{5,4},{6,5},{7,6},{8,7},{9,8},{10,9},{11,1... | collective-permute-start | bytes 786440 | tf_op jit(solution)/shard_map/ppermute | solution.py:10
  33.0 21.8 %collective-permute-start.2 = (bf16[48,16,512]{2,1,0:T(8,128)(2,1)}, bf16[48,16,512]{2,1,0:T(8,128)(2,1)S(1)}, u32[]{:S(2)}, u32[]{:S(2)}) collective-permute-start(bf16[48,16,512]{2,1,0:T(8,128)(2,1)} %get-tuple-element.17), channel_id=1, source_target_pairs={{0,32},{32,64},{64,96},{96,128},{128,160},{160,192},{192,224},{1,3... | collective-permute-start | bytes 2359304 | tf_op jit(solution)/shard_map/ppermute | solution.py:10
  34.9 23.8 %collective-permute-start.3 = (bf16[48,16,512]{2,1,0:T(8,128)(2,1)}, bf16[48,16,512]{2,1,0:T(8,128)(2,1)}, u32[]{:S(2)}, u32[]{:S(2)}) collective-permute-start(bf16[48,16,512]{2,1,0:T(8,128)(2,1)} %get-tuple-element.18), channel_id=1, source_target_pairs={{32,0},{64,32},{96,64},{128,96},{160,128},{192,160},{224,192},{33,... | collective-permute-start | bytes 2359304 | tf_op jit(solution)/shard_map/ppermute | solution.py:10
  42.2 22.9 %collective-permute-start.6 = (bf16[32,8,512]{2,1,0:T(8,128)(2,1)S(1)}, bf16[32,8,512]{2,1,0:T(8,128)(2,1)S(1)}, u32[]{:S(2)}, u32[]{:S(2)}) collective-permute-start(bf16[32,8,512]{2,1,0:T(8,128)(2,1)S(1)} %get-tuple-element.19), channel_id=1, source_target_pairs={{0,32},{32,64},{64,96},{96,128},{128,160},{160,192},{192,224},{1,3... | collective-permute-start | bytes 786440 | tf_op jit(solution)/shard_map/ppermute | solution.py:10
  46.3 18.8 %collective-permute-start.7 = (bf16[32,8,512]{2,1,0:T(8,128)(2,1)S(1)}, bf16[32,8,512]{2,1,0:T(8,128)(2,1)S(1)}, u32[]{:S(2)}, u32[]{:S(2)}) collective-permute-start(bf16[32,8,512]{2,1,0:T(8,128)(2,1)S(1)} %get-tuple-element.20), channel_id=1, source_target_pairs={{32,0},{64,32},{96,64},{128,96},{160,128},{192,160},{224,192},{33,... | collective-permute-start | bytes 786440 | tf_op jit(solution)/shard_map/ppermute | solution.py:10
  66.2 0.8 %copy-start.1 = (bf16[32,816]{1,0:T(8,128)(2,1)S(1)}, bf16[32,816]{1,0:T(8,128)(2,1)}, u32[]{:S(2)}) copy-start(bf16[32,816]{1,0:T(8,128)(2,1)} %reshape.74) | copy-start | bytes 156676
  67.7 2.2 %copy-start.3 = (bf16[4096,512]{1,0:T(8,128)(2,1)S(1)}, bf16[4096,512]{1,0:T(8,128)(2,1)}, u32[]{:S(2)}) copy-start(bf16[4096,512]{1,0:T(8,128)(2,1)} %param.5) | copy-start | bytes 12582916

commit v4 on v3

--- a/solution.py
+++ b/solution.py
@@ -59,11 +59,43 @@
     return (r >= 0) & (r < total_r) & (c >= 0) & (c < total_c)
 
 
+def windows(spectra, measured, h):
+    rows, cols, waves = spectra.shape
+    wide = 2 * h
+    down = jnp.concatenate([spectra[rows - wide :], measured[rows - h :]], axis=0)
+    up = jnp.concatenate([spectra[:wide], measured[:h]], axis=0)
+    above = send(down, "tile", 1)
+    below = send(up, "tile", -1)
+    band_s = jnp.concatenate([above[:wide], spectra, below[:wide]], axis=0)
+    band_m = jnp.concatenate([above[wide:], measured, below[wide:]], axis=0)
+    split = band_s.shape[0] * wide
+
+    def edge(lo, hi_s, hi_m):
+        return jnp.concatenate(
+            [band_s[:, lo : lo + wide].reshape(-1, waves), band_m[:, hi_m : hi_m + h].reshape(-1, waves)],
+            axis=0,
+        )
+
+    left = send(edge(cols - wide, None, cols - h), "wave", 1)
+    right = send(edge(0, None, 0), "wave", -1)
+
+    def parts(piece):
+        return (
+            piece[:split].reshape(band_s.shape[0], wide, waves),
+            piece[split:].reshape(band_m.shape[0], h, waves),
+        )
+
+    left_s, left_m = parts(left)
+    right_s, right_m = parts(right)
+    near_s = jnp.concatenate([left_s, band_s, right_s], axis=1)
+    near_m = jnp.concatenate([left_m, band_m, right_m], axis=1)
+    return near_s, near_m
+
+
 def shards(coefficients, profile_basis, point_spread, observed):
     rows, cols, profiles = coefficients.shape
     waves = profile_basis.shape[1]
     h = point_spread.shape[0] // 2
-    measured = window(observed.transpose(1, 2, 0), h)
     opacity = jnp.dot(
         coefficients.reshape(rows * cols, profiles), profile_basis, preferred_element_type=jnp.float32
     )
@@ -71,7 +103,7 @@
     group = 4 if rows % 4 == 0 else rows
     forward = blur_mat(point_spread, group, cols + 2 * h, h)
     adjoint = blur_mat(point_spread[::-1, ::-1], group, cols, h)
-    near = window(spectra.reshape(rows, cols, waves), 2 * h)
+    near, measured = windows(spectra.reshape(rows, cols, waves), observed.transpose(1, 2, 0), h)
     blurred = blur(near, forward, group, rows + 2 * h, cols + 2 * h, h)
     blurred = blurred.reshape(rows + 2 * h, cols + 2 * h, waves)
     residual = (blurred - measured.astype(jnp.float32)).astype(jnp.bfloat16)

time: 74.7 us -> 89.6 us (1.20)
  the two profiles are of different devices: /device:TPU:29 before, /device:TPU:38 now
where the time goes in v4:
time: 89.6 us; the launch traced here: 89.2 us
  waiting for transfers between devices  41.4 us (46%)
  starting transfers between devices  17.9 us (20%)
  matrix products  15.7 us (18%)
  local copies, waits for them, and re-layouts  10.1 us (11%)
  other arithmetic  3.87 us (4%)
    ppermute x4, waiting for transfers between devices, send(): return lax.ppermute(block, axis, pairs)  41.4 us
    ppermute x4, starting transfers between devices, send(): return lax.ppermute(block, axis, pairs)  17.9 us
    dot_general x1, matrix products, shards(): jnp.dot(coefficients.reshape(rows * cols, profiles), profile_basis, prefe...  5.8 us
    dot_general x12, matrix products, blur(): jnp.dot(mat, flat[g * win_cols:g * win_cols + span], preferred_element_ty...  5 us
    dot_general x1, matrix products, shards(): lax.dot_general(tau_grad, profile_basis, (((1,), (1,)), ((), ())), prefer...  4.4 us
    slice x2, local copies, waits for them, and re-layouts, parts(): piece[:split].reshape(band_s.shape[0], wide, waves)  2.37 us
    unnamed x6, local copies, waits for them, and re-layouts  2.14 us
    concatenate x2, other arithmetic, edge(): jnp.concatenate([band_s[:, lo:lo + wide].reshape(-1, waves), band_m[:, hi...  2.08 us
  transfers between devices with their start and end apart: 4, of which 3 were waited for; matrix products, arithmetic and copies ran while one was open for 4% of the time, Pallas kernels for 0%

profile of v4, /device:TPU:38, one launch (start us, length us, event | category | flops | bytes accessed | tf_op | source)
XLA Modules:
  0.0 89.2 jit_solution(14702034344469576870)
XLA Ops:
  0.0 1.1 %fusion.50 = (bf16[8,32,512]{2,1,0:T(8,128)(2,1)S(1)}, bf16[8,32,512]{2,1,0:T(8,128)(2,1)S(1)}) fusion(bf16[16,32,512]{2,1,0:T(8,128)(2,1)} %bitcast.57), kind=kLoop, calls=%fused_computation.79 | loop fusion | bytes 1048576 | tf_op jit(solution)/shard_map/slice | solution.py:65
  1.1 5.8 %fusion.2 = bf16[512,512]{1,0:T(8,128)(2,1)S(1)} fusion(bf16[512,4096]{1,0:T(8,128)(2,1)} %bitcast.77, bf16[4096,512]{1,0:T(8,128)(2,1)} %param.5), kind=kOutput, calls=%fused_computation.11 | convolution fusion | flops 2148007936 | bytes 8912896 | tf_op jit(solution)/shard_map/dot_general | solution.py:99
  7.0 1.9 %collective-permute-start = (bf16[24,32,512]{2,1,0:T(8,128)(2,1)S(1)}, bf16[24,32,512]{2,1,0:T(8,128)(2,1)S(1)}, u32[]{:S(2)}, u32[]{:S(2)}) collective-permute-start(bf16[24,32,512]{2,1,0:T(8,128)(2,1)S(1)} %get-tuple-element.21), channel_id=1, source_target_pairs={{0,1},{1,2},{2,3},{3,4},{4,5},{5,6},{6,7},{7,8},{8,9},{9,10},{10,1... | collective-permute-start | bytes 2359304 | tf_op jit(solution)/shard_map/ppermute | solution.py:10
  8.9 7.0 %collective-permute-start.1 = (bf16[24,32,512]{2,1,0:T(8,128)(2,1)S(1)}, bf16[24,32,512]{2,1,0:T(8,128)(2,1)S(1)}, u32[]{:S(2)}, u32[]{:S(2)}) collective-permute-start(bf16[24,32,512]{2,1,0:T(8,128)(2,1)S(1)} %get-tuple-element.22), channel_id=1, source_target_pairs={{1,0},{2,1},{3,2},{4,3},{5,4},{6,5},{7,6},{8,7},{9,8},{10,9},{11,1... | collective-permute-start | bytes 2359304 | tf_op jit(solution)/shard_map/ppermute | solution.py:10
  15.9 16.2 %collective-permute-done = bf16[24,32,512]{2,1,0:T(8,128)(2,1)S(1)} collective-permute-done((bf16[24,32,512]{2,1,0:T(8,128)(2,1)S(1)}, bf16[24,32,512]{2,1,0:T(8,128)(2,1)S(1)}, u32[]{:S(2)}, u32[]{:S(2)}) %collective-permute-start) | collective-permute-done | bytes 786464 | tf_op jit(solution)/shard_map/ppermute | solution.py:10
  32.6 0.7 copy-done
  33.3 1.0 %pad_maximum_fusion.3 = bf16[1024,512]{1,0:T(8,128)(2,1)} fusion(bf16[256,512]{1,0:T(8,128)(2,1)S(1)} %get-tuple-element.20, bf16[768,512]{1,0:T(8,128)(2,1)S(1)} %bitcast.64), kind=kLoop, calls=%fused_computation.25 | loop fusion | flops 2097152 | bytes 2097152 | tf_op jit(solution)/shard_map/concatenate | solution.py:74
  34.3 7.1 %collective-permute-start.3 = (bf16[1024,512]{1,0:T(8,128)(2,1)}, bf16[1024,512]{1,0:T(8,128)(2,1)}, u32[]{:S(2)}, u32[]{:S(2)}) collective-permute-start(bf16[1024,512]{1,0:T(8,128)(2,1)} %pad_maximum_fusion.3), channel_id=1, source_target_pairs={{32,0},{64,32},{96,64},{128,96},{160,128},{192,160},{224,192},{33,... | collective-permute-start | bytes 3145736 | tf_op jit(solution)/shard_map/ppermute | solution.py:10
  41.4 1.0 %pad_maximum_fusion.2 = bf16[1024,512]{1,0:T(8,128)(2,1)} fusion(bf16[256,512]{1,0:T(8,128)(2,1)S(1)} %get-tuple-element.19, bf16[768,512]{1,0:T(8,128)(2,1)S(1)} %bitcast.63), kind=kLoop, calls=%fused_computation.24 | loop fusion | flops 2097152 | bytes 2097152 | tf_op jit(solution)/shard_map/concatenate | solution.py:74
  42.4 1.9 %collective-permute-start.2 = (bf16[1024,512]{1,0:T(8,128)(2,1)}, bf16[1024,512]{1,0:T(8,128)(2,1)}, u32[]{:S(2)}, u32[]{:S(2)}) collective-permute-start(bf16[1024,512]{1,0:T(8,128)(2,1)} %pad_maximum_fusion.2), channel_id=1, source_target_pairs={{0,32},{32,64},{64,96},{96,128},{128,160},{160,192},{192,224},{1,3... | collective-permute-start | bytes 3145736 | tf_op jit(solution)/shard_map/ppermute | solution.py:10
  45.4 19.1 %collective-permute-done.3 = bf16[1024,512]{1,0:T(8,128)(2,1)} collective-permute-done((bf16[1024,512]{1,0:T(8,128)(2,1)}, bf16[1024,512]{1,0:T(8,128)(2,1)}, u32[]{:S(2)}, u32[]{:S(2)}) %collective-permute-start.3) | collective-permute-done | bytes 1048608 | tf_op jit(solution)/shard_map/ppermute | solution.py:10
  64.5 1.2 %slice.161 = bf16[768,512]{1,0:T(8,128)(2,1)S(1)} slice(bf16[1024,512]{1,0:T(8,128)(2,1)} %collective-permute-done.3), slice={[0:768], [0:512]} | slice | bytes 1572864 | tf_op jit(solution)/shard_map/slice | solution.py:84
  65.7 6.1 %collective-permute-done.2 = bf16[1024,512]{1,0:T(8,128)(2,1)} collective-permute-done((bf16[1024,512]{1,0:T(8,128)(2,1)}, bf16[1024,512]{1,0:T(8,128)(2,1)}, u32[]{:S(2)}, u32[]{:S(2)}) %collective-permute-start.2) | collective-permute-done | bytes 1048608 | tf_op jit(solution)/shard_map/ppermute | solution.py:10
  71.8 1.2 %slice.159 = bf16[768,512]{1,0:T(8,128)(2,1)S(1)} slice(bf16[1024,512]{1,0:T(8,128)(2,1)} %collective-permute-done.2), slice={[0:768], [0:512]} | slice | bytes 1572864 | tf_op jit(solution)/shard_map/slice | solution.py:84
  73.3 1.4 %fusion.47 = (bf16[20,64,512]{2,1,0:T(8,128)(2,1)S(1)}, bf16[20,64,512]{2,1,0:T(8,128)(2,1)S(1)}, bf16[20,64,512]{2,1,0:T(8,128)(2,1)S(1)}, bf16[20,64,512]{2,1,...) fusion(bf16[48,64,512]{2,1,0:T(8,128)(2,1)S(1)} %pad_maximum_fusion), kind=kLoop, calls=%fused_computation.76 | loop fusion | bytes 20971520 | tf_op jit(solution)/shard_map/slice | solution.py:45
  74.7 0.5 convolution_dynamic-update-slice_fusion.7
  75.2 0.5 convolution_dynamic-update-slice_fusion.6
  75.6 0.5 convolution_dynamic-update-slice_fusion.5
  76.1 0.5 convolution_dynamic-update-slice_fusion.4
  76.6 0.5 convolution_dynamic-update-slice_fusion.3
  77.0 0.4 convolution_dynamic-update-slice_fusion.2
  77.5 0.4 convolution_dynamic-update-slice_fusion.1
  77.9 0.4 convolution_dynamic-update-slice_fusion
  78.4 1.0 %slice_bitcast_fusion = bf16[32,8,512]{2,1,0:T(8,128)(2,1)S(1)} fusion(bf16[1024,512]{1,0:T(8,128)(2,1)} %collective-permute-done.3), kind=kLoop, calls=%fused_computation.58 | loop fusion | bytes 524288 | tf_op jit(solution)/shard_map/reshape | solution.py:85
  79.4 1.0 %slice_bitcast_fusion.1 = bf16[32,8,512]{2,1,0:T(8,128)(2,1)S(1)} fusion(bf16[1024,512]{1,0:T(8,128)(2,1)} %collective-permute-done.2), kind=kLoop, calls=%fused_computation.59 | loop fusion | bytes 524288 | tf_op jit(solution)/shard_map/reshape | solution.py:85
  80.3 1.1 %fusion = bf16[32,48,512]{2,1,0:T(8,128)(2,1)S(1)} fusion(f32[32,48,512]{2,1,0:T(8,128)S(1)} %bitcast.62, bf16[32,8,512]{2,1,0:T(8,128)(2,1)S(1)} %slice_bitcast_fusion, bf16[8,32,512]{2,1,0:T(8,128)(2,1)S(1)} %slice.158, bf16[16,32,512]{2,1,0:T(8,128)(2,1)S(1)} %bitcast.59, bf16[8,32,512]{2,1,0:T(8,128)(2,1)S(1)} %slice.157, ...), kind=kLoop, calls=%fused_computation.3 | loop fusion | flops 10223616 | bytes 6292992 | tf_op jit(solution)/shard_map/jit(_where)/select_n | solution.py:110
  81.4 0.5 fusion.48
  82.3 0.3 fusion.31
  82.7 0.3 fusion.33
  83.0 0.3 fusion.35
  83.4 1.5 %copy-done.2 = bf16[4096,512]{1,0:T(8,128)(2,1)S(1)} copy-done((bf16[4096,512]{1,0:T(8,128)(2,1)S(1)}, bf16[4096,512]{1,0:T(8,128)(2,1)}, u32[]{:S(2)}) %copy-start.2) | copy-done | bytes 4194328
  84.8 4.4 %convolution_convert_fusion = bf16[512,4096]{1,0:T(8,128)(2,1)} fusion(bf16[4096,512]{1,0:T(8,128)(2,1)S(1)} %copy-done.2, f32[128,512]{1,0:T(8,128)S(1)} %fusion.31, f32[128,512]{1,0:T(8,128)S(1)} %fusion.33, f32[128,512]{1,0:T(8,128)S(1)} %fusion.35, f32[128,512]{1,0:T(8,128)S(1)} %fusion.37, bf16[512,512]{1,0:T(8,128)(2,1)S(1)} %fusion.2), kind=kOutput, calls=%fused_computation | convolution fusion | flops 2151415808 | bytes 9961472 | tf_op jit(solution)/shard_map/dot_general | solution.py:113
  (23 shorter events, 2.2 us)
Async XLA Ops:
  7.0 25.1 %collective-permute-start = (bf16[24,32,512]{2,1,0:T(8,128)(2,1)S(1)}, bf16[24,32,512]{2,1,0:T(8,128)(2,1)S(1)}, u32[]{:S(2)}, u32[]{:S(2)}) collective-permute-start(bf16[24,32,512]{2,1,0:T(8,128)(2,1)S(1)} %get-tuple-element.21), channel_id=1, source_target_pairs={{0,1},{1,2},{2,3},{3,4},{4,5},{5,6},{6,7},{7,8},{8,9},{9,10},{10,1... | collective-permute-start | bytes 2359304 | tf_op jit(solution)/shard_map/ppermute | solution.py:10
  8.9 23.2 %collective-permute-start.1 = (bf16[24,32,512]{2,1,0:T(8,128)(2,1)S(1)}, bf16[24,32,512]{2,1,0:T(8,128)(2,1)S(1)}, u32[]{:S(2)}, u32[]{:S(2)}) collective-permute-start(bf16[24,32,512]{2,1,0:T(8,128)(2,1)S(1)} %get-tuple-element.22), channel_id=1, source_target_pairs={{1,0},{2,1},{3,2},{4,3},{5,4},{6,5},{7,6},{8,7},{9,8},{10,9},{11,1... | collective-permute-start | bytes 2359304 | tf_op jit(solution)/shard_map/ppermute | solution.py:10
  32.2 1.0 %copy-start = (bf16[512,16,32]{0,2,1:T(8,128)(2,1)S(1)}, bf16[512,16,32]{0,2,1:T(8,128)(2,1)}, u32[]{:S(2)}) copy-start(bf16[512,16,32]{0,2,1:T(8,128)(2,1)} %param.7) | copy-start | bytes 1572868
  32.6 11.8 %copy-start.1 = (bf16[17,17]{1,0:T(8,128)(2,1)S(1)}, bf16[17,17]{1,0:T(8,128)(2,1)}, u32[]{:S(2)}) copy-start(bf16[17,17]{1,0:T(8,128)(2,1)} %param.6) | copy-start | bytes 1738
  34.3 30.2 %collective-permute-start.3 = (bf16[1024,512]{1,0:T(8,128)(2,1)}, bf16[1024,512]{1,0:T(8,128)(2,1)}, u32[]{:S(2)}, u32[]{:S(2)}) collective-permute-start(bf16[1024,512]{1,0:T(8,128)(2,1)} %pad_maximum_fusion.3), channel_id=1, source_target_pairs={{32,0},{64,32},{96,64},{128,96},{160,128},{192,160},{224,192},{33,... | collective-permute-start | bytes 3145736 | tf_op jit(solution)/shard_map/ppermute | solution.py:10
  42.4 29.4 %collective-permute-start.2 = (bf16[1024,512]{1,0:T(8,128)(2,1)}, bf16[1024,512]{1,0:T(8,128)(2,1)}, u32[]{:S(2)}, u32[]{:S(2)}) collective-permute-start(bf16[1024,512]{1,0:T(8,128)(2,1)} %pad_maximum_fusion.2), channel_id=1, source_target_pairs={{0,32},{32,64},{64,96},{96,128},{128,160},{160,192},{192,224},{1,3... | collective-permute-start | bytes 3145736 | tf_op jit(solution)/shard_map/ppermute | solution.py:10
  82.7 2.2 %copy-start.2 = (bf16[4096,512]{1,0:T(8,128)(2,1)S(1)}, bf16[4096,512]{1,0:T(8,128)(2,1)}, u32[]{:S(2)}) copy-start(bf16[4096,512]{1,0:T(8,128)(2,1)} %param.5) | copy-start | bytes 12582916

commit v5 on v2

--- a/solution.py
+++ b/solution.py
@@ -14,10 +14,14 @@
     rows, cols = block.shape[0], block.shape[1]
     top = send(block[rows - h :], "tile", 1)
     bottom = send(block[:h], "tile", -1)
-    band = jnp.concatenate([top, block, bottom], axis=0)
-    left = send(band[:, cols - h :], "wave", 1)
-    right = send(band[:, :h], "wave", -1)
-    return jnp.concatenate([left, band, right], axis=1)
+    left = send(block[:, cols - h :], "wave", 1)
+    right = send(block[:, :h], "wave", -1)
+    corner_left = send(jnp.concatenate([top[:, cols - h :], bottom[:, cols - h :]], axis=0), "wave", 1)
+    corner_right = send(jnp.concatenate([top[:, :h], bottom[:, :h]], axis=0), "wave", -1)
+    upper = jnp.concatenate([corner_left[:h], top, corner_right[:h]], axis=1)
+    middle = jnp.concatenate([left, block, right], axis=1)
+    lower = jnp.concatenate([corner_left[h:], bottom, corner_right[h:]], axis=1)
+    return jnp.concatenate([upper, middle, lower], axis=0)
 
 
 def blur_mat(psf, group, cols, h):

time: 76.1 us -> 78.3 us (1.029)
  the two profiles are of different devices: /device:TPU:89 before, /device:TPU:30 now
where the time goes in v5:
time: 78.3 us; the launch traced here: 77.8 us
  starting transfers between devices  42.1 us (54%)
  waiting for transfers between devices  17.2 us (22%)
  matrix products  13.4 us (17%)
  local copies, waits for them, and re-layouts  3.72 us (5%)
  other arithmetic  0.98 us (1%)
    ppermute x12, starting transfers between devices, send(): return lax.ppermute(block, axis, pairs)  42.1 us
    ppermute x12, waiting for transfers between devices, send(): return lax.ppermute(block, axis, pairs)  17.2 us
    dot_general x1, matrix products, shards(): jnp.dot(coefficients.reshape(rows * cols, profiles), profile_basis, prefe...  5.81 us
    dot_general x1, matrix products, shards(): lax.dot_general(tau_grad, profile_basis, (((1,), (1,)), ((), ())), prefer...  4.4 us
    dot_general x8, matrix products, blur(): jnp.dot(mat, flat[g * win_cols:g * win_cols + span], preferred_element_ty...  2.77 us
    unnamed x6, local copies, waits for them, and re-layouts  2.17 us
  transfers between devices with their start and end apart: 12, of which 6 were waited for; matrix products, arithmetic and copies ran while one was open for 1% of the time, Pallas kernels for 0%

profile of v5, /device:TPU:30, one launch (start us, length us, event | category | flops | bytes accessed | tf_op | source)
XLA Modules:
  0.0 77.8 jit_solution(1722696990880382123)
XLA Ops:
  0.0 5.8 %fusion.1 = bf16[512,512]{1,0:T(8,128)(2,1)S(1)} fusion(bf16[512,4096]{1,0:T(8,128)(2,1)} %bitcast.61, bf16[4096,512]{1,0:T(8,128)(2,1)} %param.5), kind=kOutput, calls=%fused_computation.3 | convolution fusion | flops 2148007936 | bytes 8912896 | tf_op jit(solution)/shard_map/dot_general | solution.py:60
  5.9 1.9 %collective-permute-start = (bf16[8,32,512]{2,1,0:T(8,128)(2,1)S(1)}, bf16[8,32,512]{2,1,0:T(8,128)(2,1)S(1)}, u32[]{:S(2)}, u32[]{:S(2)}) collective-permute-start(bf16[8,32,512]{2,1,0:T(8,128)(2,1)S(1)} %bitcast.58), channel_id=1, source_target_pairs={{0,1},{1,2},{2,3},{3,4},{4,5},{5,6},{6,7},{7,8},{8,9},{9,10},{10,1... | collective-permute-start | bytes 786440 | tf_op jit(solution)/shard_map/ppermute | solution.py:10
  7.8 7.9 %collective-permute-start.1 = (bf16[8,32,512]{2,1,0:T(8,128)(2,1)S(1)}, bf16[8,32,512]{2,1,0:T(8,128)(2,1)S(1)}, u32[]{:S(2)}, u32[]{:S(2)}) collective-permute-start(bf16[8,32,512]{2,1,0:T(8,128)(2,1)S(1)} %bitcast.57), channel_id=1, source_target_pairs={{1,0},{2,1},{3,2},{4,3},{5,4},{6,5},{7,6},{8,7},{9,8},{10,9},{11,1... | collective-permute-start | bytes 786440 | tf_op jit(solution)/shard_map/ppermute | solution.py:10
  15.7 2.6 %collective-permute-start.4 = (bf16[16,8,512]{2,1,0:T(8,128)(2,1)S(1)}, bf16[16,8,512]{2,1,0:T(8,128)(2,1)S(1)}, u32[]{:S(2)}, u32[]{:S(2)}) collective-permute-start(bf16[16,8,512]{2,1,0:T(8,128)(2,1)S(1)} %get-tuple-element.23), channel_id=1, source_target_pairs={{0,32},{32,64},{64,96},{96,128},{128,160},{160,192},{192,224},{1,3... | collective-permute-start | bytes 393224 | tf_op jit(solution)/shard_map/ppermute | solution.py:10
  18.3 3.3 %collective-permute-start.5 = (bf16[16,8,512]{2,1,0:T(8,128)(2,1)S(1)}, bf16[16,8,512]{2,1,0:T(8,128)(2,1)S(1)}, u32[]{:S(2)}, u32[]{:S(2)}) collective-permute-start(bf16[16,8,512]{2,1,0:T(8,128)(2,1)S(1)} %get-tuple-element.24), channel_id=1, source_target_pairs={{32,0},{64,32},{96,64},{128,96},{160,128},{192,160},{224,192},{33,... | collective-permute-start | bytes 393224 | tf_op jit(solution)/shard_map/ppermute | solution.py:10
  21.9 0.4 collective-permute-done.1
  22.4 4.3 %collective-permute-start.2 = (bf16[16,8,512]{2,1,0:T(8,128)(2,1)S(1)}, bf16[16,8,512]{2,1,0:T(8,128)(2,1)S(1)}, u32[]{:S(2)}, u32[]{:S(2)}) collective-permute-start(bf16[16,8,512]{2,1,0:T(8,128)(2,1)S(1)} %pad_maximum_fusion.1), channel_id=1, source_target_pairs={{0,32},{32,64},{64,96},{96,128},{128,160},{160,192},{192,224},{1,3... | collective-permute-start | bytes 393224 | tf_op jit(solution)/shard_map/ppermute | solution.py:10
  27.2 1.9 %collective-permute-start.3 = (bf16[16,8,512]{2,1,0:T(8,128)(2,1)S(1)}, bf16[16,8,512]{2,1,0:T(8,128)(2,1)S(1)}, u32[]{:S(2)}, u32[]{:S(2)}) collective-permute-start(bf16[16,8,512]{2,1,0:T(8,128)(2,1)S(1)} %pad_maximum_fusion.2), channel_id=1, source_target_pairs={{32,0},{64,32},{96,64},{128,96},{160,128},{192,160},{224,192},{33,... | collective-permute-start | bytes 393224 | tf_op jit(solution)/shard_map/ppermute | solution.py:10
  29.2 0.8 collective-permute-done.2
  30.0 6.3 %collective-permute-done.3 = bf16[16,8,512]{2,1,0:T(8,128)(2,1)S(1)} collective-permute-done((bf16[16,8,512]{2,1,0:T(8,128)(2,1)S(1)}, bf16[16,8,512]{2,1,0:T(8,128)(2,1)S(1)}, u32[]{:S(2)}, u32[]{:S(2)}) %collective-permute-start.3) | collective-permute-done | bytes 131104 | tf_op jit(solution)/shard_map/ppermute | solution.py:10
  36.3 0.3 maximum_maximum_fusion
  36.6 0.5 fusion.45
  37.1 0.3 fusion.27
  37.4 0.3 fusion.29
  37.8 0.3 fusion.31
  38.1 0.3 fusion.33
  38.5 0.7 copy-done
  39.4 1.9 %collective-permute-start.6 = (bf16[8,32,512]{2,1,0:T(8,128)(2,1)S(1)}, bf16[8,32,512]{2,1,0:T(8,128)(2,1)S(1)}, u32[]{:S(2)}, u32[]{:S(2)}) collective-permute-start(bf16[8,32,512]{2,1,0:T(8,128)(2,1)S(1)} %bitcast.60), channel_id=1, source_target_pairs={{0,1},{1,2},{2,3},{3,4},{4,5},{5,6},{6,7},{7,8},{8,9},{9,10},{10,1... | collective-permute-start | bytes 786440 | tf_op jit(solution)/shard_map/ppermute | solution.py:10
  41.3 6.7 %collective-permute-start.7 = (bf16[8,32,512]{2,1,0:T(8,128)(2,1)S(1)}, bf16[8,32,512]{2,1,0:T(8,128)(2,1)S(1)}, u32[]{:S(2)}, u32[]{:S(2)}) collective-permute-start(bf16[8,32,512]{2,1,0:T(8,128)(2,1)S(1)} %bitcast.59), channel_id=1, source_target_pairs={{1,0},{2,1},{3,2},{4,3},{5,4},{6,5},{7,6},{8,7},{9,8},{10,9},{11,1... | collective-permute-start | bytes 786440 | tf_op jit(solution)/shard_map/ppermute | solution.py:10
  48.2 1.9 %collective-permute-done.6 = bf16[8,32,512]{2,1,0:T(8,128)(2,1)S(1)} collective-permute-done((bf16[8,32,512]{2,1,0:T(8,128)(2,1)S(1)}, bf16[8,32,512]{2,1,0:T(8,128)(2,1)S(1)}, u32[]{:S(2)}, u32[]{:S(2)}) %collective-permute-start.6) | collective-permute-done | bytes 262176 | tf_op jit(solution)/shard_map/ppermute | solution.py:10
  50.1 1.7 %collective-permute-done.7 = bf16[8,32,512]{2,1,0:T(8,128)(2,1)S(1)} collective-permute-done((bf16[8,32,512]{2,1,0:T(8,128)(2,1)S(1)}, bf16[8,32,512]{2,1,0:T(8,128)(2,1)S(1)}, u32[]{:S(2)}, u32[]{:S(2)}) %collective-permute-start.7) | collective-permute-done | bytes 262176 | tf_op jit(solution)/shard_map/ppermute | solution.py:10
  51.9 2.9 %collective-permute-start.8 = (bf16[16,8,512]{2,1,0:T(8,128)(2,1)S(1)}, bf16[16,8,512]{2,1,0:T(8,128)(2,1)S(1)}, u32[]{:S(2)}, u32[]{:S(2)}) collective-permute-start(bf16[16,8,512]{2,1,0:T(8,128)(2,1)S(1)} %pad_maximum_fusion.3), channel_id=1, source_target_pairs={{0,32},{32,64},{64,96},{96,128},{128,160},{160,192},{192,224},{1,3... | collective-permute-start | bytes 393224 | tf_op jit(solution)/shard_map/ppermute | solution.py:10
  54.9 2.5 %collective-permute-start.10 = (bf16[16,8,512]{2,1,0:T(8,128)(2,1)S(1)}, bf16[16,8,512]{2,1,0:T(8,128)(2,1)S(1)}, u32[]{:S(2)}, u32[]{:S(2)}) collective-permute-start(bf16[16,8,512]{2,1,0:T(8,128)(2,1)S(1)} %get-tuple-element.19), channel_id=1, source_target_pairs={{0,32},{32,64},{64,96},{96,128},{128,160},{160,192},{192,224},{1,3... | collective-permute-start | bytes 393224 | tf_op jit(solution)/shard_map/ppermute | solution.py:10
  57.3 3.4 %collective-permute-start.11 = (bf16[16,8,512]{2,1,0:T(8,128)(2,1)S(1)}, bf16[16,8,512]{2,1,0:T(8,128)(2,1)S(1)}, u32[]{:S(2)}, u32[]{:S(2)}) collective-permute-start(bf16[16,8,512]{2,1,0:T(8,128)(2,1)S(1)} %get-tuple-element.20), channel_id=1, source_target_pairs={{32,0},{64,32},{96,64},{128,96},{160,128},{192,160},{224,192},{33,... | collective-permute-start | bytes 393224 | tf_op jit(solution)/shard_map/ppermute | solution.py:10
  60.8 2.9 %collective-permute-start.9 = (bf16[16,8,512]{2,1,0:T(8,128)(2,1)S(1)}, bf16[16,8,512]{2,1,0:T(8,128)(2,1)S(1)}, u32[]{:S(2)}, u32[]{:S(2)}) collective-permute-start(bf16[16,8,512]{2,1,0:T(8,128)(2,1)S(1)} %pad_maximum_fusion.4), channel_id=1, source_target_pairs={{32,0},{64,32},{96,64},{128,96},{160,128},{192,160},{224,192},{33,... | collective-permute-start | bytes 393224 | tf_op jit(solution)/shard_map/ppermute | solution.py:10
  63.7 6.0 %collective-permute-done.9 = bf16[16,8,512]{2,1,0:T(8,128)(2,1)S(1)} collective-permute-done((bf16[16,8,512]{2,1,0:T(8,128)(2,1)S(1)}, bf16[16,8,512]{2,1,0:T(8,128)(2,1)S(1)}, u32[]{:S(2)}, u32[]{:S(2)}) %collective-permute-start.9) | collective-permute-done | bytes 131104 | tf_op jit(solution)/shard_map/ppermute | solution.py:10
  70.3 0.3 fusion.35
  70.6 0.3 fusion.37
  71.2 0.3 fusion.39
  71.6 0.3 fusion.41
  71.9 1.5 %copy-done.2 = bf16[4096,512]{1,0:T(8,128)(2,1)S(1)} copy-done((bf16[4096,512]{1,0:T(8,128)(2,1)S(1)}, bf16[4096,512]{1,0:T(8,128)(2,1)}, u32[]{:S(2)}) %copy-start.2) | copy-done | bytes 4194328
  73.4 4.4 %convolution_convert_fusion = bf16[512,4096]{1,0:T(8,128)(2,1)} fusion(bf16[4096,512]{1,0:T(8,128)(2,1)S(1)} %copy-done.2, f32[128,512]{1,0:T(8,128)S(1)} %fusion.35, f32[128,512]{1,0:T(8,128)S(1)} %fusion.37, f32[128,512]{1,0:T(8,128)S(1)} %fusion.39, f32[128,512]{1,0:T(8,128)S(1)} %fusion.41, bf16[512,512]{1,0:T(8,128)(2,1)S(1)} %fusion.1), kind=kOutput, calls=%fused_computation | convolution fusion | flops 2151415808 | bytes 9961472 | tf_op jit(solution)/shard_map/dot_general | solution.py:72
  (36 shorter events, 2.2 us)
Async XLA Ops:
  0.0 21.6 %copy-start.1 = (bf16[17,17]{1,0:T(8,128)(2,1)S(1)}, bf16[17,17]{1,0:T(8,128)(2,1)}, u32[]{:S(2)}) copy-start(bf16[17,17]{1,0:T(8,128)(2,1)} %param.6) | copy-start | bytes 1738
  5.9 16.1 %collective-permute-start = (bf16[8,32,512]{2,1,0:T(8,128)(2,1)S(1)}, bf16[8,32,512]{2,1,0:T(8,128)(2,1)S(1)}, u32[]{:S(2)}, u32[]{:S(2)}) collective-permute-start(bf16[8,32,512]{2,1,0:T(8,128)(2,1)S(1)} %bitcast.58), channel_id=1, source_target_pairs={{0,1},{1,2},{2,3},{3,4},{4,5},{5,6},{6,7},{7,8},{8,9},{9,10},{10,1... | collective-permute-start | bytes 786440 | tf_op jit(solution)/shard_map/ppermute | solution.py:10
  7.8 14.6 %collective-permute-start.1 = (bf16[8,32,512]{2,1,0:T(8,128)(2,1)S(1)}, bf16[8,32,512]{2,1,0:T(8,128)(2,1)S(1)}, u32[]{:S(2)}, u32[]{:S(2)}) collective-permute-start(bf16[8,32,512]{2,1,0:T(8,128)(2,1)S(1)} %bitcast.57), channel_id=1, source_target_pairs={{1,0},{2,1},{3,2},{4,3},{5,4},{6,5},{7,6},{8,7},{9,8},{10,9},{11,1... | collective-permute-start | bytes 786440 | tf_op jit(solution)/shard_map/ppermute | solution.py:10
  15.7 20.5 %collective-permute-start.4 = (bf16[16,8,512]{2,1,0:T(8,128)(2,1)S(1)}, bf16[16,8,512]{2,1,0:T(8,128)(2,1)S(1)}, u32[]{:S(2)}, u32[]{:S(2)}) collective-permute-start(bf16[16,8,512]{2,1,0:T(8,128)(2,1)S(1)} %get-tuple-element.23), channel_id=1, source_target_pairs={{0,32},{32,64},{64,96},{96,128},{128,160},{160,192},{192,224},{1,3... | collective-permute-start | bytes 393224 | tf_op jit(solution)/shard_map/ppermute | solution.py:10
  18.3 17.9 %collective-permute-start.5 = (bf16[16,8,512]{2,1,0:T(8,128)(2,1)S(1)}, bf16[16,8,512]{2,1,0:T(8,128)(2,1)S(1)}, u32[]{:S(2)}, u32[]{:S(2)}) collective-permute-start(bf16[16,8,512]{2,1,0:T(8,128)(2,1)S(1)} %get-tuple-element.24), channel_id=1, source_target_pairs={{32,0},{64,32},{96,64},{128,96},{160,128},{192,160},{224,192},{33,... | collective-permute-start | bytes 393224 | tf_op jit(solution)/shard_map/ppermute | solution.py:10
  22.4 7.5 %collective-permute-start.2 = (bf16[16,8,512]{2,1,0:T(8,128)(2,1)S(1)}, bf16[16,8,512]{2,1,0:T(8,128)(2,1)S(1)}, u32[]{:S(2)}, u32[]{:S(2)}) collective-permute-start(bf16[16,8,512]{2,1,0:T(8,128)(2,1)S(1)} %pad_maximum_fusion.1), channel_id=1, source_target_pairs={{0,32},{32,64},{64,96},{96,128},{128,160},{160,192},{192,224},{1,3... | collective-permute-start | bytes 393224 | tf_op jit(solution)/shard_map/ppermute | solution.py:10
  27.2 9.0 %collective-permute-start.3 = (bf16[16,8,512]{2,1,0:T(8,128)(2,1)S(1)}, bf16[16,8,512]{2,1,0:T(8,128)(2,1)S(1)}, u32[]{:S(2)}, u32[]{:S(2)}) collective-permute-start(bf16[16,8,512]{2,1,0:T(8,128)(2,1)S(1)} %pad_maximum_fusion.2), channel_id=1, source_target_pairs={{32,0},{64,32},{96,64},{128,96},{160,128},{192,160},{224,192},{33,... | collective-permute-start | bytes 393224 | tf_op jit(solution)/shard_map/ppermute | solution.py:10
  38.1 1.0 %copy-start = (bf16[512,16,32]{0,2,1:T(8,128)(2,1)S(1)}, bf16[512,16,32]{0,2,1:T(8,128)(2,1)}, u32[]{:S(2)}) copy-start(bf16[512,16,32]{0,2,1:T(8,128)(2,1)} %param.7) | copy-start | bytes 1572868
  39.4 10.7 %collective-permute-start.6 = (bf16[8,32,512]{2,1,0:T(8,128)(2,1)S(1)}, bf16[8,32,512]{2,1,0:T(8,128)(2,1)S(1)}, u32[]{:S(2)}, u32[]{:S(2)}) collective-permute-start(bf16[8,32,512]{2,1,0:T(8,128)(2,1)S(1)} %bitcast.60), channel_id=1, source_target_pairs={{0,1},{1,2},{2,3},{3,4},{4,5},{5,6},{6,7},{7,8},{8,9},{9,10},{10,1... | collective-permute-start | bytes 786440 | tf_op jit(solution)/shard_map/ppermute | solution.py:10
  41.3 10.5 %collective-permute-start.7 = (bf16[8,32,512]{2,1,0:T(8,128)(2,1)S(1)}, bf16[8,32,512]{2,1,0:T(8,128)(2,1)S(1)}, u32[]{:S(2)}, u32[]{:S(2)}) collective-permute-start(bf16[8,32,512]{2,1,0:T(8,128)(2,1)S(1)} %bitcast.59), channel_id=1, source_target_pairs={{1,0},{2,1},{3,2},{4,3},{5,4},{6,5},{7,6},{8,7},{9,8},{10,9},{11,1... | collective-permute-start | bytes 786440 | tf_op jit(solution)/shard_map/ppermute | solution.py:10
  51.9 11.8 %collective-permute-start.8 = (bf16[16,8,512]{2,1,0:T(8,128)(2,1)S(1)}, bf16[16,8,512]{2,1,0:T(8,128)(2,1)S(1)}, u32[]{:S(2)}, u32[]{:S(2)}) collective-permute-start(bf16[16,8,512]{2,1,0:T(8,128)(2,1)S(1)} %pad_maximum_fusion.3), channel_id=1, source_target_pairs={{0,32},{32,64},{64,96},{96,128},{128,160},{160,192},{192,224},{1,3... | collective-permute-start | bytes 393224 | tf_op jit(solution)/shard_map/ppermute | solution.py:10
  54.9 14.9 %collective-permute-start.10 = (bf16[16,8,512]{2,1,0:T(8,128)(2,1)S(1)}, bf16[16,8,512]{2,1,0:T(8,128)(2,1)S(1)}, u32[]{:S(2)}, u32[]{:S(2)}) collective-permute-start(bf16[16,8,512]{2,1,0:T(8,128)(2,1)S(1)} %get-tuple-element.19), channel_id=1, source_target_pairs={{0,32},{32,64},{64,96},{96,128},{128,160},{160,192},{192,224},{1,3... | collective-permute-start | bytes 393224 | tf_op jit(solution)/shard_map/ppermute | solution.py:10
  57.3 12.4 %collective-permute-start.11 = (bf16[16,8,512]{2,1,0:T(8,128)(2,1)S(1)}, bf16[16,8,512]{2,1,0:T(8,128)(2,1)S(1)}, u32[]{:S(2)}, u32[]{:S(2)}) collective-permute-start(bf16[16,8,512]{2,1,0:T(8,128)(2,1)S(1)} %get-tuple-element.20), channel_id=1, source_target_pairs={{32,0},{64,32},{96,64},{128,96},{160,128},{192,160},{224,192},{33,... | collective-permute-start | bytes 393224 | tf_op jit(solution)/shard_map/ppermute | solution.py:10
  60.8 9.0 %collective-permute-start.9 = (bf16[16,8,512]{2,1,0:T(8,128)(2,1)S(1)}, bf16[16,8,512]{2,1,0:T(8,128)(2,1)S(1)}, u32[]{:S(2)}, u32[]{:S(2)}) collective-permute-start(bf16[16,8,512]{2,1,0:T(8,128)(2,1)S(1)} %pad_maximum_fusion.4), channel_id=1, source_target_pairs={{32,0},{64,32},{96,64},{128,96},{160,128},{192,160},{224,192},{33,... | collective-permute-start | bytes 393224 | tf_op jit(solution)/shard_map/ppermute | solution.py:10
  71.2 2.2 %copy-start.2 = (bf16[4096,512]{1,0:T(8,128)(2,1)S(1)}, bf16[4096,512]{1,0:T(8,128)(2,1)}, u32[]{:S(2)}) copy-start(bf16[4096,512]{1,0:T(8,128)(2,1)} %param.5) | copy-start | bytes 12582916

commit v6 on v4

--- a/solution.py
+++ b/solution.py
@@ -62,22 +62,22 @@
 def windows(spectra, measured, h):
     rows, cols, waves = spectra.shape
     wide = 2 * h
-    down = jnp.concatenate([spectra[rows - wide :], measured[rows - h :]], axis=0)
-    up = jnp.concatenate([spectra[:wide], measured[:h]], axis=0)
-    above = send(down, "tile", 1)
-    below = send(up, "tile", -1)
-    band_s = jnp.concatenate([above[:wide], spectra, below[:wide]], axis=0)
-    band_m = jnp.concatenate([above[wide:], measured, below[wide:]], axis=0)
+    above_s = send(spectra[rows - wide :], "tile", 1)
+    below_s = send(spectra[:wide], "tile", -1)
+    above_m = send(measured[rows - h :], "tile", 1)
+    below_m = send(measured[:h], "tile", -1)
+    band_s = jnp.concatenate([above_s, spectra, below_s], axis=0)
+    band_m = jnp.concatenate([above_m, measured, below_m], axis=0)
     split = band_s.shape[0] * wide
 
-    def edge(lo, hi_s, hi_m):
+    def edge(lo_s, lo_m):
         return jnp.concatenate(
-            [band_s[:, lo : lo + wide].reshape(-1, waves), band_m[:, hi_m : hi_m + h].reshape(-1, waves)],
+            [band_s[:, lo_s : lo_s + wide].reshape(-1, waves), band_m[:, lo_m : lo_m + h].reshape(-1, waves)],
             axis=0,
         )
 
-    left = send(edge(cols - wide, None, cols - h), "wave", 1)
-    right = send(edge(0, None, 0), "wave", -1)
+    left = send(edge(cols - wide, cols - h), "wave", 1)
+    right = send(edge(0, 0), "wave", -1)
 
     def parts(piece):
         return (

time: 89.6 us -> 85.6 us (0.955)
  the two profiles are of different devices: /device:TPU:38 before, /device:TPU:228 now
where the time goes in v6:
time: 85.6 us; the launch traced here: 85.2 us
  waiting for transfers between devices  33.9 us (40%)
  starting transfers between devices  20.7 us (24%)
  matrix products  17.1 us (20%)
  local copies, waits for them, and re-layouts  9.35 us (11%)
  other arithmetic  3.77 us (4%)
    ppermute x6, waiting for transfers between devices, send(): return lax.ppermute(block, axis, pairs)  33.9 us
    ppermute x6, starting transfers between devices, send(): return lax.ppermute(block, axis, pairs)  20.7 us
    dot_general x1, matrix products, shards(): jnp.dot(coefficients.reshape(rows * cols, profiles), profile_basis, prefe...  5.84 us
    dot_general x12, matrix products, blur(): jnp.dot(mat, flat[g * win_cols:g * win_cols + span], preferred_element_ty...  4.99 us
    dot_general x1, matrix products, shards(): lax.dot_general(tau_grad, profile_basis, (((1,), (1,)), ((), ())), prefer...  4.4 us
    reshape x2, local copies, waits for them, and re-layouts, blur_mat(): strip = strip.astype(psf.dtype).reshape(cols, k * win_cols)  2.87 us
    concatenate x2, other arithmetic, edge(): jnp.concatenate([band_s[:, lo_s:lo_s + wide].reshape(-1, waves), band_m[:...  2.09 us
    unnamed x12, local copies, waits for them, and re-layouts  2.07 us
  transfers between devices with their start and end apart: 6, of which 3 were waited for; matrix products, arithmetic and copies ran while one was open for 7% of the time, Pallas kernels for 0%

profile of v6, /device:TPU:228, one launch (start us, length us, event | category | flops | bytes accessed | tf_op | source)
XLA Modules:
  0.0 85.2 jit_solution(18307875438552860008)
XLA Ops:
  0.0 5.8 %fusion.2 = bf16[512,512]{1,0:T(8,128)(2,1)S(1)} fusion(bf16[512,4096]{1,0:T(8,128)(2,1)} %bitcast.78, bf16[4096,512]{1,0:T(8,128)(2,1)} %param.5), kind=kOutput, calls=%fused_computation.11 | convolution fusion | flops 2148007936 | bytes 8912896 | tf_op jit(solution)/shard_map/dot_general | solution.py:99
  5.9 2.8 %collective-permute-start.1 = (bf16[16,32,512]{2,1,0:T(8,128)(2,1)S(1)}, bf16[16,32,512]{2,1,0:T(8,128)(2,1)S(1)}, u32[]{:S(2)}, u32[]{:S(2)}) collective-permute-start(bf16[16,32,512]{2,1,0:T(8,128)(2,1)S(1)} %bitcast.62), channel_id=1, source_target_pairs={{1,0},{2,1},{3,2},{4,3},{5,4},{6,5},{7,6},{8,7},{9,8},{10,9},{11,1... | collective-permute-start | bytes 1572872 | tf_op jit(solution)/shard_map/ppermute | solution.py:10
  8.7 1.9 %collective-permute-start = (bf16[16,32,512]{2,1,0:T(8,128)(2,1)S(1)}, bf16[16,32,512]{2,1,0:T(8,128)(2,1)S(1)}, u32[]{:S(2)}, u32[]{:S(2)}) collective-permute-start(bf16[16,32,512]{2,1,0:T(8,128)(2,1)S(1)} %bitcast.63), channel_id=1, source_target_pairs={{0,1},{1,2},{2,3},{3,4},{4,5},{5,6},{6,7},{7,8},{8,9},{9,10},{10,1... | collective-permute-start | bytes 1572872 | tf_op jit(solution)/shard_map/ppermute | solution.py:10
  10.6 5.6 %collective-permute-start.2 = (bf16[8,32,512]{2,1,0:T(8,128)(2,1)S(1)}, bf16[8,32,512]{2,1,0:T(8,128)(2,1)S(1)}, u32[]{:S(2)}, u32[]{:S(2)}) collective-permute-start(bf16[8,32,512]{2,1,0:T(8,128)(2,1)S(1)} %get-tuple-element.21), channel_id=1, source_target_pairs={{0,1},{1,2},{2,3},{3,4},{4,5},{5,6},{6,7},{7,8},{8,9},{9,10},{10,1... | collective-permute-start | bytes 786440 | tf_op jit(solution)/shard_map/ppermute | solution.py:10
  16.3 1.9 %collective-permute-start.3 = (bf16[8,32,512]{2,1,0:T(8,128)(2,1)S(1)}, bf16[8,32,512]{2,1,0:T(8,128)(2,1)S(1)}, u32[]{:S(2)}, u32[]{:S(2)}) collective-permute-start(bf16[8,32,512]{2,1,0:T(8,128)(2,1)S(1)} %get-tuple-element.22), channel_id=1, source_target_pairs={{1,0},{2,1},{3,2},{4,3},{5,4},{6,5},{7,6},{8,7},{9,8},{10,9},{11,1... | collective-permute-start | bytes 786440 | tf_op jit(solution)/shard_map/ppermute | solution.py:10
  18.2 12.0 %collective-permute-done.2 = bf16[8,32,512]{2,1,0:T(8,128)(2,1)S(1)} collective-permute-done((bf16[8,32,512]{2,1,0:T(8,128)(2,1)S(1)}, bf16[8,32,512]{2,1,0:T(8,128)(2,1)S(1)}, u32[]{:S(2)}, u32[]{:S(2)}) %collective-permute-start.2) | collective-permute-done | bytes 262176 | tf_op jit(solution)/shard_map/ppermute | solution.py:10
  30.9 1.0 %pad_maximum_fusion.3 = bf16[1024,512]{1,0:T(8,128)(2,1)} fusion(bf16[256,512]{1,0:T(8,128)(2,1)S(1)} %get-tuple-element.20, bf16[768,512]{1,0:T(8,128)(2,1)S(1)} %bitcast.61), kind=kLoop, calls=%fused_computation.25 | loop fusion | flops 2097152 | bytes 2097152 | tf_op jit(solution)/shard_map/concatenate | solution.py:74
  31.9 6.6 %collective-permute-start.5 = (bf16[1024,512]{1,0:T(8,128)(2,1)}, bf16[1024,512]{1,0:T(8,128)(2,1)S(1)}, u32[]{:S(2)}, u32[]{:S(2)}) collective-permute-start(bf16[1024,512]{1,0:T(8,128)(2,1)} %pad_maximum_fusion.3), channel_id=1, source_target_pairs={{32,0},{64,32},{96,64},{128,96},{160,128},{192,160},{224,192},{33,... | collective-permute-start | bytes 3145736 | tf_op jit(solution)/shard_map/ppermute | solution.py:10
  38.5 1.1 %pad_maximum_fusion.2 = bf16[1024,512]{1,0:T(8,128)(2,1)} fusion(bf16[256,512]{1,0:T(8,128)(2,1)S(1)} %get-tuple-element.19, bf16[768,512]{1,0:T(8,128)(2,1)S(1)} %bitcast.60), kind=kLoop, calls=%fused_computation.24 | loop fusion | flops 2097152 | bytes 2097152 | tf_op jit(solution)/shard_map/concatenate | solution.py:74
  39.5 1.9 %collective-permute-start.4 = (bf16[1024,512]{1,0:T(8,128)(2,1)}, bf16[1024,512]{1,0:T(8,128)(2,1)}, u32[]{:S(2)}, u32[]{:S(2)}) collective-permute-start(bf16[1024,512]{1,0:T(8,128)(2,1)} %pad_maximum_fusion.2), channel_id=1, source_target_pairs={{0,32},{32,64},{64,96},{96,128},{128,160},{160,192},{192,224},{1,3... | collective-permute-start | bytes 3145736 | tf_op jit(solution)/shard_map/ppermute | solution.py:10
  41.6 0.9 %fusion.4 = bf16[32,17,48]{2,1,0:T(8,128)(2,1)} fusion(bf16[17,17]{1,0:T(8,128)(2,1)S(1)} %rev.3), kind=kOutput, calls=%fused_computation.23 | convolution fusion | flops 966144 | bytes 52802 | tf_op jit(solution)/shard_map/ab,xbX->xaX/dot_general | solution.py:29
  42.5 1.7 %reshape.98 = bf16[32,816]{1,0:T(8,128)(2,1)} reshape(bf16[32,17,48]{2,1,0:T(8,128)(2,1)} %fusion.4) | data formatting | bytes 104448 | tf_op jit(solution)/shard_map/reshape | solution.py:30
  44.2 1.0 %fusion.3 = bf16[48,17,64]{2,1,0:T(8,128)(2,1)} fusion(bf16[17,17]{1,0:T(8,128)(2,1)S(1)} %copy-done.4), kind=kOutput, calls=%fused_computation.21 | convolution fusion | flops 1932288 | bytes 105026 | tf_op jit(solution)/shard_map/ab,xbX->xaX/dot_general | solution.py:29
  45.1 1.2 %reshape.99 = bf16[48,1088]{1,0:T(8,128)(2,1)S(1)} reshape(bf16[48,17,64]{2,1,0:T(8,128)(2,1)} %fusion.3) | data formatting | bytes 208896 | tf_op jit(solution)/shard_map/reshape | solution.py:30
  46.4 14.7 %collective-permute-done.5 = bf16[1024,512]{1,0:T(8,128)(2,1)S(1)} collective-permute-done((bf16[1024,512]{1,0:T(8,128)(2,1)}, bf16[1024,512]{1,0:T(8,128)(2,1)S(1)}, u32[]{:S(2)}, u32[]{:S(2)}) %collective-permute-start.5) | collective-permute-done | bytes 1048608 | tf_op jit(solution)/shard_map/ppermute | solution.py:10
  61.2 7.2 %collective-permute-done.4 = bf16[1024,512]{1,0:T(8,128)(2,1)} collective-permute-done((bf16[1024,512]{1,0:T(8,128)(2,1)}, bf16[1024,512]{1,0:T(8,128)(2,1)}, u32[]{:S(2)}, u32[]{:S(2)}) %collective-permute-start.4) | collective-permute-done | bytes 1048608 | tf_op jit(solution)/shard_map/ppermute | solution.py:10
  68.4 1.2 %slice.139 = bf16[768,512]{1,0:T(8,128)(2,1)S(1)} slice(bf16[1024,512]{1,0:T(8,128)(2,1)} %collective-permute-done.4), slice={[0:768], [0:512]} | slice | bytes 1572864 | tf_op jit(solution)/shard_map/slice | solution.py:84
  69.9 1.4 %fusion.47 = (bf16[20,64,512]{2,1,0:T(8,128)(2,1)S(1)}, bf16[20,64,512]{2,1,0:T(8,128)(2,1)S(1)}, bf16[20,64,512]{2,1,0:T(8,128)(2,1)S(1)}, bf16[20,64,512]{2,1,...) fusion(bf16[48,64,512]{2,1,0:T(8,128)(2,1)S(1)} %pad_maximum_fusion), kind=kLoop, calls=%fused_computation.74 | loop fusion | bytes 20971520 | tf_op jit(solution)/shard_map/slice | solution.py:45
  71.3 0.4 convolution_dynamic-update-slice_fusion.7
  71.8 0.5 convolution_dynamic-update-slice_fusion.6
  72.2 0.5 convolution_dynamic-update-slice_fusion.5
  72.7 0.5 convolution_dynamic-update-slice_fusion.4
  73.2 0.5 convolution_dynamic-update-slice_fusion.3
  73.6 0.4 convolution_dynamic-update-slice_fusion.2
  74.1 0.4 convolution_dynamic-update-slice_fusion.1
  74.5 0.4 convolution_dynamic-update-slice_fusion
  75.0 1.0 %slice_bitcast_fusion.1 = bf16[32,8,512]{2,1,0:T(8,128)(2,1)S(1)} fusion(bf16[1024,512]{1,0:T(8,128)(2,1)} %collective-permute-done.4), kind=kLoop, calls=%fused_computation.57 | loop fusion | bytes 524288 | tf_op jit(solution)/shard_map/reshape | solution.py:85
  76.0 1.1 %fusion = bf16[32,48,512]{2,1,0:T(8,128)(2,1)S(1)} fusion(f32[32,48,512]{2,1,0:T(8,128)S(1)} %bitcast.59, bf16[32,8,512]{2,1,0:T(8,128)(2,1)S(1)} %slice_bitcast_fusion, bf16[8,32,512]{2,1,0:T(8,128)(2,1)S(1)} %copy-done.2, bf16[16,32,512]{2,1,0:T(8,128)(2,1)S(1)} %bitcast.56, bf16[8,32,512]{2,1,0:T(8,128)(2,1)S(1)} %collective-permute-done.2, ...), kind=kLoop, calls=%fused_computation.3 | loop fusion | flops 10223616 | bytes 6292992 | tf_op jit(solution)/shard_map/jit(_where)/select_n | solution.py:110
  77.1 0.5 fusion.48
  79.0 0.3 fusion.35
  79.3 1.5 %copy-done.5 = bf16[4096,512]{1,0:T(8,128)(2,1)S(1)} copy-done((bf16[4096,512]{1,0:T(8,128)(2,1)S(1)}, bf16[4096,512]{1,0:T(8,128)(2,1)}, u32[]{:S(2)}) %copy-start.5) | copy-done | bytes 4194328
  80.8 4.4 %convolution_convert_fusion = bf16[512,4096]{1,0:T(8,128)(2,1)} fusion(bf16[4096,512]{1,0:T(8,128)(2,1)S(1)} %copy-done.5, f32[128,512]{1,0:T(8,128)S(1)} %fusion.31, f32[128,512]{1,0:T(8,128)S(1)} %fusion.33, f32[128,512]{1,0:T(8,128)S(1)} %fusion.35, f32[128,512]{1,0:T(8,128)S(1)} %fusion.37, bf16[512,512]{1,0:T(8,128)(2,1)S(1)} %fusion.2), kind=kOutput, calls=%fused_computation | convolution fusion | flops 2151415808 | bytes 9961472 | tf_op jit(solution)/shard_map/dot_general | solution.py:113
  (28 shorter events, 2.6 us)
Async XLA Ops:
  0.0 10.6 %copy-start = (bf16[512,16,32]{0,2,1:T(8,128)(2,1)S(1)}, bf16[512,16,32]{0,2,1:T(8,128)(2,1)}, u32[]{:S(2)}) copy-start(bf16[512,16,32]{0,2,1:T(8,128)(2,1)} %param.7) | copy-start | bytes 1572868
  5.9 24.4 %collective-permute-start.1 = (bf16[16,32,512]{2,1,0:T(8,128)(2,1)S(1)}, bf16[16,32,512]{2,1,0:T(8,128)(2,1)S(1)}, u32[]{:S(2)}, u32[]{:S(2)}) collective-permute-start(bf16[16,32,512]{2,1,0:T(8,128)(2,1)S(1)} %bitcast.62), channel_id=1, source_target_pairs={{1,0},{2,1},{3,2},{4,3},{5,4},{6,5},{7,6},{8,7},{9,8},{10,9},{11,1... | collective-permute-start | bytes 1572872 | tf_op jit(solution)/shard_map/ppermute | solution.py:10
  8.7 21.6 %collective-permute-start = (bf16[16,32,512]{2,1,0:T(8,128)(2,1)S(1)}, bf16[16,32,512]{2,1,0:T(8,128)(2,1)S(1)}, u32[]{:S(2)}, u32[]{:S(2)}) collective-permute-start(bf16[16,32,512]{2,1,0:T(8,128)(2,1)S(1)} %bitcast.63), channel_id=1, source_target_pairs={{0,1},{1,2},{2,3},{3,4},{4,5},{5,6},{6,7},{7,8},{8,9},{9,10},{10,1... | collective-permute-start | bytes 1572872 | tf_op jit(solution)/shard_map/ppermute | solution.py:10
  10.6 19.5 %collective-permute-start.2 = (bf16[8,32,512]{2,1,0:T(8,128)(2,1)S(1)}, bf16[8,32,512]{2,1,0:T(8,128)(2,1)S(1)}, u32[]{:S(2)}, u32[]{:S(2)}) collective-permute-start(bf16[8,32,512]{2,1,0:T(8,128)(2,1)S(1)} %get-tuple-element.21), channel_id=1, source_target_pairs={{0,1},{1,2},{2,3},{3,4},{4,5},{5,6},{6,7},{7,8},{8,9},{9,10},{10,1... | collective-permute-start | bytes 786440 | tf_op jit(solution)/shard_map/ppermute | solution.py:10
  16.3 13.9 %collective-permute-start.3 = (bf16[8,32,512]{2,1,0:T(8,128)(2,1)S(1)}, bf16[8,32,512]{2,1,0:T(8,128)(2,1)S(1)}, u32[]{:S(2)}, u32[]{:S(2)}) collective-permute-start(bf16[8,32,512]{2,1,0:T(8,128)(2,1)S(1)} %get-tuple-element.22), channel_id=1, source_target_pairs={{1,0},{2,1},{3,2},{4,3},{5,4},{6,5},{7,6},{8,7},{9,8},{10,9},{11,1... | collective-permute-start | bytes 786440 | tf_op jit(solution)/shard_map/ppermute | solution.py:10
  30.2 0.7 copy-start.1
  30.4 11.1 %copy-start.4 = (bf16[17,17]{1,0:T(8,128)(2,1)S(1)}, bf16[17,17]{1,0:T(8,128)(2,1)}, u32[]{:S(2)}) copy-start(bf16[17,17]{1,0:T(8,128)(2,1)} %param.6) | copy-start | bytes 1738
  31.9 29.2 %collective-permute-start.5 = (bf16[1024,512]{1,0:T(8,128)(2,1)}, bf16[1024,512]{1,0:T(8,128)(2,1)S(1)}, u32[]{:S(2)}, u32[]{:S(2)}) collective-permute-start(bf16[1024,512]{1,0:T(8,128)(2,1)} %pad_maximum_fusion.3), channel_id=1, source_target_pairs={{32,0},{64,32},{96,64},{128,96},{160,128},{192,160},{224,192},{33,... | collective-permute-start | bytes 3145736 | tf_op jit(solution)/shard_map/ppermute | solution.py:10
  39.5 28.9 %collective-permute-start.4 = (bf16[1024,512]{1,0:T(8,128)(2,1)}, bf16[1024,512]{1,0:T(8,128)(2,1)}, u32[]{:S(2)}, u32[]{:S(2)}) collective-permute-start(bf16[1024,512]{1,0:T(8,128)(2,1)} %pad_maximum_fusion.2), channel_id=1, source_target_pairs={{0,32},{32,64},{64,96},{96,128},{128,160},{160,192},{192,224},{1,3... | collective-permute-start | bytes 3145736 | tf_op jit(solution)/shard_map/ppermute | solution.py:10
  74.5 1.5 %copy-start.2 = (bf16[8,32,512]{2,1,0:T(8,128)(2,1)S(1)}, bf16[8,32,512]{2,1,0:T(8,128)(2,1)}, u32[]{:S(2)}) copy-start(bf16[8,32,512]{2,1,0:T(8,128)(2,1)} %copy-done.1) | copy-start | bytes 786436
  77.1 0.8 copy-start.3
  78.6 2.2 %copy-start.5 = (bf16[4096,512]{1,0:T(8,128)(2,1)S(1)}, bf16[4096,512]{1,0:T(8,128)(2,1)}, u32[]{:S(2)}) copy-start(bf16[4096,512]{1,0:T(8,128)(2,1)} %param.5) | copy-start | bytes 12582916

commit v7 on v3

--- a/solution.py
+++ b/solution.py
@@ -4,19 +4,23 @@
 from jax.sharding import PartitionSpec as P
 
 
-def send(block, axis, step):
+def send(block, axis, step, pieces=1):
     count = lax.axis_size(axis)
     pairs = [(i, i + step) for i in range(count) if 0 <= i + step < count]
-    return lax.ppermute(block, axis, pairs)
+    if pieces == 1 or block.shape[0] % pieces:
+        return lax.ppermute(block, axis, pairs)
+    size = block.shape[0] // pieces
+    parts = [lax.ppermute(block[i * size : (i + 1) * size], axis, pairs) for i in range(pieces)]
+    return jnp.concatenate(parts, axis=0)
 
 
-def window(block, h):
+def window(block, h, pieces=1):
     rows, cols = block.shape[0], block.shape[1]
-    top = send(block[rows - h :], "tile", 1)
-    bottom = send(block[:h], "tile", -1)
+    top = send(block[rows - h :], "tile", 1, pieces)
+    bottom = send(block[:h], "tile", -1, pieces)
     band = jnp.concatenate([top, block, bottom], axis=0)
-    left = send(band[:, cols - h :], "wave", 1)
-    right = send(band[:, :h], "wave", -1)
+    left = send(band[:, cols - h :], "wave", 1, pieces)
+    right = send(band[:, :h], "wave", -1, pieces)
     return jnp.concatenate([left, band, right], axis=1)
 
 
@@ -71,7 +75,7 @@
     group = 4 if rows % 4 == 0 else rows
     forward = blur_mat(point_spread, group, cols + 2 * h, h)
     adjoint = blur_mat(point_spread[::-1, ::-1], group, cols, h)
-    near = window(spectra.reshape(rows, cols, waves), 2 * h)
+    near = window(spectra.reshape(rows, cols, waves), 2 * h, 2)
     blurred = blur(near, forward, group, rows + 2 * h, cols + 2 * h, h)
     blurred = blurred.reshape(rows + 2 * h, cols + 2 * h, waves)
     residual = (blurred - measured.astype(jnp.float32)).astype(jnp.bfloat16)

time: 74.7 us -> 78.8 us (1.055)
  the two profiles are of different devices: /device:TPU:29 before, /device:TPU:30 now
where the time goes in v7:
time: 78.8 us; the launch traced here: 78.4 us
  starting transfers between devices  45.3 us (57%)
  matrix products  16.4 us (21%)
  waiting for transfers between devices  9 us (11%)
  local copies, waits for them, and re-layouts  5.76 us (7%)
  other arithmetic  1.55 us (2%)
    ppermute x8, starting transfers between devices, send(): lax.ppermute(block[i * size:(i + 1) * size], axis, pairs)  30.1 us
    ppermute x4, starting transfers between devices, send(): return lax.ppermute(block, axis, pairs)  15.2 us
    ppermute x8, waiting for transfers between devices, send(): lax.ppermute(block[i * size:(i + 1) * size], axis, pairs)  8.99 us
    dot_general x1, matrix products, shards(): jnp.dot(coefficients.reshape(rows * cols, profiles), profile_basis, prefe...  5.84 us
    dot_general x12, matrix products, blur(): jnp.dot(mat, flat[g * win_cols:g * win_cols + span], preferred_element_ty...  5.01 us
    dot_general x1, matrix products, shards(): lax.dot_general(tau_grad, profile_basis, (((1,), (1,)), ((), ())), prefer...  4.41 us
    slice x2, local copies, waits for them, and re-layouts, blur(): flat[g * win_cols:g * win_cols + span]  1.93 us
    unnamed x10, local copies, waits for them, and re-layouts  1.58 us
  transfers between devices with their start and end apart: 12, of which 3 were waited for; matrix products, arithmetic and copies ran while one was open for 10% of the time, Pallas kernels for 0%

profile of v7, /device:TPU:30, one launch (start us, length us, event | category | flops | bytes accessed | tf_op | source)
XLA Modules:
  0.0 78.4 jit_solution(7057125419805723773)
XLA Ops:
  0.0 5.8 %fusion.2 = bf16[512,512]{1,0:T(8,128)(2,1)S(1)} fusion(bf16[512,4096]{1,0:T(8,128)(2,1)} %bitcast.62, bf16[4096,512]{1,0:T(8,128)(2,1)} %param.5), kind=kOutput, calls=%fused_computation.10 | convolution fusion | flops 2148007936 | bytes 8912896 | tf_op jit(solution)/shard_map/dot_general | solution.py:71
  5.9 0.8 %fusion.49 = (bf16[256,512]{1,0:T(8,128)(2,1)}, bf16[256,512]{1,0:T(8,128)(2,1)}) fusion(bf16[512,512]{1,0:T(8,128)(2,1)S(1)} %fusion.2), kind=kLoop, calls=%fused_computation.82 | loop fusion | bytes 1048576 | tf_op jit(solution)/shard_map/slice | solution.py:13
  6.7 1.9 %collective-permute-start = (bf16[8,32,512]{2,1,0:T(8,128)(2,1)}, bf16[8,32,512]{2,1,0:T(8,128)(2,1)S(1)}, u32[]{:S(2)}, u32[]{:S(2)}) collective-permute-start(bf16[8,32,512]{2,1,0:T(8,128)(2,1)} %bitcast.5), channel_id=1, source_target_pairs={{0,1},{1,2},{2,3},{3,4},{4,5},{5,6},{6,7},{7,8},{8,9},{9,10},{10,1... | collective-permute-start | bytes 786440 | tf_op jit(solution)/shard_map/ppermute | solution.py:13
  8.6 7.9 %collective-permute-start.3 = (bf16[8,32,512]{2,1,0:T(8,128)(2,1)}, bf16[8,32,512]{2,1,0:T(8,128)(2,1)S(1)}, u32[]{:S(2)}, u32[]{:S(2)}) collective-permute-start(bf16[8,32,512]{2,1,0:T(8,128)(2,1)} %bitcast.5), channel_id=1, source_target_pairs={{1,0},{2,1},{3,2},{4,3},{5,4},{6,5},{7,6},{8,7},{9,8},{10,9},{11,1... | collective-permute-start | bytes 786440 | tf_op jit(solution)/shard_map/ppermute | solution.py:13
  16.5 1.9 %collective-permute-start.1 = (bf16[8,32,512]{2,1,0:T(8,128)(2,1)}, bf16[8,32,512]{2,1,0:T(8,128)(2,1)S(1)}, u32[]{:S(2)}, u32[]{:S(2)}) collective-permute-start(bf16[8,32,512]{2,1,0:T(8,128)(2,1)} %bitcast.6), channel_id=1, source_target_pairs={{0,1},{1,2},{2,3},{3,4},{4,5},{5,6},{6,7},{7,8},{8,9},{9,10},{10,1... | collective-permute-start | bytes 786440 | tf_op jit(solution)/shard_map/ppermute | solution.py:13
  18.4 6.7 %collective-permute-start.4 = (bf16[8,32,512]{2,1,0:T(8,128)(2,1)}, bf16[8,32,512]{2,1,0:T(8,128)(2,1)S(1)}, u32[]{:S(2)}, u32[]{:S(2)}) collective-permute-start(bf16[8,32,512]{2,1,0:T(8,128)(2,1)} %bitcast.6), channel_id=1, source_target_pairs={{1,0},{2,1},{3,2},{4,3},{5,4},{6,5},{7,6},{8,7},{9,8},{10,9},{11,1... | collective-permute-start | bytes 786440 | tf_op jit(solution)/shard_map/ppermute | solution.py:13
  25.1 1.9 %collective-permute-start.8 = (bf16[8,32,512]{2,1,0:T(8,128)(2,1)S(1)}, bf16[8,32,512]{2,1,0:T(8,128)(2,1)S(1)}, u32[]{:S(2)}, u32[]{:S(2)}) collective-permute-start(bf16[8,32,512]{2,1,0:T(8,128)(2,1)S(1)} %get-tuple-element.23), channel_id=1, source_target_pairs={{0,1},{1,2},{2,3},{3,4},{4,5},{5,6},{6,7},{7,8},{8,9},{9,10},{10,1... | collective-permute-start | bytes 786440 | tf_op jit(solution)/shard_map/ppermute | solution.py:11
  27.4 0.9 %fusion.4 = bf16[32,17,48]{2,1,0:T(8,128)(2,1)} fusion(bf16[17,17]{1,0:T(8,128)(2,1)S(1)} %rev.3), kind=kOutput, calls=%fused_computation.22 | convolution fusion | flops 966144 | bytes 52802 | tf_op jit(solution)/shard_map/ab,xbX->xaX/dot_general | solution.py:33
  28.3 6.7 %collective-permute-start.9 = (bf16[8,32,512]{2,1,0:T(8,128)(2,1)S(1)}, bf16[8,32,512]{2,1,0:T(8,128)(2,1)S(1)}, u32[]{:S(2)}, u32[]{:S(2)}) collective-permute-start(bf16[8,32,512]{2,1,0:T(8,128)(2,1)S(1)} %get-tuple-element.24), channel_id=1, source_target_pairs={{1,0},{2,1},{3,2},{4,3},{5,4},{6,5},{7,6},{8,7},{9,8},{10,9},{11,1... | collective-permute-start | bytes 786440 | tf_op jit(solution)/shard_map/ppermute | solution.py:11
  35.3 1.1 %reshape.76 = bf16[32,816]{1,0:T(8,128)(2,1)S(1)} reshape(bf16[32,17,48]{2,1,0:T(8,128)(2,1)} %fusion.4) | data formatting | bytes 104448 | tf_op jit(solution)/shard_map/reshape | solution.py:34
  36.5 2.6 %collective-permute-start.2 = (bf16[24,16,512]{2,1,0:T(8,128)(2,1)S(1)}, bf16[24,16,512]{2,1,0:T(8,128)(2,1)S(1)}, u32[]{:S(2)}, u32[]{:S(2)}) collective-permute-start(bf16[24,16,512]{2,1,0:T(8,128)(2,1)S(1)} %get-tuple-element.19), channel_id=1, source_target_pairs={{0,32},{32,64},{64,96},{96,128},{128,160},{160,192},{192,224},{1,3... | collective-permute-start | bytes 1179656 | tf_op jit(solution)/shard_map/ppermute | solution.py:13
  39.1 3.5 %collective-permute-start.5 = (bf16[24,16,512]{2,1,0:T(8,128)(2,1)S(1)}, bf16[24,16,512]{2,1,0:T(8,128)(2,1)S(1)}, u32[]{:S(2)}, u32[]{:S(2)}) collective-permute-start(bf16[24,16,512]{2,1,0:T(8,128)(2,1)S(1)} %get-tuple-element.26), channel_id=1, source_target_pairs={{0,32},{32,64},{64,96},{96,128},{128,160},{160,192},{192,224},{1,3... | collective-permute-start | bytes 1179656 | tf_op jit(solution)/shard_map/ppermute | solution.py:13
  42.6 2.4 %collective-permute-start.6 = (bf16[24,16,512]{2,1,0:T(8,128)(2,1)S(1)}, bf16[24,16,512]{2,1,0:T(8,128)(2,1)S(1)}, u32[]{:S(2)}, u32[]{:S(2)}) collective-permute-start(bf16[24,16,512]{2,1,0:T(8,128)(2,1)S(1)} %get-tuple-element.20), channel_id=1, source_target_pairs={{32,0},{64,32},{96,64},{128,96},{160,128},{192,160},{224,192},{33,... | collective-permute-start | bytes 1179656 | tf_op jit(solution)/shard_map/ppermute | solution.py:13
  45.0 3.3 %collective-permute-start.7 = (bf16[24,16,512]{2,1,0:T(8,128)(2,1)S(1)}, bf16[24,16,512]{2,1,0:T(8,128)(2,1)S(1)}, u32[]{:S(2)}, u32[]{:S(2)}) collective-permute-start(bf16[24,16,512]{2,1,0:T(8,128)(2,1)S(1)} %get-tuple-element.25), channel_id=1, source_target_pairs={{32,0},{64,32},{96,64},{128,96},{160,128},{192,160},{224,192},{33,... | collective-permute-start | bytes 1179656 | tf_op jit(solution)/shard_map/ppermute | solution.py:13
  48.3 4.7 %collective-permute-start.10 = (bf16[32,8,512]{2,1,0:T(8,128)(2,1)S(1)}, bf16[32,8,512]{2,1,0:T(8,128)(2,1)S(1)}, u32[]{:S(2)}, u32[]{:S(2)}) collective-permute-start(bf16[32,8,512]{2,1,0:T(8,128)(2,1)S(1)} %get-tuple-element.17), channel_id=1, source_target_pairs={{0,32},{32,64},{64,96},{96,128},{128,160},{160,192},{192,224},{1,3... | collective-permute-start | bytes 786440 | tf_op jit(solution)/shard_map/ppermute | solution.py:11
  53.2 1.9 %collective-permute-start.11 = (bf16[32,8,512]{2,1,0:T(8,128)(2,1)S(1)}, bf16[32,8,512]{2,1,0:T(8,128)(2,1)S(1)}, u32[]{:S(2)}, u32[]{:S(2)}) collective-permute-start(bf16[32,8,512]{2,1,0:T(8,128)(2,1)S(1)} %get-tuple-element.18), channel_id=1, source_target_pairs={{32,0},{64,32},{96,64},{128,96},{160,128},{192,160},{224,192},{33,... | collective-permute-start | bytes 786440 | tf_op jit(solution)/shard_map/ppermute | solution.py:11
  55.1 1.3 %collective-permute-done.5 = bf16[24,16,512]{2,1,0:T(8,128)(2,1)S(1)} collective-permute-done((bf16[24,16,512]{2,1,0:T(8,128)(2,1)S(1)}, bf16[24,16,512]{2,1,0:T(8,128)(2,1)S(1)}, u32[]{:S(2)}, u32[]{:S(2)}) %collective-permute-start.5) | collective-permute-done | bytes 393248 | tf_op jit(solution)/shard_map/ppermute | solution.py:13
  56.5 2.2 %collective-permute-done.6 = bf16[24,16,512]{2,1,0:T(8,128)(2,1)S(1)} collective-permute-done((bf16[24,16,512]{2,1,0:T(8,128)(2,1)S(1)}, bf16[24,16,512]{2,1,0:T(8,128)(2,1)S(1)}, u32[]{:S(2)}, u32[]{:S(2)}) %collective-permute-start.6) | collective-permute-done | bytes 393248 | tf_op jit(solution)/shard_map/ppermute | solution.py:13
  58.6 5.5 %collective-permute-done.7 = bf16[24,16,512]{2,1,0:T(8,128)(2,1)S(1)} collective-permute-done((bf16[24,16,512]{2,1,0:T(8,128)(2,1)S(1)}, bf16[24,16,512]{2,1,0:T(8,128)(2,1)S(1)}, u32[]{:S(2)}, u32[]{:S(2)}) %collective-permute-start.7) | collective-permute-done | bytes 393248 | tf_op jit(solution)/shard_map/ppermute | solution.py:13
  64.3 1.4 %fusion.46 = (bf16[20,64,512]{2,1,0:T(8,128)(2,1)S(1)}, bf16[20,64,512]{2,1,0:T(8,128)(2,1)S(1)}, bf16[20,64,512]{2,1,0:T(8,128)(2,1)S(1)}, bf16[20,64,512]{2,1,...) fusion(bf16[48,64,512]{2,1,0:T(8,128)(2,1)S(1)} %maximum_maximu, ...), kind=kLoop, calls=%fused_computation.79 | loop fusion | bytes 20971520 | tf_op jit(solution)/shard_map/slice | solution.py:49
  65.7 0.5 convolution_dynamic-update-slice_fusion.7
  66.2 0.5 convolution_dynamic-update-slice_fusion.6
  66.7 0.5 convolution_dynamic-update-slice_fusion.5
  67.1 0.5 convolution_dynamic-update-slice_fusion.4
  67.6 0.4 convolution_dynamic-update-slice_fusion.3
  68.1 0.4 convolution_dynamic-update-slice_fusion.2
  68.5 0.4 convolution_dynamic-update-slice_fusion.1
  69.0 0.4 convolution_dynamic-update-slice_fusion
  69.4 1.0 %fusion = bf16[32,48,512]{2,1,0:T(8,128)(2,1)S(1)} fusion(f32[32,48,512]{2,1,0:T(8,128)S(1)} %bitcast.49, bf16[32,8,512]{2,1,0:T(8,128)(2,1)S(1)} %collective-permute-done.11, bf16[8,32,512]{2,1,0:T(8,128)(2,1)S(1)} %collective-permute-done.9, bf16[16,32,512]{2,1,0:T(8,128)(2,1)S(1)} %bitcast.48, bf16[8,32,512]{2,1,0:T(8,128)(2,1)S(1)} %collective-permute-done.8, ...), kind=kLoop, calls=%fused_computation.3 | loop fusion | flops 10223616 | bytes 6292992 | tf_op jit(solution)/shard_map/jit(_where)/select_n | solution.py:82
  70.5 0.5 fusion.47
  72.5 1.5 %copy-done.2 = bf16[4096,512]{1,0:T(8,128)(2,1)S(1)} copy-done((bf16[4096,512]{1,0:T(8,128)(2,1)S(1)}, bf16[4096,512]{1,0:T(8,128)(2,1)}, u32[]{:S(2)}) %copy-start.2) | copy-done | bytes 4194328
  73.9 4.4 %convolution_convert_fusion = bf16[512,4096]{1,0:T(8,128)(2,1)} fusion(bf16[4096,512]{1,0:T(8,128)(2,1)S(1)} %copy-done.2, f32[128,512]{1,0:T(8,128)S(1)} %fusion.30, f32[128,512]{1,0:T(8,128)S(1)} %fusion.32, f32[128,512]{1,0:T(8,128)S(1)} %fusion.34, f32[128,512]{1,0:T(8,128)S(1)} %fusion.36, bf16[512,512]{1,0:T(8,128)(2,1)S(1)} %fusion.2), kind=kOutput, calls=%fused_computation | convolution fusion | flops 2151415808 | bytes 9961472 | tf_op jit(solution)/shard_map/dot_general | solution.py:85
  (33 shorter events, 2.6 us)
Async XLA Ops:
  0.0 25.1 %copy-start = (bf16[512,16,32]{0,2,1:T(8,128)(2,1)S(1)}, bf16[512,16,32]{0,2,1:T(8,128)(2,1)}, u32[]{:S(2)}) copy-start(bf16[512,16,32]{0,2,1:T(8,128)(2,1)} %param.7) | copy-start | bytes 1572868
  0.0 27.1 %copy-start.1 = (bf16[17,17]{1,0:T(8,128)(2,1)S(1)}, bf16[17,17]{1,0:T(8,128)(2,1)}, u32[]{:S(2)}) copy-start(bf16[17,17]{1,0:T(8,128)(2,1)} %param.6) | copy-start | bytes 1738
  6.7 21.7 %collective-permute-start = (bf16[8,32,512]{2,1,0:T(8,128)(2,1)}, bf16[8,32,512]{2,1,0:T(8,128)(2,1)S(1)}, u32[]{:S(2)}, u32[]{:S(2)}) collective-permute-start(bf16[8,32,512]{2,1,0:T(8,128)(2,1)} %bitcast.5), channel_id=1, source_target_pairs={{0,1},{1,2},{2,3},{3,4},{4,5},{5,6},{6,7},{7,8},{8,9},{9,10},{10,1... | collective-permute-start | bytes 786440 | tf_op jit(solution)/shard_map/ppermute | solution.py:13
  8.6 27.8 %collective-permute-start.3 = (bf16[8,32,512]{2,1,0:T(8,128)(2,1)}, bf16[8,32,512]{2,1,0:T(8,128)(2,1)S(1)}, u32[]{:S(2)}, u32[]{:S(2)}) collective-permute-start(bf16[8,32,512]{2,1,0:T(8,128)(2,1)} %bitcast.5), channel_id=1, source_target_pairs={{1,0},{2,1},{3,2},{4,3},{5,4},{6,5},{7,6},{8,7},{9,8},{10,9},{11,1... | collective-permute-start | bytes 786440 | tf_op jit(solution)/shard_map/ppermute | solution.py:13
  16.5 19.9 %collective-permute-start.1 = (bf16[8,32,512]{2,1,0:T(8,128)(2,1)}, bf16[8,32,512]{2,1,0:T(8,128)(2,1)S(1)}, u32[]{:S(2)}, u32[]{:S(2)}) collective-permute-start(bf16[8,32,512]{2,1,0:T(8,128)(2,1)} %bitcast.6), channel_id=1, source_target_pairs={{0,1},{1,2},{2,3},{3,4},{4,5},{5,6},{6,7},{7,8},{8,9},{9,10},{10,1... | collective-permute-start | bytes 786440 | tf_op jit(solution)/shard_map/ppermute | solution.py:13
  18.4 17.9 %collective-permute-start.4 = (bf16[8,32,512]{2,1,0:T(8,128)(2,1)}, bf16[8,32,512]{2,1,0:T(8,128)(2,1)S(1)}, u32[]{:S(2)}, u32[]{:S(2)}) collective-permute-start(bf16[8,32,512]{2,1,0:T(8,128)(2,1)} %bitcast.6), channel_id=1, source_target_pairs={{1,0},{2,1},{3,2},{4,3},{5,4},{6,5},{7,6},{8,7},{9,8},{10,9},{11,1... | collective-permute-start | bytes 786440 | tf_op jit(solution)/shard_map/ppermute | solution.py:13
  25.1 19.8 %collective-permute-start.8 = (bf16[8,32,512]{2,1,0:T(8,128)(2,1)S(1)}, bf16[8,32,512]{2,1,0:T(8,128)(2,1)S(1)}, u32[]{:S(2)}, u32[]{:S(2)}) collective-permute-start(bf16[8,32,512]{2,1,0:T(8,128)(2,1)S(1)} %get-tuple-element.23), channel_id=1, source_target_pairs={{0,1},{1,2},{2,3},{3,4},{4,5},{5,6},{6,7},{7,8},{8,9},{9,10},{10,1... | collective-permute-start | bytes 786440 | tf_op jit(solution)/shard_map/ppermute | solution.py:11
  28.3 19.9 %collective-permute-start.9 = (bf16[8,32,512]{2,1,0:T(8,128)(2,1)S(1)}, bf16[8,32,512]{2,1,0:T(8,128)(2,1)S(1)}, u32[]{:S(2)}, u32[]{:S(2)}) collective-permute-start(bf16[8,32,512]{2,1,0:T(8,128)(2,1)S(1)} %get-tuple-element.24), channel_id=1, source_target_pairs={{1,0},{2,1},{3,2},{4,3},{5,4},{6,5},{7,6},{8,7},{9,8},{10,9},{11,1... | collective-permute-start | bytes 786440 | tf_op jit(solution)/shard_map/ppermute | solution.py:11
  36.5 16.6 %collective-permute-start.2 = (bf16[24,16,512]{2,1,0:T(8,128)(2,1)S(1)}, bf16[24,16,512]{2,1,0:T(8,128)(2,1)S(1)}, u32[]{:S(2)}, u32[]{:S(2)}) collective-permute-start(bf16[24,16,512]{2,1,0:T(8,128)(2,1)S(1)} %get-tuple-element.19), channel_id=1, source_target_pairs={{0,32},{32,64},{64,96},{96,128},{128,160},{160,192},{192,224},{1,3... | collective-permute-start | bytes 1179656 | tf_op jit(solution)/shard_map/ppermute | solution.py:13
  39.1 17.3 %collective-permute-start.5 = (bf16[24,16,512]{2,1,0:T(8,128)(2,1)S(1)}, bf16[24,16,512]{2,1,0:T(8,128)(2,1)S(1)}, u32[]{:S(2)}, u32[]{:S(2)}) collective-permute-start(bf16[24,16,512]{2,1,0:T(8,128)(2,1)S(1)} %get-tuple-element.26), channel_id=1, source_target_pairs={{0,32},{32,64},{64,96},{96,128},{128,160},{160,192},{192,224},{1,3... | collective-permute-start | bytes 1179656 | tf_op jit(solution)/shard_map/ppermute | solution.py:13
  42.6 16.0 %collective-permute-start.6 = (bf16[24,16,512]{2,1,0:T(8,128)(2,1)S(1)}, bf16[24,16,512]{2,1,0:T(8,128)(2,1)S(1)}, u32[]{:S(2)}, u32[]{:S(2)}) collective-permute-start(bf16[24,16,512]{2,1,0:T(8,128)(2,1)S(1)} %get-tuple-element.20), channel_id=1, source_target_pairs={{32,0},{64,32},{96,64},{128,96},{160,128},{192,160},{224,192},{33,... | collective-permute-start | bytes 1179656 | tf_op jit(solution)/shard_map/ppermute | solution.py:13
  45.0 19.1 %collective-permute-start.7 = (bf16[24,16,512]{2,1,0:T(8,128)(2,1)S(1)}, bf16[24,16,512]{2,1,0:T(8,128)(2,1)S(1)}, u32[]{:S(2)}, u32[]{:S(2)}) collective-permute-start(bf16[24,16,512]{2,1,0:T(8,128)(2,1)S(1)} %get-tuple-element.25), channel_id=1, source_target_pairs={{32,0},{64,32},{96,64},{128,96},{160,128},{192,160},{224,192},{33,... | collective-permute-start | bytes 1179656 | tf_op jit(solution)/shard_map/ppermute | solution.py:13
  48.3 21.1 %collective-permute-start.10 = (bf16[32,8,512]{2,1,0:T(8,128)(2,1)S(1)}, bf16[32,8,512]{2,1,0:T(8,128)(2,1)S(1)}, u32[]{:S(2)}, u32[]{:S(2)}) collective-permute-start(bf16[32,8,512]{2,1,0:T(8,128)(2,1)S(1)} %get-tuple-element.17), channel_id=1, source_target_pairs={{0,32},{32,64},{64,96},{96,128},{128,160},{160,192},{192,224},{1,3... | collective-permute-start | bytes 786440 | tf_op jit(solution)/shard_map/ppermute | solution.py:11
  53.2 16.2 %collective-permute-start.11 = (bf16[32,8,512]{2,1,0:T(8,128)(2,1)S(1)}, bf16[32,8,512]{2,1,0:T(8,128)(2,1)S(1)}, u32[]{:S(2)}, u32[]{:S(2)}) collective-permute-start(bf16[32,8,512]{2,1,0:T(8,128)(2,1)S(1)} %get-tuple-element.18), channel_id=1, source_target_pairs={{32,0},{64,32},{96,64},{128,96},{160,128},{192,160},{224,192},{33,... | collective-permute-start | bytes 786440 | tf_op jit(solution)/shard_map/ppermute | solution.py:11
  71.8 2.2 %copy-start.2 = (bf16[4096,512]{1,0:T(8,128)(2,1)S(1)}, bf16[4096,512]{1,0:T(8,128)(2,1)}, u32[]{:S(2)}) copy-start(bf16[4096,512]{1,0:T(8,128)(2,1)} %param.5) | copy-start | bytes 12582916

commit v8 on v3

--- a/solution.py
+++ b/solution.py
@@ -1,4 +1,5 @@
 import jax
+import numpy as np
 import jax.numpy as jnp
 from jax import lax
 from jax.sharding import PartitionSpec as P
@@ -10,39 +11,47 @@
     return lax.ppermute(block, axis, pairs)
 
 
-def window(block, h):
+def pieces(block, h):
     rows, cols = block.shape[0], block.shape[1]
     top = send(block[rows - h :], "tile", 1)
     bottom = send(block[:h], "tile", -1)
     band = jnp.concatenate([top, block, bottom], axis=0)
     left = send(band[:, cols - h :], "wave", 1)
     right = send(band[:, :h], "wave", -1)
+    return band, left, right
+
+
+def window(block, h):
+    band, left, right = pieces(block, h)
     return jnp.concatenate([left, band, right], axis=1)
 
 
-def blur_mat(psf, group, cols, h):
+def blur_mat(psf, group, out_cols, h, columns=None):
     k = psf.shape[0]
-    win_cols = cols + 2 * h
-    shape_c = (cols, k, win_cols)
-    col_gap = lax.broadcasted_iota(jnp.int32, shape_c, 2) - lax.broadcasted_iota(jnp.int32, shape_c, 0)
+    if columns is None:
+        columns = np.arange(out_cols + 2 * h)
+    width = len(columns)
+    shape_c = (out_cols, k, width)
+    spots = jnp.asarray(np.asarray(columns, np.int32))[None, None, :]
+    col_gap = spots - lax.broadcasted_iota(jnp.int32, shape_c, 0)
     hot = (col_gap == lax.broadcasted_iota(jnp.int32, shape_c, 1)).astype(psf.dtype)
     strip = jnp.einsum("ab,xbX->xaX", psf, hot, preferred_element_type=jnp.float32)
-    strip = strip.astype(psf.dtype).reshape(cols, k * win_cols)
-    total = (group + 2 * h) * win_cols
+    strip = strip.astype(psf.dtype).reshape(out_cols, k * width)
+    total = (group + 2 * h) * width
     blocks = [
-        jnp.pad(strip, ((0, 0), (y * win_cols, total - y * win_cols - k * win_cols)))
+        jnp.pad(strip, ((0, 0), (y * width, total - y * width - k * width)))
         for y in range(group)
     ]
     return jnp.concatenate(blocks, axis=0)
 
 
-def blur(near, mat, group, out_rows, out_cols, h):
+def blur(near, mat, group, out_rows, h):
     waves = near.shape[-1]
-    win_cols = out_cols + 2 * h
+    width = near.shape[1]
     flat = near.reshape(-1, waves)
-    span = (group + 2 * h) * win_cols
+    span = (group + 2 * h) * width
     outs = [
-        jnp.dot(mat, flat[g * win_cols : g * win_cols + span], preferred_element_type=jnp.float32)
+        jnp.dot(mat, flat[g * width : g * width + span], preferred_element_type=jnp.float32)
         for g in range(0, out_rows, group)
     ]
     return jnp.concatenate(outs, axis=0)
@@ -69,14 +78,19 @@
     )
     spectra = jnp.exp(-opacity).astype(jnp.bfloat16)
     group = 4 if rows % 4 == 0 else rows
-    forward = blur_mat(point_spread, group, cols + 2 * h, h)
+    wide = 2 * h
+    mid = np.arange(wide, wide + cols)
+    side = np.concatenate([np.arange(wide), np.arange(wide + cols, 2 * wide + cols)])
+    forward_mid = blur_mat(point_spread, group, cols + 2 * h, h, mid)
+    forward_side = blur_mat(point_spread, group, cols + 2 * h, h, side)
     adjoint = blur_mat(point_spread[::-1, ::-1], group, cols, h)
-    near = window(spectra.reshape(rows, cols, waves), 2 * h)
-    blurred = blur(near, forward, group, rows + 2 * h, cols + 2 * h, h)
+    band, left, right = pieces(spectra.reshape(rows, cols, waves), wide)
+    blurred = blur(band, forward_mid, group, rows + 2 * h, h)
+    blurred = blurred + blur(jnp.concatenate([left, right], axis=1), forward_side, group, rows + 2 * h, h)
     blurred = blurred.reshape(rows + 2 * h, cols + 2 * h, waves)
     residual = (blurred - measured.astype(jnp.float32)).astype(jnp.bfloat16)
     residual = jnp.where(inside(rows, cols, h), residual, jnp.zeros_like(residual))
-    adjoint_field = blur(residual, adjoint, group, rows, cols, h)
+    adjoint_field = blur(residual, adjoint, group, rows, h)
     tau_grad = (-spectra.astype(jnp.float32) * adjoint_field).astype(jnp.bfloat16)
     coef_grad = lax.dot_general(
         tau_grad, profile_basis, (((1,), (1,)), ((), ())), preferred_element_type=jnp.float32

time: 74.7 us -> 83.5 us (1.12)
  the two profiles are of different devices: /device:TPU:29 before, /device:TPU:30 now
where the time goes in v8:
time: 83.5 us; the launch traced here: 83.1 us
  starting transfers between devices  32.3 us (39%)
  matrix products  24.5 us (29%)
  waiting for transfers between devices  18.3 us (22%)
  local copies, waits for them, and re-layouts  5.01 us (6%)
  other arithmetic  2.62 us (3%)
    ppermute x8, starting transfers between devices, send(): return lax.ppermute(block, axis, pairs)  32.3 us
    ppermute x8, waiting for transfers between devices, send(): return lax.ppermute(block, axis, pairs)  18.3 us
    dot_general x20, matrix products, blur(): jnp.dot(mat, flat[g * width:g * width + span], preferred_element_type=jnp...  12.2 us
    dot_general x1, matrix products, shards(): jnp.dot(coefficients.reshape(rows * cols, profiles), profile_basis, prefe...  5.84 us
    dot_general x1, matrix products, shards(): lax.dot_general(tau_grad, profile_basis, (((1,), (1,)), ((), ())), prefer...  4.41 us
    dot_general x3, matrix products, blur_mat(): jnp.einsum('ab,xbX->xaX', psf, hot, preferred_element_type=jnp.float32)  2.08 us
    unnamed x11, local copies, waits for them, and re-layouts  1.77 us
  transfers between devices with their start and end apart: 8, of which 4 were waited for; matrix products, arithmetic and copies ran while one was open for 21% of the time, Pallas kernels for 0%

profile of v8, /device:TPU:30, one launch (start us, length us, event | category | flops | bytes accessed | tf_op | source)
XLA Modules:
  0.0 83.1 jit_solution(706012221107080515)
XLA Ops:
  0.0 5.8 %fusion.2 = bf16[512,512]{1,0:T(8,128)(2,1)S(1)} fusion(bf16[512,4096]{1,0:T(8,128)(2,1)} %bitcast.108, bf16[4096,512]{1,0:T(8,128)(2,1)} %param.8), kind=kOutput, calls=%fused_computation.18 | convolution fusion | flops 2148007936 | bytes 8912896 | tf_op jit(solution)/shard_map/dot_general | solution.py:76
  5.9 1.9 %collective-permute-start = (bf16[16,32,512]{2,1,0:T(8,128)(2,1)S(1)}, bf16[16,32,512]{2,1,0:T(8,128)(2,1)S(1)}, u32[]{:S(2)}, u32[]{:S(2)}) collective-permute-start(bf16[16,32,512]{2,1,0:T(8,128)(2,1)S(1)} %bitcast.68), channel_id=1, source_target_pairs={{0,1},{1,2},{2,3},{3,4},{4,5},{5,6},{6,7},{7,8},{8,9},{9,10},{10,1... | collective-permute-start | bytes 1572872 | tf_op jit(solution)/shard_map/ppermute | solution.py:11
  7.8 7.9 %collective-permute-start.1 = (bf16[16,32,512]{2,1,0:T(8,128)(2,1)S(1)}, bf16[16,32,512]{2,1,0:T(8,128)(2,1)S(1)}, u32[]{:S(2)}, u32[]{:S(2)}) collective-permute-start(bf16[16,32,512]{2,1,0:T(8,128)(2,1)S(1)} %bitcast.69), channel_id=1, source_target_pairs={{1,0},{2,1},{3,2},{4,3},{5,4},{6,5},{7,6},{8,7},{9,8},{10,9},{11,1... | collective-permute-start | bytes 1572872 | tf_op jit(solution)/shard_map/ppermute | solution.py:11
  15.8 1.9 %collective-permute-start.4 = (bf16[8,32,512]{2,1,0:T(8,128)(2,1)S(1)}, bf16[8,32,512]{2,1,0:T(8,128)(2,1)S(1)}, u32[]{:S(2)}, u32[]{:S(2)}) collective-permute-start(bf16[8,32,512]{2,1,0:T(8,128)(2,1)S(1)} %get-tuple-element.29), channel_id=1, source_target_pairs={{0,1},{1,2},{2,3},{3,4},{4,5},{5,6},{6,7},{7,8},{8,9},{9,10},{10,1... | collective-permute-start | bytes 786440 | tf_op jit(solution)/shard_map/ppermute | solution.py:11
  17.7 6.7 %collective-permute-start.5 = (bf16[8,32,512]{2,1,0:T(8,128)(2,1)S(1)}, bf16[8,32,512]{2,1,0:T(8,128)(2,1)S(1)}, u32[]{:S(2)}, u32[]{:S(2)}) collective-permute-start(bf16[8,32,512]{2,1,0:T(8,128)(2,1)S(1)} %get-tuple-element.30), channel_id=1, source_target_pairs={{1,0},{2,1},{3,2},{4,3},{5,4},{6,5},{7,6},{8,7},{9,8},{10,9},{11,1... | collective-permute-start | bytes 786440 | tf_op jit(solution)/shard_map/ppermute | solution.py:11
  24.7 0.9 %fusion.4 = bf16[48,17,32]{0,1,2:T(8,128)(2,1)S(1)} fusion(s32[32]{0:T(128)} %constant.33.clone, bf16[17,17]{1,0:T(8,128)(2,1)S(1)} %copy-done.2), kind=kOutput, calls=%fused_computation.39 | convolution fusion | flops 966144 | bytes 52930 | tf_op jit(solution)/shard_map/ab,xbX->xaX/dot_general | solution.py:38
  25.7 0.9 %fusion.3 = bf16[32,17,48]{2,1,0:T(8,128)(2,1)} fusion(bf16[17,17]{1,0:T(8,128)(2,1)S(1)} %rev.3), kind=kOutput, calls=%fused_computation.38 | convolution fusion | flops 966144 | bytes 52802 | tf_op jit(solution)/shard_map/ab,xbX->xaX/dot_general | solution.py:38
  26.6 0.7 copy.9
  27.3 1.1 %reshape.90 = bf16[32,816]{1,0:T(8,128)(2,1)S(1)} reshape(bf16[32,17,48]{2,1,0:T(8,128)(2,1)} %fusion.3) | data formatting | bytes 104448 | tf_op jit(solution)/shard_map/reshape | solution.py:39
  28.5 0.7 collective-permute-done.4
  29.2 3.3 %collective-permute-done.5 = bf16[8,32,512]{2,1,0:T(8,128)(2,1)S(1)} collective-permute-done((bf16[8,32,512]{2,1,0:T(8,128)(2,1)S(1)}, bf16[8,32,512]{2,1,0:T(8,128)(2,1)S(1)}, u32[]{:S(2)}, u32[]{:S(2)}) %collective-permute-start.5) | collective-permute-done | bytes 262176 | tf_op jit(solution)/shard_map/ppermute | solution.py:11
  32.5 3.9 %collective-permute-start.6 = (bf16[32,8,512]{2,1,0:T(8,128)(2,1)S(1)}, bf16[32,8,512]{2,1,0:T(8,128)(2,1)S(1)}, u32[]{:S(2)}, u32[]{:S(2)}) collective-permute-start(bf16[32,8,512]{2,1,0:T(8,128)(2,1)S(1)} %get-tuple-element.19), channel_id=1, source_target_pairs={{0,32},{32,64},{64,96},{96,128},{128,160},{160,192},{192,224},{1,3... | collective-permute-start | bytes 786440 | tf_op jit(solution)/shard_map/ppermute | solution.py:11
  36.4 2.0 %collective-permute-start.7 = (bf16[32,8,512]{2,1,0:T(8,128)(2,1)S(1)}, bf16[32,8,512]{2,1,0:T(8,128)(2,1)S(1)}, u32[]{:S(2)}, u32[]{:S(2)}) collective-permute-start(bf16[32,8,512]{2,1,0:T(8,128)(2,1)S(1)} %get-tuple-element.20), channel_id=1, source_target_pairs={{32,0},{64,32},{96,64},{128,96},{160,128},{192,160},{224,192},{33,... | collective-permute-start | bytes 786440 | tf_op jit(solution)/shard_map/ppermute | solution.py:11
  38.7 6.0 %collective-permute-start.2 = (bf16[48,16,512]{2,1,0:T(8,128)(2,1)S(1)}, bf16[48,16,512]{2,1,0:T(8,128)(2,1)S(1)}, u32[]{:S(2)}, u32[]{:S(2)}) collective-permute-start(bf16[48,16,512]{2,1,0:T(8,128)(2,1)S(1)} %get-tuple-element.18), channel_id=1, source_target_pairs={{0,32},{32,64},{64,96},{96,128},{128,160},{160,192},{192,224},{1,3... | collective-permute-start | bytes 2359304 | tf_op jit(solution)/shard_map/ppermute | solution.py:11
  44.7 2.1 %collective-permute-start.3 = (bf16[48,16,512]{2,1,0:T(8,128)(2,1)S(1)}, bf16[48,16,512]{2,1,0:T(8,128)(2,1)S(1)}, u32[]{:S(2)}, u32[]{:S(2)}) collective-permute-start(bf16[48,16,512]{2,1,0:T(8,128)(2,1)S(1)} %get-tuple-element.17), channel_id=1, source_target_pairs={{32,0},{64,32},{96,64},{128,96},{160,128},{192,160},{224,192},{33,... | collective-permute-start | bytes 2359304 | tf_op jit(solution)/shard_map/ppermute | solution.py:11
  48.1 0.7 convolution_dynamic-update-slice_fusion.14
  48.7 0.7 convolution_dynamic-update-slice_fusion.13
  49.4 0.7 convolution_dynamic-update-slice_fusion.12
  52.1 0.7 convolution_dynamic-update-slice_fusion.8
  52.8 8.2 %collective-permute-done.2 = bf16[48,16,512]{2,1,0:T(8,128)(2,1)S(1)} collective-permute-done((bf16[48,16,512]{2,1,0:T(8,128)(2,1)S(1)}, bf16[48,16,512]{2,1,0:T(8,128)(2,1)S(1)}, u32[]{:S(2)}, u32[]{:S(2)}) %collective-permute-start.2) | collective-permute-done | bytes 786464 | tf_op jit(solution)/shard_map/ppermute | solution.py:11
  61.0 6.1 %collective-permute-done.3 = bf16[48,16,512]{2,1,0:T(8,128)(2,1)S(1)} collective-permute-done((bf16[48,16,512]{2,1,0:T(8,128)(2,1)S(1)}, bf16[48,16,512]{2,1,0:T(8,128)(2,1)S(1)}, u32[]{:S(2)}, u32[]{:S(2)}) %collective-permute-start.3) | collective-permute-done | bytes 786464 | tf_op jit(solution)/shard_map/ppermute | solution.py:11
  68.7 0.7 convolution_dynamic-update-slice_fusion.6
  69.4 0.7 convolution_dynamic-update-slice_fusion.5
  70.1 0.7 convolution_dynamic-update-slice_fusion.4
  70.8 0.7 convolution_dynamic-update-slice_fusion.3
  71.5 0.7 convolution_dynamic-update-slice_fusion.2
  72.1 0.7 convolution_dynamic-update-slice_fusion.1
  72.8 0.7 convolution_dynamic-update-slice_fusion
  73.5 0.8 add.51
  74.3 1.0 %fusion = bf16[32,48,512]{2,1,0:T(8,128)(2,1)S(1)} fusion(f32[32,48,512]{2,1,0:T(8,128)S(1)} %bitcast.64, bf16[32,8,512]{2,1,0:T(8,128)(2,1)S(1)} %collective-permute-done.7, bf16[8,32,512]{2,1,0:T(8,128)(2,1)S(1)} %collective-permute-done.5, bf16[16,32,512]{2,1,0:T(8,128)(2,1)S(1)} %bitcast.67, bf16[8,32,512]{2,1,0:T(8,128)(2,1)S(1)} %collective-permute-done.4, ...), kind=kLoop, calls=%fused_computation.2 | loop fusion | flops 10223616 | bytes 6292992 | tf_op jit(solution)/shard_map/jit(_where)/select_n | solution.py:92
  77.3 1.5 %copy-done.3 = bf16[4096,512]{1,0:T(8,128)(2,1)S(1)} copy-done((bf16[4096,512]{1,0:T(8,128)(2,1)S(1)}, bf16[4096,512]{1,0:T(8,128)(2,1)}, u32[]{:S(2)}) %copy-start.3) | copy-done | bytes 4194328
  78.7 4.4 %convolution_convert_fusion = bf16[512,4096]{1,0:T(8,128)(2,1)} fusion(bf16[4096,512]{1,0:T(8,128)(2,1)S(1)} %copy-done.3, f32[128,512]{1,0:T(8,128)S(1)} %fusion.49, f32[128,512]{1,0:T(8,128)S(1)} %fusion.51, f32[128,512]{1,0:T(8,128)S(1)} %fusion.53, f32[128,512]{1,0:T(8,128)S(1)} %fusion.55, bf16[512,512]{1,0:T(8,128)(2,1)S(1)} %fusion.2), kind=kOutput, calls=%fused_computation | convolution fusion | flops 2151415808 | bytes 9961472 | tf_op jit(solution)/shard_map/dot_general | solution.py:95
  (37 shorter events, 7.6 us)
Async XLA Ops:
  0.0 15.7 %copy-start = (bf16[512,16,32]{0,2,1:T(8,128)(2,1)S(1)}, bf16[512,16,32]{0,2,1:T(8,128)(2,1)}, u32[]{:S(2)}) copy-start(bf16[512,16,32]{0,2,1:T(8,128)(2,1)} %param.10) | copy-start | bytes 1572868
  0.0 24.4 %copy-start.2 = (bf16[17,17]{1,0:T(8,128)(2,1)S(1)}, bf16[17,17]{1,0:T(8,128)(2,1)}, u32[]{:S(2)}) copy-start(bf16[17,17]{1,0:T(8,128)(2,1)} %param.9) | copy-start | bytes 1738
  0.0 24.5 %copy-start.4 = (s32[32]{0:T(128)S(1)}, s32[32]{0:T(128)}, u32[]{:S(2)}) copy-start(s32[32]{0:T(128)} %constant.34.clone) | copy-start | bytes 388
  5.9 32.5 %collective-permute-start = (bf16[16,32,512]{2,1,0:T(8,128)(2,1)S(1)}, bf16[16,32,512]{2,1,0:T(8,128)(2,1)S(1)}, u32[]{:S(2)}, u32[]{:S(2)}) collective-permute-start(bf16[16,32,512]{2,1,0:T(8,128)(2,1)S(1)} %bitcast.68), channel_id=1, source_target_pairs={{0,1},{1,2},{2,3},{3,4},{4,5},{5,6},{6,7},{7,8},{8,9},{9,10},{10,1... | collective-permute-start | bytes 1572872 | tf_op jit(solution)/shard_map/ppermute | solution.py:11
  7.8 30.6 %collective-permute-start.1 = (bf16[16,32,512]{2,1,0:T(8,128)(2,1)S(1)}, bf16[16,32,512]{2,1,0:T(8,128)(2,1)S(1)}, u32[]{:S(2)}, u32[]{:S(2)}) collective-permute-start(bf16[16,32,512]{2,1,0:T(8,128)(2,1)S(1)} %bitcast.69), channel_id=1, source_target_pairs={{1,0},{2,1},{3,2},{4,3},{5,4},{6,5},{7,6},{8,7},{9,8},{10,9},{11,1... | collective-permute-start | bytes 1572872 | tf_op jit(solution)/shard_map/ppermute | solution.py:11
  15.8 13.4 %collective-permute-start.4 = (bf16[8,32,512]{2,1,0:T(8,128)(2,1)S(1)}, bf16[8,32,512]{2,1,0:T(8,128)(2,1)S(1)}, u32[]{:S(2)}, u32[]{:S(2)}) collective-permute-start(bf16[8,32,512]{2,1,0:T(8,128)(2,1)S(1)} %get-tuple-element.29), channel_id=1, source_target_pairs={{0,1},{1,2},{2,3},{3,4},{4,5},{5,6},{6,7},{7,8},{8,9},{9,10},{10,1... | collective-permute-start | bytes 786440 | tf_op jit(solution)/shard_map/ppermute | solution.py:11
  17.7 14.8 %collective-permute-start.5 = (bf16[8,32,512]{2,1,0:T(8,128)(2,1)S(1)}, bf16[8,32,512]{2,1,0:T(8,128)(2,1)S(1)}, u32[]{:S(2)}, u32[]{:S(2)}) collective-permute-start(bf16[8,32,512]{2,1,0:T(8,128)(2,1)S(1)} %get-tuple-element.30), channel_id=1, source_target_pairs={{1,0},{2,1},{3,2},{4,3},{5,4},{6,5},{7,6},{8,7},{9,8},{10,9},{11,1... | collective-permute-start | bytes 786440 | tf_op jit(solution)/shard_map/ppermute | solution.py:11
  32.5 41.7 %collective-permute-start.6 = (bf16[32,8,512]{2,1,0:T(8,128)(2,1)S(1)}, bf16[32,8,512]{2,1,0:T(8,128)(2,1)S(1)}, u32[]{:S(2)}, u32[]{:S(2)}) collective-permute-start(bf16[32,8,512]{2,1,0:T(8,128)(2,1)S(1)} %get-tuple-element.19), channel_id=1, source_target_pairs={{0,32},{32,64},{64,96},{96,128},{128,160},{160,192},{192,224},{1,3... | collective-permute-start | bytes 786440 | tf_op jit(solution)/shard_map/ppermute | solution.py:11
  36.4 37.8 %collective-permute-start.7 = (bf16[32,8,512]{2,1,0:T(8,128)(2,1)S(1)}, bf16[32,8,512]{2,1,0:T(8,128)(2,1)S(1)}, u32[]{:S(2)}, u32[]{:S(2)}) collective-permute-start(bf16[32,8,512]{2,1,0:T(8,128)(2,1)S(1)} %get-tuple-element.20), channel_id=1, source_target_pairs={{32,0},{64,32},{96,64},{128,96},{160,128},{192,160},{224,192},{33,... | collective-permute-start | bytes 786440 | tf_op jit(solution)/shard_map/ppermute | solution.py:11
  38.7 22.2 %collective-permute-start.2 = (bf16[48,16,512]{2,1,0:T(8,128)(2,1)S(1)}, bf16[48,16,512]{2,1,0:T(8,128)(2,1)S(1)}, u32[]{:S(2)}, u32[]{:S(2)}) collective-permute-start(bf16[48,16,512]{2,1,0:T(8,128)(2,1)S(1)} %get-tuple-element.18), channel_id=1, source_target_pairs={{0,32},{32,64},{64,96},{96,128},{128,160},{160,192},{192,224},{1,3... | collective-permute-start | bytes 2359304 | tf_op jit(solution)/shard_map/ppermute | solution.py:11
  44.7 22.4 %collective-permute-start.3 = (bf16[48,16,512]{2,1,0:T(8,128)(2,1)S(1)}, bf16[48,16,512]{2,1,0:T(8,128)(2,1)S(1)}, u32[]{:S(2)}, u32[]{:S(2)}) collective-permute-start(bf16[48,16,512]{2,1,0:T(8,128)(2,1)S(1)} %get-tuple-element.17), channel_id=1, source_target_pairs={{32,0},{64,32},{96,64},{128,96},{160,128},{192,160},{224,192},{33,... | collective-permute-start | bytes 2359304 | tf_op jit(solution)/shard_map/ppermute | solution.py:11
  67.2 0.9 %copy-start.1 = (bf16[48,17,32]{0,2,1:T(8,128)(2,1)S(1)}, bf16[48,17,32]{0,2,1:T(8,128)(2,1)}, u32[]{:S(2)}) copy-start(bf16[48,17,32]{0,2,1:T(8,128)(2,1)} %copy.9) | copy-start | bytes 156676
  76.5 2.2 %copy-start.3 = (bf16[4096,512]{1,0:T(8,128)(2,1)S(1)}, bf16[4096,512]{1,0:T(8,128)(2,1)}, u32[]{:S(2)}) copy-start(bf16[4096,512]{1,0:T(8,128)(2,1)} %param.8) | copy-start | bytes 12582916

commit v9 on v3

--- a/solution.py
+++ b/solution.py
@@ -68,7 +68,7 @@
         coefficients.reshape(rows * cols, profiles), profile_basis, preferred_element_type=jnp.float32
     )
     spectra = jnp.exp(-opacity).astype(jnp.bfloat16)
-    group = 4 if rows % 4 == 0 else rows
+    group = 8 if rows % 8 == 0 else rows
     forward = blur_mat(point_spread, group, cols + 2 * h, h)
     adjoint = blur_mat(point_spread[::-1, ::-1], group, cols, h)
     near = window(spectra.reshape(rows, cols, waves), 2 * h)

time: 74.7 us -> 76.9 us (1.029)
  the two profiles are of different devices: /device:TPU:29 before, /device:TPU:30 now
where the time goes in v9:
time: 76.9 us; the launch traced here: 76.5 us
  starting transfers between devices  30.9 us (40%)
  matrix products  19.9 us (26%)
  waiting for transfers between devices  13.5 us (18%)
  local copies, waits for them, and re-layouts  9.96 us (13%)
  other arithmetic  1.96 us (3%)
    ppermute x8, starting transfers between devices, send(): return lax.ppermute(block, axis, pairs)  30.9 us
    ppermute x8, waiting for transfers between devices, send(): return lax.ppermute(block, axis, pairs)  13.5 us
    dot_general x6, matrix products, blur(): jnp.dot(mat, flat[g * win_cols:g * win_cols + span], preferred_element_ty...  9.18 us
    unnamed x20, local copies, waits for them, and re-layouts  6.71 us
    dot_general x1, matrix products, shards(): jnp.dot(coefficients.reshape(rows * cols, profiles), profile_basis, prefe...  5.84 us
    dot_general x1, matrix products, shards(): lax.dot_general(tau_grad, profile_basis, (((1,), (1,)), ((), ())), prefer...  4.4 us
  transfers between devices with their start and end apart: 8, of which 2 were waited for; matrix products, arithmetic and copies ran while one was open for 24% of the time, Pallas kernels for 0%

profile of v9, /device:TPU:30, one launch (start us, length us, event | category | flops | bytes accessed | tf_op | source)
XLA Modules:
  0.0 76.5 jit_solution(5908719990681501522)
XLA Ops:
  0.0 5.8 %fusion.2 = bf16[512,512]{1,0:T(8,128)(2,1)S(1)} fusion(bf16[512,4096]{1,0:T(8,128)(2,1)} %bitcast.50, bf16[4096,512]{1,0:T(8,128)(2,1)} %param.5), kind=kOutput, calls=%fused_computation.8 | convolution fusion | flops 2148007936 | bytes 8912896 | tf_op jit(solution)/shard_map/dot_general | solution.py:67
  5.9 1.9 %collective-permute-start = (bf16[16,32,512]{2,1,0:T(8,128)(2,1)S(1)}, bf16[16,32,512]{2,1,0:T(8,128)(2,1)S(1)}, u32[]{:S(2)}, u32[]{:S(2)}) collective-permute-start(bf16[16,32,512]{2,1,0:T(8,128)(2,1)S(1)} %bitcast.42), channel_id=1, source_target_pairs={{0,1},{1,2},{2,3},{3,4},{4,5},{5,6},{6,7},{7,8},{8,9},{9,10},{10,1... | collective-permute-start | bytes 1572872 | tf_op jit(solution)/shard_map/ppermute | solution.py:10
  7.8 7.9 %collective-permute-start.1 = (bf16[16,32,512]{2,1,0:T(8,128)(2,1)S(1)}, bf16[16,32,512]{2,1,0:T(8,128)(2,1)S(1)}, u32[]{:S(2)}, u32[]{:S(2)}) collective-permute-start(bf16[16,32,512]{2,1,0:T(8,128)(2,1)S(1)} %bitcast.43), channel_id=1, source_target_pairs={{1,0},{2,1},{3,2},{4,3},{5,4},{6,5},{7,6},{8,7},{9,8},{10,9},{11,1... | collective-permute-start | bytes 1572872 | tf_op jit(solution)/shard_map/ppermute | solution.py:10
  15.7 0.7 fusion.15
  16.4 1.9 %collective-permute-start.4 = (bf16[8,32,512]{2,1,0:T(8,128)(2,1)}, bf16[8,32,512]{2,1,0:T(8,128)(2,1)S(1)}, u32[]{:S(2)}, u32[]{:S(2)}) collective-permute-start(bf16[8,32,512]{2,1,0:T(8,128)(2,1)} %get-tuple-element.15), channel_id=1, source_target_pairs={{0,1},{1,2},{2,3},{3,4},{4,5},{5,6},{6,7},{7,8},{8,9},{9,10},{10,1... | collective-permute-start | bytes 786440 | tf_op jit(solution)/shard_map/ppermute | solution.py:10
  18.4 6.7 %collective-permute-start.5 = (bf16[8,32,512]{2,1,0:T(8,128)(2,1)S(1)}, bf16[8,32,512]{2,1,0:T(8,128)(2,1)S(1)}, u32[]{:S(2)}, u32[]{:S(2)}) collective-permute-start(bf16[8,32,512]{2,1,0:T(8,128)(2,1)S(1)} %get-tuple-element.16), channel_id=1, source_target_pairs={{1,0},{2,1},{3,2},{4,3},{5,4},{6,5},{7,6},{8,7},{9,8},{10,9},{11,1... | collective-permute-start | bytes 786440 | tf_op jit(solution)/shard_map/ppermute | solution.py:10
  25.6 0.7 pad_dynamic-update-slice_fusion.7
  26.3 0.8 pad_dynamic-update-slice_fusion.6
  27.0 0.7 pad_dynamic-update-slice_fusion.5
  27.7 0.8 pad_dynamic-update-slice_fusion.4
  28.5 0.7 pad_dynamic-update-slice_fusion.3
  30.1 0.8 %pad_dynamic-update-slice_fusion.2 = bf16[384,1536]{1,0:T(8,128)(2,1)} fusion(bf16[384,1536]{1,0:T(8,128)(2,1)} %pad_dynamic-update-slice_fusion.3, bf16[48,1088]{1,0:T(8,128)(2,1)S(1)} %reshape.69), kind=kLoop, calls=%fused_computation.22 | loop fusion | bytes 251904
  30.9 0.7 pad_dynamic-update-slice_fusion.1
  31.9 2.6 %collective-permute-start.2 = (bf16[48,16,512]{2,1,0:T(8,128)(2,1)S(1)}, bf16[48,16,512]{2,1,0:T(8,128)(2,1)S(1)}, u32[]{:S(2)}, u32[]{:S(2)}) collective-permute-start(bf16[48,16,512]{2,1,0:T(8,128)(2,1)S(1)} %get-tuple-element.11), channel_id=1, source_target_pairs={{0,32},{32,64},{64,96},{96,128},{128,160},{160,192},{192,224},{1,3... | collective-permute-start | bytes 2359304 | tf_op jit(solution)/shard_map/ppermute | solution.py:10
  34.5 3.3 %collective-permute-start.3 = (bf16[48,16,512]{2,1,0:T(8,128)(2,1)S(1)}, bf16[48,16,512]{2,1,0:T(8,128)(2,1)S(1)}, u32[]{:S(2)}, u32[]{:S(2)}) collective-permute-start(bf16[48,16,512]{2,1,0:T(8,128)(2,1)S(1)} %get-tuple-element.12), channel_id=1, source_target_pairs={{32,0},{64,32},{96,64},{128,96},{160,128},{192,160},{224,192},{33,... | collective-permute-start | bytes 2359304 | tf_op jit(solution)/shard_map/ppermute | solution.py:10
  37.9 0.8 %pad_dynamic-update-slice_fusion = bf16[384,1536]{1,0:T(8,128)(2,1)} fusion(bf16[384,1536]{1,0:T(8,128)(2,1)} %pad_dynamic-update-slice_fusion.1, bf16[48,1088]{1,0:T(8,128)(2,1)S(1)} %reshape.69), kind=kLoop, calls=%fused_computation.20 | loop fusion | bytes 251904 | tf_op jit(solution)/shard_map/concatenate | solution.py:36
  38.7 4.7 %collective-permute-start.6 = (bf16[32,8,512]{2,1,0:T(8,128)(2,1)S(1)}, bf16[32,8,512]{2,1,0:T(8,128)(2,1)S(1)}, u32[]{:S(2)}, u32[]{:S(2)}) collective-permute-start(bf16[32,8,512]{2,1,0:T(8,128)(2,1)S(1)} %get-tuple-element.13), channel_id=1, source_target_pairs={{0,32},{32,64},{64,96},{96,128},{128,160},{160,192},{192,224},{1,3... | collective-permute-start | bytes 786440 | tf_op jit(solution)/shard_map/ppermute | solution.py:10
  43.4 1.9 %collective-permute-start.7 = (bf16[32,8,512]{2,1,0:T(8,128)(2,1)S(1)}, bf16[32,8,512]{2,1,0:T(8,128)(2,1)S(1)}, u32[]{:S(2)}, u32[]{:S(2)}) collective-permute-start(bf16[32,8,512]{2,1,0:T(8,128)(2,1)S(1)} %get-tuple-element.14), channel_id=1, source_target_pairs={{32,0},{64,32},{96,64},{128,96},{160,128},{192,160},{224,192},{33,... | collective-permute-start | bytes 786440 | tf_op jit(solution)/shard_map/ppermute | solution.py:10
  45.3 8.8 %collective-permute-done.2 = bf16[48,16,512]{2,1,0:T(8,128)(2,1)S(1)} collective-permute-done((bf16[48,16,512]{2,1,0:T(8,128)(2,1)S(1)}, bf16[48,16,512]{2,1,0:T(8,128)(2,1)S(1)}, u32[]{:S(2)}, u32[]{:S(2)}) %collective-permute-start.2) | collective-permute-done | bytes 786464 | tf_op jit(solution)/shard_map/ppermute | solution.py:10
  54.2 4.7 %collective-permute-done.3 = bf16[48,16,512]{2,1,0:T(8,128)(2,1)S(1)} collective-permute-done((bf16[48,16,512]{2,1,0:T(8,128)(2,1)S(1)}, bf16[48,16,512]{2,1,0:T(8,128)(2,1)S(1)}, u32[]{:S(2)}, u32[]{:S(2)}) %collective-permute-start.3) | collective-permute-done | bytes 786464 | tf_op jit(solution)/shard_map/ppermute | solution.py:10
  59.2 0.8 %fusion.12 = (bf16[24,64,512]{2,1,0:T(8,128)(2,1)S(1)}, bf16[24,64,512]{2,1,0:T(8,128)(2,1)S(1)}, bf16[24,64,512]{2,1,0:T(8,128)(2,1)S(1)}, bf16[24,64,512]{2,1,0:T(8,128)(2,1)S(1)}) fusion(bf16[48,64,512]{2,1,0:T(8,128)(2,1)S(1)} %pad_maximum_fusion), kind=kLoop, calls=%fused_computation.44 | loop fusion | bytes 12582912 | tf_op jit(solution)/shard_map/slice | solution.py:45
  60.0 2.0 %fusion.16 = f32[384,512]{1,0:T(8,128)S(1)} fusion(bf16[384,1536]{1,0:T(8,128)(2,1)} %pad_dynamic-update-slice_fusion, bf16[1536,512]{1,0:T(8,128)(2,1)S(1)} %bitcast.49), kind=kOutput, calls=%fused_computation.48 | convolution fusion | flops 603979776 | bytes 3538944 | tf_op jit(solution)/shard_map/dot_general | solution.py:45
  62.0 2.0 %fusion.17 = f32[384,512]{1,0:T(8,128)S(1)} fusion(bf16[384,1536]{1,0:T(8,128)(2,1)} %pad_dynamic-update-slice_fusion, bf16[1536,512]{1,0:T(8,128)(2,1)S(1)} %bitcast.48), kind=kOutput, calls=%fused_computation.49 | convolution fusion | flops 603979776 | bytes 3538944 | tf_op jit(solution)/shard_map/dot_general | solution.py:45
  64.1 2.0 %fusion.18 = f32[384,512]{1,0:T(8,128)S(1)} fusion(bf16[384,1536]{1,0:T(8,128)(2,1)} %pad_dynamic-update-slice_fusion, bf16[1536,512]{1,0:T(8,128)(2,1)S(1)} %bitcast.47), kind=kOutput, calls=%fused_computation.50 | convolution fusion | flops 603979776 | bytes 3538944 | tf_op jit(solution)/shard_map/dot_general | solution.py:45
  66.1 2.0 %fusion.19 = f32[384,512]{1,0:T(8,128)S(1)} fusion(bf16[384,1536]{1,0:T(8,128)(2,1)} %pad_dynamic-update-slice_fusion, bf16[1536,512]{1,0:T(8,128)(2,1)S(1)} %bitcast.46), kind=kOutput, calls=%fused_computation.51 | convolution fusion | flops 603979776 | bytes 3538944 | tf_op jit(solution)/shard_map/dot_general | solution.py:45
  68.2 0.3 pad_maximum_fusion.1
  68.5 1.1 %fusion = bf16[32,48,512]{2,1,0:T(8,128)(2,1)S(1)} fusion(f32[32,48,512]{2,1,0:T(8,128)S(1)} %bitcast.36, bf16[32,8,512]{2,1,0:T(8,128)(2,1)S(1)} %collective-permute-done.7, bf16[8,32,512]{2,1,0:T(8,128)(2,1)S(1)} %collective-permute-done.5, bf16[16,32,512]{2,1,0:T(8,128)(2,1)S(1)} %bitcast.41, bf16[8,32,512]{2,1,0:T(8,128)(2,1)S(1)} %collective-permute-done.4, ...), kind=kLoop, calls=%fused_computation.4 | loop fusion | flops 10223616 | bytes 6292992 | tf_op jit(solution)/shard_map/jit(_where)/select_n | solution.py:78
  69.6 0.3 fusion.13
  69.9 0.5 fusion.20
  70.4 0.5 fusion.21
  70.9 1.2 %copy-done.2 = bf16[4096,512]{1,0:T(8,128)(2,1)S(1)} copy-done((bf16[4096,512]{1,0:T(8,128)(2,1)S(1)}, bf16[4096,512]{1,0:T(8,128)(2,1)}, u32[]{:S(2)}) %copy-start.2) | copy-done | bytes 4194328
  72.1 4.4 %convolution_convert_fusion = bf16[512,4096]{1,0:T(8,128)(2,1)} fusion(bf16[4096,512]{1,0:T(8,128)(2,1)S(1)} %copy-done.2, f32[256,512]{1,0:T(8,128)S(1)} %fusion.21, f32[256,512]{1,0:T(8,128)S(1)} %fusion.20, bf16[512,512]{1,0:T(8,128)(2,1)S(1)} %fusion.2), kind=kOutput, calls=%fused_computation | convolution fusion | flops 2150891520 | bytes 9961472 | tf_op jit(solution)/shard_map/dot_general | solution.py:81
  (31 shorter events, 2.3 us)
Async XLA Ops:
  0.0 15.7 %copy-start = (bf16[512,16,32]{0,2,1:T(8,128)(2,1)S(1)}, bf16[512,16,32]{0,2,1:T(8,128)(2,1)}, u32[]{:S(2)}) copy-start(bf16[512,16,32]{0,2,1:T(8,128)(2,1)} %param.7) | copy-start | bytes 1572868
  0.0 25.0 %copy-start.1 = (bf16[17,17]{1,0:T(8,128)(2,1)S(1)}, bf16[17,17]{1,0:T(8,128)(2,1)}, u32[]{:S(2)}) copy-start(bf16[17,17]{1,0:T(8,128)(2,1)} %param.6) | copy-start | bytes 1738
  5.9 25.7 %collective-permute-start = (bf16[16,32,512]{2,1,0:T(8,128)(2,1)S(1)}, bf16[16,32,512]{2,1,0:T(8,128)(2,1)S(1)}, u32[]{:S(2)}, u32[]{:S(2)}) collective-permute-start(bf16[16,32,512]{2,1,0:T(8,128)(2,1)S(1)} %bitcast.42), channel_id=1, source_target_pairs={{0,1},{1,2},{2,3},{3,4},{4,5},{5,6},{6,7},{7,8},{8,9},{9,10},{10,1... | collective-permute-start | bytes 1572872 | tf_op jit(solution)/shard_map/ppermute | solution.py:10
  7.8 23.8 %collective-permute-start.1 = (bf16[16,32,512]{2,1,0:T(8,128)(2,1)S(1)}, bf16[16,32,512]{2,1,0:T(8,128)(2,1)S(1)}, u32[]{:S(2)}, u32[]{:S(2)}) collective-permute-start(bf16[16,32,512]{2,1,0:T(8,128)(2,1)S(1)} %bitcast.43), channel_id=1, source_target_pairs={{1,0},{2,1},{3,2},{4,3},{5,4},{6,5},{7,6},{8,7},{9,8},{10,9},{11,1... | collective-permute-start | bytes 1572872 | tf_op jit(solution)/shard_map/ppermute | solution.py:10
  16.4 22.2 %collective-permute-start.4 = (bf16[8,32,512]{2,1,0:T(8,128)(2,1)}, bf16[8,32,512]{2,1,0:T(8,128)(2,1)S(1)}, u32[]{:S(2)}, u32[]{:S(2)}) collective-permute-start(bf16[8,32,512]{2,1,0:T(8,128)(2,1)} %get-tuple-element.15), channel_id=1, source_target_pairs={{0,1},{1,2},{2,3},{3,4},{4,5},{5,6},{6,7},{7,8},{8,9},{9,10},{10,1... | collective-permute-start | bytes 786440 | tf_op jit(solution)/shard_map/ppermute | solution.py:10
  18.4 20.3 %collective-permute-start.5 = (bf16[8,32,512]{2,1,0:T(8,128)(2,1)S(1)}, bf16[8,32,512]{2,1,0:T(8,128)(2,1)S(1)}, u32[]{:S(2)}, u32[]{:S(2)}) collective-permute-start(bf16[8,32,512]{2,1,0:T(8,128)(2,1)S(1)} %get-tuple-element.16), channel_id=1, source_target_pairs={{1,0},{2,1},{3,2},{4,3},{5,4},{6,5},{7,6},{8,7},{9,8},{10,9},{11,1... | collective-permute-start | bytes 786440 | tf_op jit(solution)/shard_map/ppermute | solution.py:10
  31.9 22.3 %collective-permute-start.2 = (bf16[48,16,512]{2,1,0:T(8,128)(2,1)S(1)}, bf16[48,16,512]{2,1,0:T(8,128)(2,1)S(1)}, u32[]{:S(2)}, u32[]{:S(2)}) collective-permute-start(bf16[48,16,512]{2,1,0:T(8,128)(2,1)S(1)} %get-tuple-element.11), channel_id=1, source_target_pairs={{0,32},{32,64},{64,96},{96,128},{128,160},{160,192},{192,224},{1,3... | collective-permute-start | bytes 2359304 | tf_op jit(solution)/shard_map/ppermute | solution.py:10
  34.5 24.4 %collective-permute-start.3 = (bf16[48,16,512]{2,1,0:T(8,128)(2,1)S(1)}, bf16[48,16,512]{2,1,0:T(8,128)(2,1)S(1)}, u32[]{:S(2)}, u32[]{:S(2)}) collective-permute-start(bf16[48,16,512]{2,1,0:T(8,128)(2,1)S(1)} %get-tuple-element.12), channel_id=1, source_target_pairs={{32,0},{64,32},{96,64},{128,96},{160,128},{192,160},{224,192},{33,... | collective-permute-start | bytes 2359304 | tf_op jit(solution)/shard_map/ppermute | solution.py:10
  38.7 29.8 %collective-permute-start.6 = (bf16[32,8,512]{2,1,0:T(8,128)(2,1)S(1)}, bf16[32,8,512]{2,1,0:T(8,128)(2,1)S(1)}, u32[]{:S(2)}, u32[]{:S(2)}) collective-permute-start(bf16[32,8,512]{2,1,0:T(8,128)(2,1)S(1)} %get-tuple-element.13), channel_id=1, source_target_pairs={{0,32},{32,64},{64,96},{96,128},{128,160},{160,192},{192,224},{1,3... | collective-permute-start | bytes 786440 | tf_op jit(solution)/shard_map/ppermute | solution.py:10
  43.4 25.1 %collective-permute-start.7 = (bf16[32,8,512]{2,1,0:T(8,128)(2,1)S(1)}, bf16[32,8,512]{2,1,0:T(8,128)(2,1)S(1)}, u32[]{:S(2)}, u32[]{:S(2)}) collective-permute-start(bf16[32,8,512]{2,1,0:T(8,128)(2,1)S(1)} %get-tuple-element.14), channel_id=1, source_target_pairs={{32,0},{64,32},{96,64},{128,96},{160,128},{192,160},{224,192},{33,... | collective-permute-start | bytes 786440 | tf_op jit(solution)/shard_map/ppermute | solution.py:10
  69.9 2.2 %copy-start.2 = (bf16[4096,512]{1,0:T(8,128)(2,1)S(1)}, bf16[4096,512]{1,0:T(8,128)(2,1)}, u32[]{:S(2)}) copy-start(bf16[4096,512]{1,0:T(8,128)(2,1)} %param.5) | copy-start | bytes 12582916

commit v10 on v3

--- a/solution.py
+++ b/solution.py
@@ -71,8 +71,27 @@
     group = 4 if rows % 4 == 0 else rows
     forward = blur_mat(point_spread, group, cols + 2 * h, h)
     adjoint = blur_mat(point_spread[::-1, ::-1], group, cols, h)
-    near = window(spectra.reshape(rows, cols, waves), 2 * h)
-    blurred = blur(near, forward, group, rows + 2 * h, cols + 2 * h, h)
+    wide = 2 * h
+    block = spectra.reshape(rows, cols, waves)
+    top = send(block[rows - wide :], "tile", 1)
+    bottom = send(block[:wide], "tile", -1)
+    band = jnp.concatenate([top, block, bottom], axis=0)
+    left = send(band[:, cols - wide :], "wave", 1)
+    right = send(band[:, :wide], "wave", -1)
+    span = group + 2 * h
+    blurred = jnp.concatenate(
+        [
+            jnp.dot(
+                forward,
+                jnp.concatenate(
+                    [left[g : g + span], band[g : g + span], right[g : g + span]], axis=1
+                ).reshape(-1, waves),
+                preferred_element_type=jnp.float32,
+            )
+            for g in range(0, rows + 2 * h, group)
+        ],
+        axis=0,
+    )
     blurred = blurred.reshape(rows + 2 * h, cols + 2 * h, waves)
     residual = (blurred - measured.astype(jnp.float32)).astype(jnp.bfloat16)
     residual = jnp.where(inside(rows, cols, h), residual, jnp.zeros_like(residual))

time: 74.7 us -> 76 us (1.017)
  the two profiles are of different devices: /device:TPU:29 before, /device:TPU:34 now
where the time goes in v10:
time: 76 us; the launch traced here: 75.5 us
  starting transfers between devices  34.7 us (46%)
  matrix products  17.1 us (23%)
  waiting for transfers between devices  9.15 us (12%)
  local copies, waits for them, and re-layouts  8.65 us (11%)
  other arithmetic  5.59 us (7%)
    ppermute x8, starting transfers between devices, send(): return lax.ppermute(block, axis, pairs)  34.7 us
    ppermute x8, waiting for transfers between devices, send(): return lax.ppermute(block, axis, pairs)  9.15 us
    dot_general x1, matrix products, shards(): jnp.dot(coefficients.reshape(rows * cols, profiles), profile_basis, prefe...  5.84 us
    dot_general x1, matrix products, shards(): lax.dot_general(tau_grad, profile_basis, (((1,), (1,)), ((), ())), prefer...  4.41 us
    dot_general x8, matrix products, shards(): jnp.dot(forward, jnp.concatenate([left[g:g + span], band[g:g + span], rig...  3.61 us
    reshape x2, local copies, waits for them, and re-layouts, blur_mat(): strip = strip.astype(psf.dtype).reshape(cols, k * win_cols)  2.88 us
    unnamed x12, local copies, waits for them, and re-layouts  2.33 us
    select_n x1, other arithmetic, shards(): jnp.where(inside(rows, cols, h), residual, jnp.zeros_like(residual))  1.98 us
  transfers between devices with their start and end apart: 8, of which 2 were waited for; matrix products, arithmetic and copies ran while one was open for 20% of the time, Pallas kernels for 0%

profile of v10, /device:TPU:34, one launch (start us, length us, event | category | flops | bytes accessed | tf_op | source)
XLA Modules:
  0.0 75.5 jit_solution(18191038915602509848)
XLA Ops:
  0.0 5.8 %fusion.6 = bf16[512,512]{1,0:T(8,128)(2,1)S(1)} fusion(bf16[512,4096]{1,0:T(8,128)(2,1)} %bitcast.63, bf16[4096,512]{1,0:T(8,128)(2,1)} %param.5), kind=kOutput, calls=%fused_computation.34 | convolution fusion | flops 2148007936 | bytes 8912896 | tf_op jit(solution)/shard_map/dot_general | solution.py:67
  5.9 6.7 %collective-permute-start.1 = (bf16[16,32,512]{2,1,0:T(8,128)(2,1)S(1)}, bf16[16,32,512]{2,1,0:T(8,128)(2,1)S(1)}, u32[]{:S(2)}, u32[]{:S(2)}) collective-permute-start(bf16[16,32,512]{2,1,0:T(8,128)(2,1)S(1)} %bitcast.45), channel_id=1, source_target_pairs={{1,0},{2,1},{3,2},{4,3},{5,4},{6,5},{7,6},{8,7},{9,8},{10,9},{11,1... | collective-permute-start | bytes 1572872 | tf_op jit(solution)/shard_map/ppermute | solution.py:10
  12.6 1.9 %collective-permute-start = (bf16[16,32,512]{2,1,0:T(8,128)(2,1)S(1)}, bf16[16,32,512]{2,1,0:T(8,128)(2,1)S(1)}, u32[]{:S(2)}, u32[]{:S(2)}) collective-permute-start(bf16[16,32,512]{2,1,0:T(8,128)(2,1)S(1)} %bitcast.46), channel_id=1, source_target_pairs={{0,1},{1,2},{2,3},{3,4},{4,5},{5,6},{6,7},{7,8},{8,9},{9,10},{10,1... | collective-permute-start | bytes 1572872 | tf_op jit(solution)/shard_map/ppermute | solution.py:10
  14.5 0.8 %fusion.60 = (bf16[8,32,512]{2,1,0:T(8,128)(2,1)}, bf16[8,32,512]{2,1,0:T(8,128)(2,1)}) fusion(bf16[16,32,512]{2,1,0:T(8,128)(2,1)S(1)} %bitcast.42), kind=kLoop, calls=%fused_computation.102 | loop fusion | bytes 1048576 | tf_op jit(solution)/shard_map/slice | solution.py:15
  15.4 6.6 %collective-permute-start.5 = (bf16[8,32,512]{2,1,0:T(8,128)(2,1)}, bf16[8,32,512]{2,1,0:T(8,128)(2,1)S(1)}, u32[]{:S(2)}, u32[]{:S(2)}) collective-permute-start(bf16[8,32,512]{2,1,0:T(8,128)(2,1)} %get-tuple-element.36), channel_id=1, source_target_pairs={{1,0},{2,1},{3,2},{4,3},{5,4},{6,5},{7,6},{8,7},{9,8},{10,9},{11,1... | collective-permute-start | bytes 786440 | tf_op jit(solution)/shard_map/ppermute | solution.py:10
  22.0 1.9 %collective-permute-start.4 = (bf16[8,32,512]{2,1,0:T(8,128)(2,1)}, bf16[8,32,512]{2,1,0:T(8,128)(2,1)}, u32[]{:S(2)}, u32[]{:S(2)}) collective-permute-start(bf16[8,32,512]{2,1,0:T(8,128)(2,1)} %get-tuple-element.35), channel_id=1, source_target_pairs={{0,1},{1,2},{2,3},{3,4},{4,5},{5,6},{6,7},{7,8},{8,9},{9,10},{10,1... | collective-permute-start | bytes 786440 | tf_op jit(solution)/shard_map/ppermute | solution.py:10
  24.1 0.9 %fusion.8 = bf16[32,17,48]{2,1,0:T(8,128)(2,1)} fusion(bf16[17,17]{1,0:T(8,128)(2,1)S(1)} %rev.3), kind=kOutput, calls=%fused_computation.46 | convolution fusion | flops 966144 | bytes 52802 | tf_op jit(solution)/shard_map/ab,xbX->xaX/dot_general | solution.py:29
  24.9 1.0 %fusion.7 = bf16[48,17,64]{2,1,0:T(8,128)(2,1)} fusion(bf16[17,17]{1,0:T(8,128)(2,1)S(1)} %copy-done.4), kind=kOutput, calls=%fused_computation.44 | convolution fusion | flops 1932288 | bytes 105026 | tf_op jit(solution)/shard_map/ab,xbX->xaX/dot_general | solution.py:29
  25.9 5.8 %collective-permute-done = bf16[16,32,512]{2,1,0:T(8,128)(2,1)S(1)} collective-permute-done((bf16[16,32,512]{2,1,0:T(8,128)(2,1)S(1)}, bf16[16,32,512]{2,1,0:T(8,128)(2,1)S(1)}, u32[]{:S(2)}, u32[]{:S(2)}) %collective-permute-start) | collective-permute-done | bytes 524320 | tf_op jit(solution)/shard_map/ppermute | solution.py:10
  31.8 1.3 %fusion.57 = (bf16[48,16,512]{2,1,0:T(8,128)(2,1)}, bf16[48,16,512]{2,1,0:T(8,128)(2,1)}) fusion(bf16[48,32,512]{2,1,0:T(8,128)(2,1)S(1)} %pad_maximum_fusion), kind=kLoop, calls=%fused_computation.99 | loop fusion | bytes 3145728 | tf_op jit(solution)/shard_map/slice | solution.py:79
  33.1 7.6 %collective-permute-start.3 = (bf16[48,16,512]{2,1,0:T(8,128)(2,1)}, bf16[48,16,512]{2,1,0:T(8,128)(2,1)S(1)}, u32[]{:S(2)}, u32[]{:S(2)}) collective-permute-start(bf16[48,16,512]{2,1,0:T(8,128)(2,1)} %get-tuple-element.10), channel_id=1, source_target_pairs={{32,0},{64,32},{96,64},{128,96},{160,128},{192,160},{224,192},{33,... | collective-permute-start | bytes 2359304 | tf_op jit(solution)/shard_map/ppermute | solution.py:10
  40.8 1.9 %collective-permute-start.2 = (bf16[48,16,512]{2,1,0:T(8,128)(2,1)}, bf16[48,16,512]{2,1,0:T(8,128)(2,1)S(1)}, u32[]{:S(2)}, u32[]{:S(2)}) collective-permute-start(bf16[48,16,512]{2,1,0:T(8,128)(2,1)} %get-tuple-element.9), channel_id=1, source_target_pairs={{0,32},{32,64},{64,96},{96,128},{128,160},{160,192},{192,224},{1,3... | collective-permute-start | bytes 2359304 | tf_op jit(solution)/shard_map/ppermute | solution.py:10
  42.8 1.2 %reshape.90 = bf16[48,1088]{1,0:T(8,128)(2,1)S(1)} reshape(bf16[48,17,64]{2,1,0:T(8,128)(2,1)} %fusion.7) | data formatting | bytes 208896 | tf_op jit(solution)/shard_map/reshape | solution.py:30
  44.0 1.7 %reshape.89 = bf16[32,816]{1,0:T(8,128)(2,1)} reshape(bf16[32,17,48]{2,1,0:T(8,128)(2,1)} %fusion.8) | data formatting | bytes 104448 | tf_op jit(solution)/shard_map/reshape | solution.py:30
  45.7 0.9 %pad_maximum_fusion.11 = (bf16[32,8,512]{2,1,0:T(8,128)(2,1)S(1)}, bf16[32,8,512]{2,1,0:T(8,128)(2,1)S(1)}) fusion(bf16[8,32,512]{2,1,0:T(8,128)(2,1)S(1)} %collective-permute-done.5, bf16[16,32,512]{2,1,0:T(8,128)(2,1)S(1)} %bitcast.43, bf16[8,32,512]{2,1,0:T(8,128)(2,1)} %collective-permute-done.4), kind=kLoop, calls=%fused_computation.85 | loop fusion | flops 1572864 | bytes 1572864 | tf_op jit(solution)/shard_map/slice | solution.py:18
  46.6 6.0 %collective-permute-start.7 = (bf16[32,8,512]{2,1,0:T(8,128)(2,1)S(1)}, bf16[32,8,512]{2,1,0:T(8,128)(2,1)S(1)}, u32[]{:S(2)}, u32[]{:S(2)}) collective-permute-start(bf16[32,8,512]{2,1,0:T(8,128)(2,1)S(1)} %get-tuple-element.12), channel_id=1, source_target_pairs={{32,0},{64,32},{96,64},{128,96},{160,128},{192,160},{224,192},{33,... | collective-permute-start | bytes 786440 | tf_op jit(solution)/shard_map/ppermute | solution.py:10
  52.6 1.9 %collective-permute-start.6 = (bf16[32,8,512]{2,1,0:T(8,128)(2,1)S(1)}, bf16[32,8,512]{2,1,0:T(8,128)(2,1)S(1)}, u32[]{:S(2)}, u32[]{:S(2)}) collective-permute-start(bf16[32,8,512]{2,1,0:T(8,128)(2,1)S(1)} %get-tuple-element.11), channel_id=1, source_target_pairs={{0,32},{32,64},{64,96},{96,128},{128,160},{160,192},{192,224},{1,3... | collective-permute-start | bytes 786440 | tf_op jit(solution)/shard_map/ppermute | solution.py:10
  54.6 1.5 %fusion.16 = (bf16[20,32,512]{2,1,0:T(8,128)(2,1)S(1)}, bf16[20,32,512]{2,1,0:T(8,128)(2,1)S(1)}, bf16[20,32,512]{2,1,0:T(8,128)(2,1)S(1)}, bf16[20,32,512]{2,1,...) fusion(bf16[16,32,512]{2,1,0:T(8,128)(2,1)S(1)} %bitcast.48, ...), kind=kLoop, calls=%fused_computation.61 | loop fusion | flops 1966080 | bytes 5505024 | tf_op jit(solution)/shard_map/concatenate | solution.py:78
  56.4 3.4 %collective-permute-done.2 = bf16[48,16,512]{2,1,0:T(8,128)(2,1)S(1)} collective-permute-done((bf16[48,16,512]{2,1,0:T(8,128)(2,1)}, bf16[48,16,512]{2,1,0:T(8,128)(2,1)S(1)}, u32[]{:S(2)}, u32[]{:S(2)}) %collective-permute-start.2) | collective-permute-done | bytes 786464 | tf_op jit(solution)/shard_map/ppermute | solution.py:10
  60.4 0.5 convolution_dynamic-update-slice_fusion.7
  60.8 0.4 convolution_dynamic-update-slice_fusion.6
  61.5 0.5 convolution_dynamic-update-slice_fusion.5
  62.0 0.6 copy-done.2
  62.8 0.5 convolution_dynamic-update-slice_fusion.4
  63.3 0.5 convolution_dynamic-update-slice_fusion.3
  64.0 0.4 convolution_dynamic-update-slice_fusion.2
  64.4 0.4 convolution_dynamic-update-slice_fusion.1
  64.9 0.4 convolution_dynamic-update-slice_fusion
  65.4 2.0 %fusion = bf16[32,48,512]{2,1,0:T(8,128)(2,1)S(1)} fusion(f32[32,48,512]{2,1,0:T(8,128)S(1)} %bitcast.50, bf16[32,8,512]{2,1,0:T(8,128)(2,1)S(1)} %collective-permute-done.7, bf16[8,32,512]{2,1,0:T(8,128)(2,1)S(1)} %collective-permute-done.5, bf16[16,32,512]{2,1,0:T(8,128)(2,1)S(1)} %bitcast.44, bf16[8,32,512]{2,1,0:T(8,128)(2,1)} %collective-permute-done.4, ...), kind=kLoop, calls=%fused_computation.2 | loop fusion | flops 10223616 | bytes 6292992 | tf_op jit(solution)/shard_map/jit(_where)/select_n | solution.py:97
  67.4 0.5 fusion.56
  69.6 1.5 %copy-done.5 = bf16[4096,512]{1,0:T(8,128)(2,1)S(1)} copy-done((bf16[4096,512]{1,0:T(8,128)(2,1)S(1)}, bf16[4096,512]{1,0:T(8,128)(2,1)}, u32[]{:S(2)}) %copy-start.5) | copy-done | bytes 4194328
  71.1 4.4 %convolution_convert_fusion = bf16[512,4096]{1,0:T(8,128)(2,1)} fusion(bf16[4096,512]{1,0:T(8,128)(2,1)S(1)} %copy-done.5, f32[128,512]{1,0:T(8,128)S(1)} %fusion.40, f32[128,512]{1,0:T(8,128)S(1)} %fusion.42, f32[128,512]{1,0:T(8,128)S(1)} %fusion.44, f32[128,512]{1,0:T(8,128)S(1)} %fusion.46, bf16[512,512]{1,0:T(8,128)(2,1)S(1)} %fusion.6), kind=kOutput, calls=%fused_computation | convolution fusion | flops 2151415808 | bytes 9961472 | tf_op jit(solution)/shard_map/dot_general | solution.py:100
  (31 shorter events, 3.6 us)
Async XLA Ops:
  0.0 14.5 %copy-start = (bf16[512,16,32]{0,2,1:T(8,128)(2,1)S(1)}, bf16[512,16,32]{0,2,1:T(8,128)(2,1)}, u32[]{:S(2)}) copy-start(bf16[512,16,32]{0,2,1:T(8,128)(2,1)} %param.7) | copy-start | bytes 1572868
  0.0 23.9 %copy-start.4 = (bf16[17,17]{1,0:T(8,128)(2,1)S(1)}, bf16[17,17]{1,0:T(8,128)(2,1)}, u32[]{:S(2)}) copy-start(bf16[17,17]{1,0:T(8,128)(2,1)} %param.6) | copy-start | bytes 1738
  5.9 20.0 %collective-permute-start.1 = (bf16[16,32,512]{2,1,0:T(8,128)(2,1)S(1)}, bf16[16,32,512]{2,1,0:T(8,128)(2,1)S(1)}, u32[]{:S(2)}, u32[]{:S(2)}) collective-permute-start(bf16[16,32,512]{2,1,0:T(8,128)(2,1)S(1)} %bitcast.45), channel_id=1, source_target_pairs={{1,0},{2,1},{3,2},{4,3},{5,4},{6,5},{7,6},{8,7},{9,8},{10,9},{11,1... | collective-permute-start | bytes 1572872 | tf_op jit(solution)/shard_map/ppermute | solution.py:10
  12.6 19.1 %collective-permute-start = (bf16[16,32,512]{2,1,0:T(8,128)(2,1)S(1)}, bf16[16,32,512]{2,1,0:T(8,128)(2,1)S(1)}, u32[]{:S(2)}, u32[]{:S(2)}) collective-permute-start(bf16[16,32,512]{2,1,0:T(8,128)(2,1)S(1)} %bitcast.46), channel_id=1, source_target_pairs={{0,1},{1,2},{2,3},{3,4},{4,5},{5,6},{6,7},{7,8},{8,9},{9,10},{10,1... | collective-permute-start | bytes 1572872 | tf_op jit(solution)/shard_map/ppermute | solution.py:10
  15.4 30.3 %collective-permute-start.5 = (bf16[8,32,512]{2,1,0:T(8,128)(2,1)}, bf16[8,32,512]{2,1,0:T(8,128)(2,1)S(1)}, u32[]{:S(2)}, u32[]{:S(2)}) collective-permute-start(bf16[8,32,512]{2,1,0:T(8,128)(2,1)} %get-tuple-element.36), channel_id=1, source_target_pairs={{1,0},{2,1},{3,2},{4,3},{5,4},{6,5},{7,6},{8,7},{9,8},{10,9},{11,1... | collective-permute-start | bytes 786440 | tf_op jit(solution)/shard_map/ppermute | solution.py:10
  22.0 23.7 %collective-permute-start.4 = (bf16[8,32,512]{2,1,0:T(8,128)(2,1)}, bf16[8,32,512]{2,1,0:T(8,128)(2,1)}, u32[]{:S(2)}, u32[]{:S(2)}) collective-permute-start(bf16[8,32,512]{2,1,0:T(8,128)(2,1)} %get-tuple-element.35), channel_id=1, source_target_pairs={{0,1},{1,2},{2,3},{3,4},{4,5},{5,6},{6,7},{7,8},{8,9},{9,10},{10,1... | collective-permute-start | bytes 786440 | tf_op jit(solution)/shard_map/ppermute | solution.py:10
  31.7 1.5 %copy-start.1 = (bf16[16,32,512]{2,1,0:T(8,128)(2,1)}, bf16[16,32,512]{2,1,0:T(8,128)(2,1)S(1)}, u32[]{:S(2)}) copy-start(bf16[16,32,512]{2,1,0:T(8,128)(2,1)S(1)} %collective-permute-done) | copy-start | bytes 1572868
  33.1 22.9 %collective-permute-start.3 = (bf16[48,16,512]{2,1,0:T(8,128)(2,1)}, bf16[48,16,512]{2,1,0:T(8,128)(2,1)S(1)}, u32[]{:S(2)}, u32[]{:S(2)}) collective-permute-start(bf16[48,16,512]{2,1,0:T(8,128)(2,1)} %get-tuple-element.10), channel_id=1, source_target_pairs={{32,0},{64,32},{96,64},{128,96},{160,128},{192,160},{224,192},{33,... | collective-permute-start | bytes 2359304 | tf_op jit(solution)/shard_map/ppermute | solution.py:10
  40.8 19.0 %collective-permute-start.2 = (bf16[48,16,512]{2,1,0:T(8,128)(2,1)}, bf16[48,16,512]{2,1,0:T(8,128)(2,1)S(1)}, u32[]{:S(2)}, u32[]{:S(2)}) collective-permute-start(bf16[48,16,512]{2,1,0:T(8,128)(2,1)} %get-tuple-element.9), channel_id=1, source_target_pairs={{0,32},{32,64},{64,96},{96,128},{128,160},{160,192},{192,224},{1,3... | collective-permute-start | bytes 2359304 | tf_op jit(solution)/shard_map/ppermute | solution.py:10
  46.6 18.7 %collective-permute-start.7 = (bf16[32,8,512]{2,1,0:T(8,128)(2,1)S(1)}, bf16[32,8,512]{2,1,0:T(8,128)(2,1)S(1)}, u32[]{:S(2)}, u32[]{:S(2)}) collective-permute-start(bf16[32,8,512]{2,1,0:T(8,128)(2,1)S(1)} %get-tuple-element.12), channel_id=1, source_target_pairs={{32,0},{64,32},{96,64},{128,96},{160,128},{192,160},{224,192},{33,... | collective-permute-start | bytes 786440 | tf_op jit(solution)/shard_map/ppermute | solution.py:10
  52.6 12.7 %collective-permute-start.6 = (bf16[32,8,512]{2,1,0:T(8,128)(2,1)S(1)}, bf16[32,8,512]{2,1,0:T(8,128)(2,1)S(1)}, u32[]{:S(2)}, u32[]{:S(2)}) collective-permute-start(bf16[32,8,512]{2,1,0:T(8,128)(2,1)S(1)} %get-tuple-element.11), channel_id=1, source_target_pairs={{0,32},{32,64},{64,96},{96,128},{128,160},{160,192},{192,224},{1,3... | collective-permute-start | bytes 786440 | tf_op jit(solution)/shard_map/ppermute | solution.py:10
  61.5 1.0 %copy-start.2 = (bf16[16,32,512]{2,1,0:T(8,128)(2,1)S(1)}, bf16[16,32,512]{2,1,0:T(8,128)(2,1)}, u32[]{:S(2)}) copy-start(bf16[16,32,512]{2,1,0:T(8,128)(2,1)} %copy-done.1) | copy-start | bytes 1572868
  67.3 0.8 %copy-start.3 = (bf16[32,816]{1,0:T(8,128)(2,1)S(1)}, bf16[32,816]{1,0:T(8,128)(2,1)}, u32[]{:S(2)}) copy-start(bf16[32,816]{1,0:T(8,128)(2,1)} %reshape.89) | copy-start | bytes 156676
  68.9 2.2 %copy-start.5 = (bf16[4096,512]{1,0:T(8,128)(2,1)S(1)}, bf16[4096,512]{1,0:T(8,128)(2,1)}, u32[]{:S(2)}) copy-start(bf16[4096,512]{1,0:T(8,128)(2,1)} %param.5) | copy-start | bytes 12582916

commit v11 on v3

--- a/solution.py
+++ b/solution.py
@@ -10,8 +10,10 @@
     return lax.ppermute(block, axis, pairs)
 
 
-def window(block, h):
+def window(block, h, after=None):
     rows, cols = block.shape[0], block.shape[1]
+    if after is not None:
+        after, block = lax.optimization_barrier((after, block))
     top = send(block[rows - h :], "tile", 1)
     bottom = send(block[:h], "tile", -1)
     band = jnp.concatenate([top, block, bottom], axis=0)
@@ -63,7 +65,6 @@
     rows, cols, profiles = coefficients.shape
     waves = profile_basis.shape[1]
     h = point_spread.shape[0] // 2
-    measured = window(observed.transpose(1, 2, 0), h)
     opacity = jnp.dot(
         coefficients.reshape(rows * cols, profiles), profile_basis, preferred_element_type=jnp.float32
     )
@@ -71,7 +72,15 @@
     group = 4 if rows % 4 == 0 else rows
     forward = blur_mat(point_spread, group, cols + 2 * h, h)
     adjoint = blur_mat(point_spread[::-1, ::-1], group, cols, h)
-    near = window(spectra.reshape(rows, cols, waves), 2 * h)
+    block = spectra.reshape(rows, cols, waves)
+    wide = 2 * h
+    top = send(block[rows - wide :], "tile", 1)
+    bottom = send(block[:wide], "tile", -1)
+    measured = window(observed.transpose(1, 2, 0), h, (top, bottom))
+    band = jnp.concatenate([top, block, bottom], axis=0)
+    left = send(band[:, cols - wide :], "wave", 1)
+    right = send(band[:, :wide], "wave", -1)
+    near = jnp.concatenate([left, band, right], axis=1)
     blurred = blur(near, forward, group, rows + 2 * h, cols + 2 * h, h)
     blurred = blurred.reshape(rows + 2 * h, cols + 2 * h, waves)
     residual = (blurred - measured.astype(jnp.float32)).astype(jnp.bfloat16)

time: 74.7 us -> 91.5 us (1.22)
  the two profiles are of different devices: /device:TPU:29 before, /device:TPU:35 now
where the time goes in v11:
time: 91.5 us; the launch traced here: 91.1 us
  waiting for transfers between devices  34.9 us (38%)
  starting transfers between devices  29.4 us (32%)
  matrix products  16.4 us (18%)
  local copies, waits for them, and re-layouts  7.96 us (9%)
  other arithmetic  2.16 us (2%)
    ppermute x8, waiting for transfers between devices, send(): return lax.ppermute(block, axis, pairs)  34.9 us
    ppermute x8, starting transfers between devices, send(): return lax.ppermute(block, axis, pairs)  29.4 us
    dot_general x1, matrix products, shards(): jnp.dot(coefficients.reshape(rows * cols, profiles), profile_basis, prefe...  5.84 us
    dot_general x12, matrix products, blur(): jnp.dot(mat, flat[g * win_cols:g * win_cols + span], preferred_element_ty...  4.99 us
    dot_general x1, matrix products, shards(): lax.dot_general(tau_grad, profile_basis, (((1,), (1,)), ((), ())), prefer...  4.41 us
    slice x2, local copies, waits for them, and re-layouts, blur(): flat[g * win_cols:g * win_cols + span]  1.86 us
  transfers between devices with their start and end apart: 8, of which 3 were waited for; matrix products, arithmetic and copies ran while one was open for 13% of the time, Pallas kernels for 0%

profile of v11, /device:TPU:35, one launch (start us, length us, event | category | flops | bytes accessed | tf_op | source)
XLA Modules:
  0.0 91.1 jit_solution(7729163608682297569)
XLA Ops:
  0.0 5.8 %fusion.2 = bf16[512,512]{1,0:T(8,128)(2,1)S(1)} fusion(bf16[512,4096]{1,0:T(8,128)(2,1)} %bitcast.61, bf16[4096,512]{1,0:T(8,128)(2,1)} %param.5), kind=kOutput, calls=%fused_computation.11 | convolution fusion | flops 2148007936 | bytes 8912896 | tf_op jit(solution)/shard_map/dot_general | solution.py:68
  5.9 5.5 %collective-permute-start = (bf16[16,32,512]{2,1,0:T(8,128)(2,1)S(1)}, bf16[16,32,512]{2,1,0:T(8,128)(2,1)S(1)}, u32[]{:S(2)}, u32[]{:S(2)}) collective-permute-start(bf16[16,32,512]{2,1,0:T(8,128)(2,1)S(1)} %bitcast.45), channel_id=1, source_target_pairs={{0,1},{1,2},{2,3},{3,4},{4,5},{5,6},{6,7},{7,8},{8,9},{9,10},{10,1... | collective-permute-start | bytes 1572872 | tf_op jit(solution)/shard_map/ppermute | solution.py:10
  11.3 1.9 %collective-permute-start.1 = (bf16[16,32,512]{2,1,0:T(8,128)(2,1)S(1)}, bf16[16,32,512]{2,1,0:T(8,128)(2,1)S(1)}, u32[]{:S(2)}, u32[]{:S(2)}) collective-permute-start(bf16[16,32,512]{2,1,0:T(8,128)(2,1)S(1)} %bitcast.46), channel_id=1, source_target_pairs={{1,0},{2,1},{3,2},{4,3},{5,4},{6,5},{7,6},{8,7},{9,8},{10,9},{11,1... | collective-permute-start | bytes 1572872 | tf_op jit(solution)/shard_map/ppermute | solution.py:10
  13.4 0.9 fusion.4
  14.5 8.1 %collective-permute-done = bf16[16,32,512]{2,1,0:T(8,128)(2,1)S(1)} collective-permute-done((bf16[16,32,512]{2,1,0:T(8,128)(2,1)S(1)}, bf16[16,32,512]{2,1,0:T(8,128)(2,1)S(1)}, u32[]{:S(2)}, u32[]{:S(2)}) %collective-permute-start) | collective-permute-done | bytes 524320 | tf_op jit(solution)/shard_map/ppermute | solution.py:10
  22.6 1.9 %collective-permute-done.1 = bf16[16,32,512]{2,1,0:T(8,128)(2,1)S(1)} collective-permute-done((bf16[16,32,512]{2,1,0:T(8,128)(2,1)S(1)}, bf16[16,32,512]{2,1,0:T(8,128)(2,1)S(1)}, u32[]{:S(2)}, u32[]{:S(2)}) %collective-permute-start.1) | collective-permute-done | bytes 524320 | tf_op jit(solution)/shard_map/ppermute | solution.py:10
  24.5 0.9 fusion.50
  25.4 3.4 %collective-permute-start.4 = (bf16[8,32,512]{2,1,0:T(8,128)(2,1)}, bf16[8,32,512]{2,1,0:T(8,128)(2,1)S(1)}, u32[]{:S(2)}, u32[]{:S(2)}) collective-permute-start(bf16[8,32,512]{2,1,0:T(8,128)(2,1)} %get-tuple-element.24), channel_id=1, source_target_pairs={{0,1},{1,2},{2,3},{3,4},{4,5},{5,6},{6,7},{7,8},{8,9},{9,10},{10,1... | collective-permute-start | bytes 786440 | tf_op jit(solution)/shard_map/ppermute | solution.py:10
  29.0 1.3 %fusion.48 = (bf16[48,16,512]{2,1,0:T(8,128)(2,1)}, bf16[48,16,512]{2,1,0:T(8,128)(2,1)}) fusion(bf16[48,32,512]{2,1,0:T(8,128)(2,1)S(1)} %pad_maximum_fusion.1), kind=kLoop, calls=%fused_computation.71 | loop fusion | bytes 3145728 | tf_op jit(solution)/shard_map/slice | solution.py:81
  30.3 3.1 %collective-permute-start.2 = (bf16[48,16,512]{2,1,0:T(8,128)(2,1)}, bf16[48,16,512]{2,1,0:T(8,128)(2,1)S(1)}, u32[]{:S(2)}, u32[]{:S(2)}) collective-permute-start(bf16[48,16,512]{2,1,0:T(8,128)(2,1)} %get-tuple-element.19), channel_id=1, source_target_pairs={{0,32},{32,64},{64,96},{96,128},{128,160},{160,192},{192,224},{1,3... | collective-permute-start | bytes 2359304 | tf_op jit(solution)/shard_map/ppermute | solution.py:10
  33.5 5.3 %collective-permute-start.3 = (bf16[48,16,512]{2,1,0:T(8,128)(2,1)}, bf16[48,16,512]{2,1,0:T(8,128)(2,1)}, u32[]{:S(2)}, u32[]{:S(2)}) collective-permute-start(bf16[48,16,512]{2,1,0:T(8,128)(2,1)} %get-tuple-element.20), channel_id=1, source_target_pairs={{32,0},{64,32},{96,64},{128,96},{160,128},{192,160},{224,192},{33,... | collective-permute-start | bytes 2359304 | tf_op jit(solution)/shard_map/ppermute | solution.py:10
  38.8 2.7 %collective-permute-start.5 = (bf16[8,32,512]{2,1,0:T(8,128)(2,1)}, bf16[8,32,512]{2,1,0:T(8,128)(2,1)}, u32[]{:S(2)}, u32[]{:S(2)}) collective-permute-start(bf16[8,32,512]{2,1,0:T(8,128)(2,1)} %get-tuple-element.23), channel_id=1, source_target_pairs={{1,0},{2,1},{3,2},{4,3},{5,4},{6,5},{7,6},{8,7},{9,8},{10,9},{11,1... | collective-permute-start | bytes 786440 | tf_op jit(solution)/shard_map/ppermute | solution.py:10
  41.8 1.1 %reshape.74 = bf16[32,816]{1,0:T(8,128)(2,1)S(1)} reshape(bf16[32,17,48]{2,1,0:T(8,128)(2,1)} %fusion.4) | data formatting | bytes 104448 | tf_op jit(solution)/shard_map/reshape | solution.py:32
  42.9 24.9 %collective-permute-done.5 = bf16[8,32,512]{2,1,0:T(8,128)(2,1)} collective-permute-done((bf16[8,32,512]{2,1,0:T(8,128)(2,1)}, bf16[8,32,512]{2,1,0:T(8,128)(2,1)}, u32[]{:S(2)}, u32[]{:S(2)}) %collective-permute-start.5) | collective-permute-done | bytes 262176 | tf_op jit(solution)/shard_map/ppermute | solution.py:10
  67.8 1.0 %constant_dynamic-update-slice_fusion = bf16[32,32,512]{2,1,0:T(8,128)(2,1)S(1)} fusion(bf16[32,32,512]{2,1,0:T(8,128)(2,1)S(1)} %constant_dynamic-update-slice_fusion.1, bf16[8,32,512]{2,1,0:T(8,128)(2,1)} %collective-permute-done.5), kind=kLoop, calls=%fused_computation.54 | loop fusion | bytes 524288 | tf_op jit(solution)/shard_map/concatenate | solution.py:19
  68.9 1.9 %collective-permute-start.6 = (bf16[32,8,512]{2,1,0:T(8,128)(2,1)S(1)}, bf16[32,8,512]{2,1,0:T(8,128)(2,1)S(1)}, u32[]{:S(2)}, u32[]{:S(2)}) collective-permute-start(bf16[32,8,512]{2,1,0:T(8,128)(2,1)S(1)} %get-tuple-element.21), channel_id=1, source_target_pairs={{0,32},{32,64},{64,96},{96,128},{128,160},{160,192},{192,224},{1,3... | collective-permute-start | bytes 786440 | tf_op jit(solution)/shard_map/ppermute | solution.py:10
  70.8 5.5 %collective-permute-start.7 = (bf16[32,8,512]{2,1,0:T(8,128)(2,1)S(1)}, bf16[32,8,512]{2,1,0:T(8,128)(2,1)S(1)}, u32[]{:S(2)}, u32[]{:S(2)}) collective-permute-start(bf16[32,8,512]{2,1,0:T(8,128)(2,1)S(1)} %get-tuple-element.22), channel_id=1, source_target_pairs={{32,0},{64,32},{96,64},{128,96},{160,128},{192,160},{224,192},{33,... | collective-permute-start | bytes 786440 | tf_op jit(solution)/shard_map/ppermute | solution.py:10
  76.3 1.4 %pad_maximum_fusion = bf16[48,64,512]{2,1,0:T(8,128)(2,1)S(1)} fusion(bf16[48,16,512]{2,1,0:T(8,128)(2,1)} %collective-permute-done.3, bf16[16,32,512]{2,1,0:T(8,128)(2,1)S(1)} %collective-permute-done.1, bf16[16,32,512]{2,1,0:T(8,128)(2,1)S(1)} %bitcast.48, bf16[16,32,512]{2,1,0:T(8,128)(2,1)S(1)} %collective-permute-done, ...), kind=kLoop, calls=%fused_computation.1 | loop fusion | flops 15728640 | bytes 6291456 | tf_op jit(solution)/shard_map/concatenate | solution.py:83
  77.7 1.4 %fusion.46 = (bf16[20,64,512]{2,1,0:T(8,128)(2,1)S(1)}, bf16[20,64,512]{2,1,0:T(8,128)(2,1)S(1)}, bf16[20,64,512]{2,1,0:T(8,128)(2,1)S(1)}, bf16[20,64,512]{2,1,...) fusion(bf16[48,64,512]{2,1,0:T(8,128)(2,1)S(1)} %pad_maximum_fusion), kind=kLoop, calls=%fused_computation.69 | loop fusion | bytes 20971520 | tf_op jit(solution)/shard_map/slice | solution.py:47
  79.1 0.4 convolution_dynamic-update-slice_fusion.7
  79.5 0.5 convolution_dynamic-update-slice_fusion.6
  80.0 0.5 convolution_dynamic-update-slice_fusion.5
  80.4 0.5 convolution_dynamic-update-slice_fusion.4
  80.9 0.5 convolution_dynamic-update-slice_fusion.3
  81.4 0.4 convolution_dynamic-update-slice_fusion.2
  81.8 0.4 convolution_dynamic-update-slice_fusion.1
  82.3 0.4 convolution_dynamic-update-slice_fusion
  82.8 0.5 fusion
  83.3 0.5 fusion.47
  83.8 0.3 fusion.30
  85.2 1.5 %copy-done.2 = bf16[4096,512]{1,0:T(8,128)(2,1)S(1)} copy-done((bf16[4096,512]{1,0:T(8,128)(2,1)S(1)}, bf16[4096,512]{1,0:T(8,128)(2,1)}, u32[]{:S(2)}) %copy-start.2) | copy-done | bytes 4194328
  86.7 4.4 %convolution_convert_fusion = bf16[512,4096]{1,0:T(8,128)(2,1)} fusion(bf16[4096,512]{1,0:T(8,128)(2,1)S(1)} %copy-done.2, f32[128,512]{1,0:T(8,128)S(1)} %fusion.30, f32[128,512]{1,0:T(8,128)S(1)} %fusion.32, f32[128,512]{1,0:T(8,128)S(1)} %fusion.34, f32[128,512]{1,0:T(8,128)S(1)} %fusion.36, bf16[512,512]{1,0:T(8,128)(2,1)S(1)} %fusion.2), kind=kOutput, calls=%fused_computation | convolution fusion | flops 2151415808 | bytes 9961472 | tf_op jit(solution)/shard_map/dot_general | solution.py:90
  (23 shorter events, 1.9 us)
Async XLA Ops:
  0.0 13.3 %copy-start.1 = (bf16[17,17]{1,0:T(8,128)(2,1)S(1)}, bf16[17,17]{1,0:T(8,128)(2,1)}, u32[]{:S(2)}) copy-start(bf16[17,17]{1,0:T(8,128)(2,1)} %param.6) | copy-start | bytes 1738
  0.0 24.5 %copy-start = (bf16[512,16,32]{0,2,1:T(8,128)(2,1)S(1)}, bf16[512,16,32]{0,2,1:T(8,128)(2,1)}, u32[]{:S(2)}) copy-start(bf16[512,16,32]{0,2,1:T(8,128)(2,1)} %param.7) | copy-start | bytes 1572868
  5.9 16.8 %collective-permute-start = (bf16[16,32,512]{2,1,0:T(8,128)(2,1)S(1)}, bf16[16,32,512]{2,1,0:T(8,128)(2,1)S(1)}, u32[]{:S(2)}, u32[]{:S(2)}) collective-permute-start(bf16[16,32,512]{2,1,0:T(8,128)(2,1)S(1)} %bitcast.45), channel_id=1, source_target_pairs={{0,1},{1,2},{2,3},{3,4},{4,5},{5,6},{6,7},{7,8},{8,9},{9,10},{10,1... | collective-permute-start | bytes 1572872 | tf_op jit(solution)/shard_map/ppermute | solution.py:10
  11.3 13.2 %collective-permute-start.1 = (bf16[16,32,512]{2,1,0:T(8,128)(2,1)S(1)}, bf16[16,32,512]{2,1,0:T(8,128)(2,1)S(1)}, u32[]{:S(2)}, u32[]{:S(2)}) collective-permute-start(bf16[16,32,512]{2,1,0:T(8,128)(2,1)S(1)} %bitcast.46), channel_id=1, source_target_pairs={{1,0},{2,1},{3,2},{4,3},{5,4},{6,5},{7,6},{8,7},{9,8},{10,9},{11,1... | collective-permute-start | bytes 1572872 | tf_op jit(solution)/shard_map/ppermute | solution.py:10
  25.4 17.5 %collective-permute-start.4 = (bf16[8,32,512]{2,1,0:T(8,128)(2,1)}, bf16[8,32,512]{2,1,0:T(8,128)(2,1)S(1)}, u32[]{:S(2)}, u32[]{:S(2)}) collective-permute-start(bf16[8,32,512]{2,1,0:T(8,128)(2,1)} %get-tuple-element.24), channel_id=1, source_target_pairs={{0,1},{1,2},{2,3},{3,4},{4,5},{5,6},{6,7},{7,8},{8,9},{9,10},{10,1... | collective-permute-start | bytes 786440 | tf_op jit(solution)/shard_map/ppermute | solution.py:10
  30.3 46.0 %collective-permute-start.2 = (bf16[48,16,512]{2,1,0:T(8,128)(2,1)}, bf16[48,16,512]{2,1,0:T(8,128)(2,1)S(1)}, u32[]{:S(2)}, u32[]{:S(2)}) collective-permute-start(bf16[48,16,512]{2,1,0:T(8,128)(2,1)} %get-tuple-element.19), channel_id=1, source_target_pairs={{0,32},{32,64},{64,96},{96,128},{128,160},{160,192},{192,224},{1,3... | collective-permute-start | bytes 2359304 | tf_op jit(solution)/shard_map/ppermute | solution.py:10
  33.5 42.8 %collective-permute-start.3 = (bf16[48,16,512]{2,1,0:T(8,128)(2,1)}, bf16[48,16,512]{2,1,0:T(8,128)(2,1)}, u32[]{:S(2)}, u32[]{:S(2)}) collective-permute-start(bf16[48,16,512]{2,1,0:T(8,128)(2,1)} %get-tuple-element.20), channel_id=1, source_target_pairs={{32,0},{64,32},{96,64},{128,96},{160,128},{192,160},{224,192},{33,... | collective-permute-start | bytes 2359304 | tf_op jit(solution)/shard_map/ppermute | solution.py:10
  38.8 29.0 %collective-permute-start.5 = (bf16[8,32,512]{2,1,0:T(8,128)(2,1)}, bf16[8,32,512]{2,1,0:T(8,128)(2,1)}, u32[]{:S(2)}, u32[]{:S(2)}) collective-permute-start(bf16[8,32,512]{2,1,0:T(8,128)(2,1)} %get-tuple-element.23), channel_id=1, source_target_pairs={{1,0},{2,1},{3,2},{4,3},{5,4},{6,5},{7,6},{8,7},{9,8},{10,9},{11,1... | collective-permute-start | bytes 786440 | tf_op jit(solution)/shard_map/ppermute | solution.py:10
  68.9 13.9 %collective-permute-start.6 = (bf16[32,8,512]{2,1,0:T(8,128)(2,1)S(1)}, bf16[32,8,512]{2,1,0:T(8,128)(2,1)S(1)}, u32[]{:S(2)}, u32[]{:S(2)}) collective-permute-start(bf16[32,8,512]{2,1,0:T(8,128)(2,1)S(1)} %get-tuple-element.21), channel_id=1, source_target_pairs={{0,32},{32,64},{64,96},{96,128},{128,160},{160,192},{192,224},{1,3... | collective-permute-start | bytes 786440 | tf_op jit(solution)/shard_map/ppermute | solution.py:10
  70.8 12.0 %collective-permute-start.7 = (bf16[32,8,512]{2,1,0:T(8,128)(2,1)S(1)}, bf16[32,8,512]{2,1,0:T(8,128)(2,1)S(1)}, u32[]{:S(2)}, u32[]{:S(2)}) collective-permute-start(bf16[32,8,512]{2,1,0:T(8,128)(2,1)S(1)} %get-tuple-element.22), channel_id=1, source_target_pairs={{32,0},{64,32},{96,64},{128,96},{160,128},{192,160},{224,192},{33,... | collective-permute-start | bytes 786440 | tf_op jit(solution)/shard_map/ppermute | solution.py:10
  84.5 2.2 %copy-start.2 = (bf16[4096,512]{1,0:T(8,128)(2,1)S(1)}, bf16[4096,512]{1,0:T(8,128)(2,1)}, u32[]{:S(2)}) copy-start(bf16[4096,512]{1,0:T(8,128)(2,1)} %param.5) | copy-start | bytes 12582916

commit v12 on v3

--- a/solution.py
+++ b/solution.py
@@ -64,6 +64,7 @@
     waves = profile_basis.shape[1]
     h = point_spread.shape[0] // 2
     measured = window(observed.transpose(1, 2, 0), h)
+    measured, coefficients = lax.optimization_barrier((measured, coefficients))
     opacity = jnp.dot(
         coefficients.reshape(rows * cols, profiles), profile_basis, preferred_element_type=jnp.float32
     )

time: 74.7 us -> 100 us (1.34)
  the two profiles are of different devices: /device:TPU:29 before, /device:TPU:6 now
where the time goes in v12:
time: 100 us; the launch traced here: 99.5 us
  waiting for transfers between devices  45.9 us (46%)
  starting transfers between devices  26.8 us (27%)
  matrix products  15.1 us (15%)
  local copies, waits for them, and re-layouts  6.95 us (7%)
  other arithmetic  4.55 us (5%)
    ppermute x8, waiting for transfers between devices, send(): return lax.ppermute(block, axis, pairs)  45.9 us
    ppermute x8, starting transfers between devices, send(): return lax.ppermute(block, axis, pairs)  26.8 us
    dot_general x12, matrix products, blur(): jnp.dot(mat, flat[g * win_cols:g * win_cols + span], preferred_element_ty...  4.99 us
    dot_general x1, matrix products, shards(): jnp.dot(coefficients.reshape(rows * cols, profiles), profile_basis, prefe...  4.52 us
    dot_general x1, matrix products, shards(): lax.dot_general(tau_grad, profile_basis, (((1,), (1,)), ((), ())), prefer...  4.41 us
    concatenate x2, other arithmetic, window(): return jnp.concatenate([left, band, right], axis=1)  2.85 us
  transfers between devices with their start and end apart: 8, of which 8 were waited for; matrix products, arithmetic and copies ran while one was open for 2% of the time, Pallas kernels for 0%

profile of v12, /device:TPU:6, one launch (start us, length us, event | category | flops | bytes accessed | tf_op | source)
XLA Modules:
  0.0 99.5 jit_solution(11737340430918448439)
XLA Ops:
  0.0 1.2 %fusion.49 = (bf16[8,32,512]{2,1,0:T(8,128)(2,1)S(1)}, bf16[8,32,512]{2,1,0:T(8,128)(2,1)S(1)}) fusion(bf16[16,32,512]{2,1,0:T(8,128)(2,1)} %bitcast.42), kind=kLoop, calls=%fused_computation.73 | loop fusion | bytes 1048576 | tf_op jit(solution)/shard_map/slice | solution.py:15
  1.2 2.1 %collective-permute-start = (bf16[8,32,512]{2,1,0:T(8,128)(2,1)S(1)}, bf16[8,32,512]{2,1,0:T(8,128)(2,1)S(1)}, u32[]{:S(2)}, u32[]{:S(2)}) collective-permute-start(bf16[8,32,512]{2,1,0:T(8,128)(2,1)S(1)} %get-tuple-element.25), channel_id=1, source_target_pairs={{0,1},{1,2},{2,3},{3,4},{4,5},{5,6},{6,7},{7,8},{8,9},{9,10},{10,1... | collective-permute-start | bytes 786440 | tf_op jit(solution)/shard_map/ppermute | solution.py:10
  3.3 7.9 %collective-permute-start.1 = (bf16[8,32,512]{2,1,0:T(8,128)(2,1)S(1)}, bf16[8,32,512]{2,1,0:T(8,128)(2,1)S(1)}, u32[]{:S(2)}, u32[]{:S(2)}) collective-permute-start(bf16[8,32,512]{2,1,0:T(8,128)(2,1)S(1)} %get-tuple-element.26), channel_id=1, source_target_pairs={{1,0},{2,1},{3,2},{4,3},{5,4},{6,5},{7,6},{8,7},{9,8},{10,9},{11,1... | collective-permute-start | bytes 786440 | tf_op jit(solution)/shard_map/ppermute | solution.py:10
  11.2 2.7 %collective-permute-done = bf16[8,32,512]{2,1,0:T(8,128)(2,1)S(1)} collective-permute-done((bf16[8,32,512]{2,1,0:T(8,128)(2,1)S(1)}, bf16[8,32,512]{2,1,0:T(8,128)(2,1)S(1)}, u32[]{:S(2)}, u32[]{:S(2)}) %collective-permute-start) | collective-permute-done | bytes 262176 | tf_op jit(solution)/shard_map/ppermute | solution.py:10
  13.9 4.0 %collective-permute-done.1 = bf16[8,32,512]{2,1,0:T(8,128)(2,1)S(1)} collective-permute-done((bf16[8,32,512]{2,1,0:T(8,128)(2,1)S(1)}, bf16[8,32,512]{2,1,0:T(8,128)(2,1)S(1)}, u32[]{:S(2)}, u32[]{:S(2)}) %collective-permute-start.1) | collective-permute-done | bytes 262176 | tf_op jit(solution)/shard_map/ppermute | solution.py:10
  17.9 1.0 %pad_maximum_fusion.5 = (bf16[32,8,512]{2,1,0:T(8,128)(2,1)S(1)}, bf16[32,8,512]{2,1,0:T(8,128)(2,1)S(1)}) fusion(bf16[8,32,512]{2,1,0:T(8,128)(2,1)S(1)} %collective-permute-done.1, bf16[16,32,512]{2,1,0:T(8,128)(2,1)} %bitcast.43, bf16[8,32,512]{2,1,0:T(8,128)(2,1)S(1)} %collective-permute-done), kind=kLoop, calls=%fused_computation.57 | loop fusion | flops 1572864 | bytes 1572864 | tf_op jit(solution)/shard_map/slice | solution.py:18
  18.9 3.5 %collective-permute-start.2 = (bf16[32,8,512]{2,1,0:T(8,128)(2,1)S(1)}, bf16[32,8,512]{2,1,0:T(8,128)(2,1)S(1)}, u32[]{:S(2)}, u32[]{:S(2)}) collective-permute-start(bf16[32,8,512]{2,1,0:T(8,128)(2,1)S(1)} %get-tuple-element.23), channel_id=1, source_target_pairs={{0,32},{32,64},{64,96},{96,128},{128,160},{160,192},{192,224},{1,3... | collective-permute-start | bytes 786440 | tf_op jit(solution)/shard_map/ppermute | solution.py:10
  22.4 1.3 %collective-permute-start.3 = (bf16[32,8,512]{2,1,0:T(8,128)(2,1)S(1)}, bf16[32,8,512]{2,1,0:T(8,128)(2,1)S(1)}, u32[]{:S(2)}, u32[]{:S(2)}) collective-permute-start(bf16[32,8,512]{2,1,0:T(8,128)(2,1)S(1)} %get-tuple-element.24), channel_id=1, source_target_pairs={{32,0},{64,32},{96,64},{128,96},{160,128},{192,160},{224,192},{33,... | collective-permute-start | bytes 786440 | tf_op jit(solution)/shard_map/ppermute | solution.py:10
  23.7 4.6 %collective-permute-done.2 = bf16[32,8,512]{2,1,0:T(8,128)(2,1)S(1)} collective-permute-done((bf16[32,8,512]{2,1,0:T(8,128)(2,1)S(1)}, bf16[32,8,512]{2,1,0:T(8,128)(2,1)S(1)}, u32[]{:S(2)}, u32[]{:S(2)}) %collective-permute-start.2) | collective-permute-done | bytes 262176 | tf_op jit(solution)/shard_map/ppermute | solution.py:10
  28.3 4.1 %collective-permute-done.3 = bf16[32,8,512]{2,1,0:T(8,128)(2,1)S(1)} collective-permute-done((bf16[32,8,512]{2,1,0:T(8,128)(2,1)S(1)}, bf16[32,8,512]{2,1,0:T(8,128)(2,1)S(1)}, u32[]{:S(2)}, u32[]{:S(2)}) %collective-permute-start.3) | collective-permute-done | bytes 262176 | tf_op jit(solution)/shard_map/ppermute | solution.py:10
  32.4 1.2 %pad_maximum_fusion.1 = bf16[32,48,512]{2,1,0:T(8,128)(2,1)S(1)} fusion(bf16[32,8,512]{2,1,0:T(8,128)(2,1)S(1)} %collective-permute-done.3, bf16[8,32,512]{2,1,0:T(8,128)(2,1)S(1)} %collective-permute-done.1, bf16[16,32,512]{2,1,0:T(8,128)(2,1)} %bitcast.44, bf16[8,32,512]{2,1,0:T(8,128)(2,1)S(1)} %collective-permute-done, ...), kind=kLoop, calls=%fused_computation.4 | loop fusion | flops 7864320 | bytes 3145728 | tf_op jit(solution)/shard_map/concatenate | solution.py:20
  33.7 4.5 %fusion.2 = bf16[512,512]{1,0:T(8,128)(2,1)S(1)} fusion(bf16[512,4096]{1,0:T(8,128)(2,1)S(1)} %bitcast.62, bf16[4096,512]{1,0:T(8,128)(2,1)} %param.5), kind=kOutput, calls=%fused_computation.12 | convolution fusion | flops 2148007936 | bytes 8912896 | tf_op jit(solution)/shard_map/dot_general | solution.py:68
  38.2 1.9 %collective-permute-start.4 = (bf16[16,32,512]{2,1,0:T(8,128)(2,1)S(1)}, bf16[16,32,512]{2,1,0:T(8,128)(2,1)S(1)}, u32[]{:S(2)}, u32[]{:S(2)}) collective-permute-start(bf16[16,32,512]{2,1,0:T(8,128)(2,1)S(1)} %bitcast.46), channel_id=1, source_target_pairs={{0,1},{1,2},{2,3},{3,4},{4,5},{5,6},{6,7},{7,8},{8,9},{9,10},{10,1... | collective-permute-start | bytes 1572872 | tf_op jit(solution)/shard_map/ppermute | solution.py:10
  40.2 6.7 %collective-permute-start.5 = (bf16[16,32,512]{2,1,0:T(8,128)(2,1)S(1)}, bf16[16,32,512]{2,1,0:T(8,128)(2,1)S(1)}, u32[]{:S(2)}, u32[]{:S(2)}) collective-permute-start(bf16[16,32,512]{2,1,0:T(8,128)(2,1)S(1)} %bitcast.47), channel_id=1, source_target_pairs={{1,0},{2,1},{3,2},{4,3},{5,4},{6,5},{7,6},{8,7},{9,8},{10,9},{11,1... | collective-permute-start | bytes 1572872 | tf_op jit(solution)/shard_map/ppermute | solution.py:10
  46.8 10.2 %collective-permute-done.4 = bf16[16,32,512]{2,1,0:T(8,128)(2,1)S(1)} collective-permute-done((bf16[16,32,512]{2,1,0:T(8,128)(2,1)S(1)}, bf16[16,32,512]{2,1,0:T(8,128)(2,1)S(1)}, u32[]{:S(2)}, u32[]{:S(2)}) %collective-permute-start.4) | collective-permute-done | bytes 524320 | tf_op jit(solution)/shard_map/ppermute | solution.py:10
  57.0 2.2 %collective-permute-done.5 = bf16[16,32,512]{2,1,0:T(8,128)(2,1)S(1)} collective-permute-done((bf16[16,32,512]{2,1,0:T(8,128)(2,1)S(1)}, bf16[16,32,512]{2,1,0:T(8,128)(2,1)S(1)}, u32[]{:S(2)}, u32[]{:S(2)}) %collective-permute-start.5) | collective-permute-done | bytes 524320 | tf_op jit(solution)/shard_map/ppermute | solution.py:10
  59.4 1.3 %fusion.48 = (bf16[48,16,512]{2,1,0:T(8,128)(2,1)}, bf16[48,16,512]{2,1,0:T(8,128)(2,1)}) fusion(bf16[48,32,512]{2,1,0:T(8,128)(2,1)S(1)} %pad_maximum_fusion.2), kind=kLoop, calls=%fused_computation.72 | loop fusion | bytes 3145728 | tf_op jit(solution)/shard_map/slice | solution.py:18
  60.7 2.2 %collective-permute-start.6 = (bf16[48,16,512]{2,1,0:T(8,128)(2,1)}, bf16[48,16,512]{2,1,0:T(8,128)(2,1)}, u32[]{:S(2)}, u32[]{:S(2)}) collective-permute-start(bf16[48,16,512]{2,1,0:T(8,128)(2,1)} %get-tuple-element.21), channel_id=1, source_target_pairs={{0,32},{32,64},{64,96},{96,128},{128,160},{160,192},{192,224},{1,3... | collective-permute-start | bytes 2359304 | tf_op jit(solution)/shard_map/ppermute | solution.py:10
  62.8 1.3 %collective-permute-start.7 = (bf16[48,16,512]{2,1,0:T(8,128)(2,1)}, bf16[48,16,512]{2,1,0:T(8,128)(2,1)}, u32[]{:S(2)}, u32[]{:S(2)}) collective-permute-start(bf16[48,16,512]{2,1,0:T(8,128)(2,1)} %get-tuple-element.22), channel_id=1, source_target_pairs={{32,0},{64,32},{96,64},{128,96},{160,128},{192,160},{224,192},{33,... | collective-permute-start | bytes 2359304 | tf_op jit(solution)/shard_map/ppermute | solution.py:10
  64.4 0.7 rev.3
  65.3 0.9 fusion.4
  66.5 13.1 %collective-permute-done.6 = bf16[48,16,512]{2,1,0:T(8,128)(2,1)} collective-permute-done((bf16[48,16,512]{2,1,0:T(8,128)(2,1)}, bf16[48,16,512]{2,1,0:T(8,128)(2,1)}, u32[]{:S(2)}, u32[]{:S(2)}) %collective-permute-start.6) | collective-permute-done | bytes 786464 | tf_op jit(solution)/shard_map/ppermute | solution.py:10
  79.5 5.0 %collective-permute-done.7 = bf16[48,16,512]{2,1,0:T(8,128)(2,1)} collective-permute-done((bf16[48,16,512]{2,1,0:T(8,128)(2,1)}, bf16[48,16,512]{2,1,0:T(8,128)(2,1)}, u32[]{:S(2)}, u32[]{:S(2)}) %collective-permute-start.7) | collective-permute-done | bytes 786464 | tf_op jit(solution)/shard_map/ppermute | solution.py:10
  84.5 1.6 %pad_maximum_fusion = bf16[48,64,512]{2,1,0:T(8,128)(2,1)S(1)} fusion(bf16[48,16,512]{2,1,0:T(8,128)(2,1)} %collective-permute-done.7, bf16[16,32,512]{2,1,0:T(8,128)(2,1)S(1)} %collective-permute-done.5, bf16[16,32,512]{2,1,0:T(8,128)(2,1)S(1)} %bitcast.49, bf16[16,32,512]{2,1,0:T(8,128)(2,1)S(1)} %collective-permute-done.4, ...), kind=kLoop, calls=%fused_computation.1 | loop fusion | flops 15728640 | bytes 6291456 | tf_op jit(solution)/shard_map/concatenate | solution.py:20
  86.1 1.4 %fusion.46 = (bf16[20,64,512]{2,1,0:T(8,128)(2,1)S(1)}, bf16[20,64,512]{2,1,0:T(8,128)(2,1)S(1)}, bf16[20,64,512]{2,1,0:T(8,128)(2,1)S(1)}, bf16[20,64,512]{2,1,...) fusion(bf16[48,64,512]{2,1,0:T(8,128)(2,1)S(1)} %pad_maximum_fusion), kind=kLoop, calls=%fused_computation.70 | loop fusion | bytes 20971520 | tf_op jit(solution)/shard_map/slice | solution.py:45
  88.0 0.5 convolution_dynamic-update-slice_fusion.6
  88.5 0.5 convolution_dynamic-update-slice_fusion.5
  88.9 0.5 convolution_dynamic-update-slice_fusion.4
  89.4 0.5 convolution_dynamic-update-slice_fusion.3
  91.6 0.5 fusion.47
  93.6 1.5 %copy-done.2 = bf16[4096,512]{1,0:T(8,128)(2,1)S(1)} copy-done((bf16[4096,512]{1,0:T(8,128)(2,1)S(1)}, bf16[4096,512]{1,0:T(8,128)(2,1)}, u32[]{:S(2)}) %copy-start.2) | copy-done | bytes 4194328
  95.1 4.4 %convolution_convert_fusion = bf16[512,4096]{1,0:T(8,128)(2,1)} fusion(bf16[4096,512]{1,0:T(8,128)(2,1)S(1)} %copy-done.2, f32[128,512]{1,0:T(8,128)S(1)} %fusion.30, f32[128,512]{1,0:T(8,128)S(1)} %fusion.32, f32[128,512]{1,0:T(8,128)S(1)} %fusion.34, f32[128,512]{1,0:T(8,128)S(1)} %fusion.36, bf16[512,512]{1,0:T(8,128)(2,1)S(1)} %fusion.2), kind=kOutput, calls=%fused_computation | convolution fusion | flops 2151415808 | bytes 9961472 | tf_op jit(solution)/shard_map/dot_general | solution.py:82
  (21 shorter events, 4.5 us)
Async XLA Ops:
  0.0 33.7 %copy-start.1 = (bf16[16,32,4096]{2,1,0:T(8,128)(2,1)S(1)}, bf16[16,32,4096]{2,1,0:T(8,128)(2,1)}, u32[]{:S(2)}) copy-start(bf16[16,32,4096]{2,1,0:T(8,128)(2,1)} %param.4) | copy-start | bytes 12582916
  1.2 12.7 %collective-permute-start = (bf16[8,32,512]{2,1,0:T(8,128)(2,1)S(1)}, bf16[8,32,512]{2,1,0:T(8,128)(2,1)S(1)}, u32[]{:S(2)}, u32[]{:S(2)}) collective-permute-start(bf16[8,32,512]{2,1,0:T(8,128)(2,1)S(1)} %get-tuple-element.25), channel_id=1, source_target_pairs={{0,1},{1,2},{2,3},{3,4},{4,5},{5,6},{6,7},{7,8},{8,9},{9,10},{10,1... | collective-permute-start | bytes 786440 | tf_op jit(solution)/shard_map/ppermute | solution.py:10
  3.3 14.6 %collective-permute-start.1 = (bf16[8,32,512]{2,1,0:T(8,128)(2,1)S(1)}, bf16[8,32,512]{2,1,0:T(8,128)(2,1)S(1)}, u32[]{:S(2)}, u32[]{:S(2)}) collective-permute-start(bf16[8,32,512]{2,1,0:T(8,128)(2,1)S(1)} %get-tuple-element.26), channel_id=1, source_target_pairs={{1,0},{2,1},{3,2},{4,3},{5,4},{6,5},{7,6},{8,7},{9,8},{10,9},{11,1... | collective-permute-start | bytes 786440 | tf_op jit(solution)/shard_map/ppermute | solution.py:10
  18.9 9.4 %collective-permute-start.2 = (bf16[32,8,512]{2,1,0:T(8,128)(2,1)S(1)}, bf16[32,8,512]{2,1,0:T(8,128)(2,1)S(1)}, u32[]{:S(2)}, u32[]{:S(2)}) collective-permute-start(bf16[32,8,512]{2,1,0:T(8,128)(2,1)S(1)} %get-tuple-element.23), channel_id=1, source_target_pairs={{0,32},{32,64},{64,96},{96,128},{128,160},{160,192},{192,224},{1,3... | collective-permute-start | bytes 786440 | tf_op jit(solution)/shard_map/ppermute | solution.py:10
  22.4 10.0 %collective-permute-start.3 = (bf16[32,8,512]{2,1,0:T(8,128)(2,1)S(1)}, bf16[32,8,512]{2,1,0:T(8,128)(2,1)S(1)}, u32[]{:S(2)}, u32[]{:S(2)}) collective-permute-start(bf16[32,8,512]{2,1,0:T(8,128)(2,1)S(1)} %get-tuple-element.24), channel_id=1, source_target_pairs={{32,0},{64,32},{96,64},{128,96},{160,128},{192,160},{224,192},{33,... | collective-permute-start | bytes 786440 | tf_op jit(solution)/shard_map/ppermute | solution.py:10
  38.2 25.9 %copy-start = (bf16[17,17]{1,0:T(8,128)(2,1)S(1)}, bf16[17,17]{1,0:T(8,128)(2,1)}, u32[]{:S(2)}) copy-start(bf16[17,17]{1,0:T(8,128)(2,1)} %param.6) | copy-start | bytes 1738
  38.2 18.8 %collective-permute-start.4 = (bf16[16,32,512]{2,1,0:T(8,128)(2,1)S(1)}, bf16[16,32,512]{2,1,0:T(8,128)(2,1)S(1)}, u32[]{:S(2)}, u32[]{:S(2)}) collective-permute-start(bf16[16,32,512]{2,1,0:T(8,128)(2,1)S(1)} %bitcast.46), channel_id=1, source_target_pairs={{0,1},{1,2},{2,3},{3,4},{4,5},{5,6},{6,7},{7,8},{8,9},{9,10},{10,1... | collective-permute-start | bytes 1572872 | tf_op jit(solution)/shard_map/ppermute | solution.py:10
  40.2 19.0 %collective-permute-start.5 = (bf16[16,32,512]{2,1,0:T(8,128)(2,1)S(1)}, bf16[16,32,512]{2,1,0:T(8,128)(2,1)S(1)}, u32[]{:S(2)}, u32[]{:S(2)}) collective-permute-start(bf16[16,32,512]{2,1,0:T(8,128)(2,1)S(1)} %bitcast.47), channel_id=1, source_target_pairs={{1,0},{2,1},{3,2},{4,3},{5,4},{6,5},{7,6},{8,7},{9,8},{10,9},{11,1... | collective-permute-start | bytes 1572872 | tf_op jit(solution)/shard_map/ppermute | solution.py:10
  60.7 18.9 %collective-permute-start.6 = (bf16[48,16,512]{2,1,0:T(8,128)(2,1)}, bf16[48,16,512]{2,1,0:T(8,128)(2,1)}, u32[]{:S(2)}, u32[]{:S(2)}) collective-permute-start(bf16[48,16,512]{2,1,0:T(8,128)(2,1)} %get-tuple-element.21), channel_id=1, source_target_pairs={{0,32},{32,64},{64,96},{96,128},{128,160},{160,192},{192,224},{1,3... | collective-permute-start | bytes 2359304 | tf_op jit(solution)/shard_map/ppermute | solution.py:10
  62.8 21.7 %collective-permute-start.7 = (bf16[48,16,512]{2,1,0:T(8,128)(2,1)}, bf16[48,16,512]{2,1,0:T(8,128)(2,1)}, u32[]{:S(2)}, u32[]{:S(2)}) collective-permute-start(bf16[48,16,512]{2,1,0:T(8,128)(2,1)} %get-tuple-element.22), channel_id=1, source_target_pairs={{32,0},{64,32},{96,64},{128,96},{160,128},{192,160},{224,192},{33,... | collective-permute-start | bytes 2359304 | tf_op jit(solution)/shard_map/ppermute | solution.py:10
  92.9 2.2 %copy-start.2 = (bf16[4096,512]{1,0:T(8,128)(2,1)S(1)}, bf16[4096,512]{1,0:T(8,128)(2,1)}, u32[]{:S(2)}) copy-start(bf16[4096,512]{1,0:T(8,128)(2,1)} %param.5) | copy-start | bytes 12582916

commit v13 on v11

--- a/solution.py
+++ b/solution.py
@@ -10,10 +10,8 @@
     return lax.ppermute(block, axis, pairs)
 
 
-def window(block, h, after=None):
+def window(block, h):
     rows, cols = block.shape[0], block.shape[1]
-    if after is not None:
-        after, block = lax.optimization_barrier((after, block))
     top = send(block[rows - h :], "tile", 1)
     bottom = send(block[:h], "tile", -1)
     band = jnp.concatenate([top, block, bottom], axis=0)
@@ -65,6 +63,7 @@
     rows, cols, profiles = coefficients.shape
     waves = profile_basis.shape[1]
     h = point_spread.shape[0] // 2
+    measured = window(observed.transpose(1, 2, 0), h)
     opacity = jnp.dot(
         coefficients.reshape(rows * cols, profiles), profile_basis, preferred_element_type=jnp.float32
     )
@@ -76,8 +75,8 @@
     wide = 2 * h
     top = send(block[rows - wide :], "tile", 1)
     bottom = send(block[:wide], "tile", -1)
-    measured = window(observed.transpose(1, 2, 0), h, (top, bottom))
     band = jnp.concatenate([top, block, bottom], axis=0)
+    measured, band = lax.optimization_barrier((measured, band))
     left = send(band[:, cols - wide :], "wave", 1)
     right = send(band[:, :wide], "wave", -1)
     near = jnp.concatenate([left, band, right], axis=1)

time: 91.5 us -> 84.6 us (0.925)
  the two profiles are of different devices: /device:TPU:35 before, /device:TPU:30 now
where the time goes in v13:
time: 84.6 us; the launch traced here: 82.9 us
  starting transfers between devices  30.1 us (36%)
  waiting for transfers between devices  25.3 us (30%)
  matrix products  16.4 us (19%)
  local copies, waits for them, and re-layouts  9.91 us (12%)
  other arithmetic  0.9 us (1%)
    ppermute x8, starting transfers between devices, send(): return lax.ppermute(block, axis, pairs)  30.1 us
    ppermute x8, waiting for transfers between devices, send(): return lax.ppermute(block, axis, pairs)  25.3 us
    dot_general x1, matrix products, shards(): jnp.dot(coefficients.reshape(rows * cols, profiles), profile_basis, prefe...  5.84 us
    dot_general x12, matrix products, blur(): jnp.dot(mat, flat[g * win_cols:g * win_cols + span], preferred_element_ty...  4.98 us
    dot_general x1, matrix products, shards(): lax.dot_general(tau_grad, profile_basis, (((1,), (1,)), ((), ())), prefer...  4.4 us
    unnamed x12, local copies, waits for them, and re-layouts  3.05 us
    slice x2, local copies, waits for them, and re-layouts, blur(): flat[g * win_cols:g * win_cols + span]  1.93 us
  transfers between devices with their start and end apart: 8, of which 4 were waited for; matrix products, arithmetic and copies ran while one was open for 12% of the time, Pallas kernels for 0%

profile of v13, /device:TPU:30, one launch (start us, length us, event | category | flops | bytes accessed | tf_op | source)
XLA Modules:
  0.0 82.9 jit_solution(16580068037962192965)
XLA Ops:
  0.0 1.1 %fusion.49 = (bf16[8,32,512]{2,1,0:T(8,128)(2,1)S(1)}, bf16[8,32,512]{2,1,0:T(8,128)(2,1)S(1)}) fusion(bf16[16,32,512]{2,1,0:T(8,128)(2,1)} %bitcast.42), kind=kLoop, calls=%fused_computation.75 | loop fusion | bytes 1048576 | tf_op jit(solution)/shard_map/slice | solution.py:15
  1.1 1.9 %collective-permute-start = (bf16[8,32,512]{2,1,0:T(8,128)(2,1)S(1)}, bf16[8,32,512]{2,1,0:T(8,128)(2,1)S(1)}, u32[]{:S(2)}, u32[]{:S(2)}) collective-permute-start(bf16[8,32,512]{2,1,0:T(8,128)(2,1)S(1)} %get-tuple-element.25), channel_id=1, source_target_pairs={{0,1},{1,2},{2,3},{3,4},{4,5},{5,6},{6,7},{7,8},{8,9},{9,10},{10,1... | collective-permute-start | bytes 786440 | tf_op jit(solution)/shard_map/ppermute | solution.py:10
  3.0 7.9 %collective-permute-start.1 = (bf16[8,32,512]{2,1,0:T(8,128)(2,1)S(1)}, bf16[8,32,512]{2,1,0:T(8,128)(2,1)S(1)}, u32[]{:S(2)}, u32[]{:S(2)}) collective-permute-start(bf16[8,32,512]{2,1,0:T(8,128)(2,1)S(1)} %get-tuple-element.26), channel_id=1, source_target_pairs={{1,0},{2,1},{3,2},{4,3},{5,4},{6,5},{7,6},{8,7},{9,8},{10,9},{11,1... | collective-permute-start | bytes 786440 | tf_op jit(solution)/shard_map/ppermute | solution.py:10
  10.9 5.8 %fusion.2 = bf16[512,512]{1,0:T(8,128)(2,1)S(1)} fusion(bf16[512,4096]{1,0:T(8,128)(2,1)} %bitcast.61, bf16[4096,512]{1,0:T(8,128)(2,1)} %param.5), kind=kOutput, calls=%fused_computation.11 | convolution fusion | flops 2148007936 | bytes 8912896 | tf_op jit(solution)/shard_map/dot_general | solution.py:67
  16.8 1.9 %collective-permute-start.4 = (bf16[16,32,512]{2,1,0:T(8,128)(2,1)S(1)}, bf16[16,32,512]{2,1,0:T(8,128)(2,1)S(1)}, u32[]{:S(2)}, u32[]{:S(2)}) collective-permute-start(bf16[16,32,512]{2,1,0:T(8,128)(2,1)S(1)} %bitcast.58), channel_id=1, source_target_pairs={{0,1},{1,2},{2,3},{3,4},{4,5},{5,6},{6,7},{7,8},{8,9},{9,10},{10,1... | collective-permute-start | bytes 1572872 | tf_op jit(solution)/shard_map/ppermute | solution.py:10
  18.7 6.7 %collective-permute-start.5 = (bf16[16,32,512]{2,1,0:T(8,128)(2,1)S(1)}, bf16[16,32,512]{2,1,0:T(8,128)(2,1)S(1)}, u32[]{:S(2)}, u32[]{:S(2)}) collective-permute-start(bf16[16,32,512]{2,1,0:T(8,128)(2,1)S(1)} %bitcast.59), channel_id=1, source_target_pairs={{1,0},{2,1},{3,2},{4,3},{5,4},{6,5},{7,6},{8,7},{9,8},{10,9},{11,1... | collective-permute-start | bytes 1572872 | tf_op jit(solution)/shard_map/ppermute | solution.py:10
  25.5 2.6 %collective-permute-start.2 = (bf16[32,8,512]{2,1,0:T(8,128)(2,1)S(1)}, bf16[32,8,512]{2,1,0:T(8,128)(2,1)S(1)}, u32[]{:S(2)}, u32[]{:S(2)}) collective-permute-start(bf16[32,8,512]{2,1,0:T(8,128)(2,1)S(1)} %get-tuple-element.23), channel_id=1, source_target_pairs={{0,32},{32,64},{64,96},{96,128},{128,160},{160,192},{192,224},{1,3... | collective-permute-start | bytes 786440 | tf_op jit(solution)/shard_map/ppermute | solution.py:10
  28.1 3.3 %collective-permute-start.3 = (bf16[32,8,512]{2,1,0:T(8,128)(2,1)S(1)}, bf16[32,8,512]{2,1,0:T(8,128)(2,1)S(1)}, u32[]{:S(2)}, u32[]{:S(2)}) collective-permute-start(bf16[32,8,512]{2,1,0:T(8,128)(2,1)S(1)} %get-tuple-element.24), channel_id=1, source_target_pairs={{32,0},{64,32},{96,64},{128,96},{160,128},{192,160},{224,192},{33,... | collective-permute-start | bytes 786440 | tf_op jit(solution)/shard_map/ppermute | solution.py:10
  31.3 2.4 %collective-permute-done.2 = bf16[32,8,512]{2,1,0:T(8,128)(2,1)S(1)} collective-permute-done((bf16[32,8,512]{2,1,0:T(8,128)(2,1)S(1)}, bf16[32,8,512]{2,1,0:T(8,128)(2,1)S(1)}, u32[]{:S(2)}, u32[]{:S(2)}) %collective-permute-start.2) | collective-permute-done | bytes 262176 | tf_op jit(solution)/shard_map/ppermute | solution.py:10
  33.7 9.3 %collective-permute-done.3 = bf16[32,8,512]{2,1,0:T(8,128)(2,1)S(1)} collective-permute-done((bf16[32,8,512]{2,1,0:T(8,128)(2,1)S(1)}, bf16[32,8,512]{2,1,0:T(8,128)(2,1)S(1)}, u32[]{:S(2)}, u32[]{:S(2)}) %collective-permute-start.3) | collective-permute-done | bytes 262176 | tf_op jit(solution)/shard_map/ppermute | solution.py:10
  43.4 1.3 %fusion.48 = (bf16[48,16,512]{2,1,0:T(8,128)(2,1)}, bf16[48,16,512]{2,1,0:T(8,128)(2,1)}) fusion(bf16[48,32,512]{2,1,0:T(8,128)(2,1)S(1)} %pad_maximum_fusion.1), kind=kLoop, calls=%fused_computation.74 | loop fusion | bytes 3145728 | tf_op jit(solution)/shard_map/slice | solution.py:81
  44.7 1.9 %collective-permute-start.6 = (bf16[48,16,512]{2,1,0:T(8,128)(2,1)}, bf16[48,16,512]{2,1,0:T(8,128)(2,1)}, u32[]{:S(2)}, u32[]{:S(2)}) collective-permute-start(bf16[48,16,512]{2,1,0:T(8,128)(2,1)} %get-tuple-element.22), channel_id=1, source_target_pairs={{0,32},{32,64},{64,96},{96,128},{128,160},{160,192},{192,224},{1,3... | collective-permute-start | bytes 2359304 | tf_op jit(solution)/shard_map/ppermute | solution.py:10
  47.0 3.9 %collective-permute-start.7 = (bf16[48,16,512]{2,1,0:T(8,128)(2,1)}, bf16[48,16,512]{2,1,0:T(8,128)(2,1)}, u32[]{:S(2)}, u32[]{:S(2)}) collective-permute-start(bf16[48,16,512]{2,1,0:T(8,128)(2,1)} %get-tuple-element.21), channel_id=1, source_target_pairs={{32,0},{64,32},{96,64},{128,96},{160,128},{192,160},{224,192},{33,... | collective-permute-start | bytes 2359304 | tf_op jit(solution)/shard_map/ppermute | solution.py:10
  50.9 0.9 %fusion.4 = bf16[32,17,48]{2,1,0:T(8,128)(2,1)} fusion(bf16[17,17]{1,0:T(8,128)(2,1)S(1)} %rev.3), kind=kOutput, calls=%fused_computation.23 | convolution fusion | flops 966144 | bytes 52802 | tf_op jit(solution)/shard_map/ab,xbX->xaX/dot_general | solution.py:29
  52.0 1.1 %reshape.74 = bf16[32,816]{1,0:T(8,128)(2,1)S(1)} reshape(bf16[32,17,48]{2,1,0:T(8,128)(2,1)} %fusion.4) | data formatting | bytes 104448 | tf_op jit(solution)/shard_map/reshape | solution.py:30
  53.2 10.6 %collective-permute-done.6 = bf16[48,16,512]{2,1,0:T(8,128)(2,1)} collective-permute-done((bf16[48,16,512]{2,1,0:T(8,128)(2,1)}, bf16[48,16,512]{2,1,0:T(8,128)(2,1)}, u32[]{:S(2)}, u32[]{:S(2)}) %collective-permute-start.6) | collective-permute-done | bytes 786464 | tf_op jit(solution)/shard_map/ppermute | solution.py:10
  63.8 1.2 %constant_dynamic-update-slice_fusion.2 = bf16[48,64,512]{2,1,0:T(8,128)(2,1)S(1)} fusion(bf16[48,16,512]{2,1,0:T(8,128)(2,1)} %collective-permute-done.6), kind=kLoop, calls=%fused_computation.59 | loop fusion | bytes 1572864
  65.2 3.0 %collective-permute-done.7 = bf16[48,16,512]{2,1,0:T(8,128)(2,1)} collective-permute-done((bf16[48,16,512]{2,1,0:T(8,128)(2,1)}, bf16[48,16,512]{2,1,0:T(8,128)(2,1)}, u32[]{:S(2)}, u32[]{:S(2)}) %collective-permute-start.7) | collective-permute-done | bytes 786464 | tf_op jit(solution)/shard_map/ppermute | solution.py:10
  68.2 1.2 %constant_dynamic-update-slice_fusion = bf16[48,64,512]{2,1,0:T(8,128)(2,1)S(1)} fusion(bf16[48,64,512]{2,1,0:T(8,128)(2,1)S(1)} %constant_dynamic-update-slice_fusion.1, bf16[48,16,512]{2,1,0:T(8,128)(2,1)} %collective-permute-done.7), kind=kLoop, calls=%fused_computation.57 | loop fusion | bytes 1572864 | tf_op jit(solution)/shard_map/concatenate | solution.py:82
  69.4 1.4 %fusion.46 = (bf16[20,64,512]{2,1,0:T(8,128)(2,1)S(1)}, bf16[20,64,512]{2,1,0:T(8,128)(2,1)S(1)}, bf16[20,64,512]{2,1,0:T(8,128)(2,1)S(1)}, bf16[20,64,512]{2,1,...) fusion(bf16[48,64,512]{2,1,0:T(8,128)(2,1)S(1)} %constant_dynam, ...), kind=kLoop, calls=%fused_computation.72 | loop fusion | bytes 20971520 | tf_op jit(solution)/shard_map/slice | solution.py:45
  70.8 0.5 convolution_dynamic-update-slice_fusion.7
  71.2 0.5 convolution_dynamic-update-slice_fusion.6
  71.7 0.4 convolution_dynamic-update-slice_fusion.5
  72.1 0.4 convolution_dynamic-update-slice_fusion.4
  72.6 0.4 convolution_dynamic-update-slice_fusion.3
  73.1 0.4 convolution_dynamic-update-slice_fusion.2
  73.5 0.4 convolution_dynamic-update-slice_fusion.1
  74.0 0.4 convolution_dynamic-update-slice_fusion
  74.4 0.4 fusion
  74.9 0.5 fusion.47
  76.8 1.5 %copy-done.4 = bf16[4096,512]{1,0:T(8,128)(2,1)S(1)} copy-done((bf16[4096,512]{1,0:T(8,128)(2,1)S(1)}, bf16[4096,512]{1,0:T(8,128)(2,1)}, u32[]{:S(2)}) %copy-start.4) | copy-done | bytes 4194328
  78.5 4.4 %convolution_convert_fusion = bf16[512,4096]{1,0:T(8,128)(2,1)} fusion(bf16[4096,512]{1,0:T(8,128)(2,1)S(1)} %copy-done.4, f32[128,512]{1,0:T(8,128)S(1)} %fusion.30, f32[128,512]{1,0:T(8,128)S(1)} %fusion.32, f32[128,512]{1,0:T(8,128)S(1)} %fusion.34, f32[128,512]{1,0:T(8,128)S(1)} %fusion.36, bf16[512,512]{1,0:T(8,128)(2,1)S(1)} %copy-done.2), kind=kOutput, calls=%fused_computation | convolution fusion | flops 2151415808 | bytes 9961472 | tf_op jit(solution)/shard_map/dot_general | solution.py:89
  (27 shorter events, 2.8 us)
Async XLA Ops:
  1.1 24.3 %collective-permute-start = (bf16[8,32,512]{2,1,0:T(8,128)(2,1)S(1)}, bf16[8,32,512]{2,1,0:T(8,128)(2,1)S(1)}, u32[]{:S(2)}, u32[]{:S(2)}) collective-permute-start(bf16[8,32,512]{2,1,0:T(8,128)(2,1)S(1)} %get-tuple-element.25), channel_id=1, source_target_pairs={{0,1},{1,2},{2,3},{3,4},{4,5},{5,6},{6,7},{7,8},{8,9},{9,10},{10,1... | collective-permute-start | bytes 786440 | tf_op jit(solution)/shard_map/ppermute | solution.py:10
  3.0 22.4 %collective-permute-start.1 = (bf16[8,32,512]{2,1,0:T(8,128)(2,1)S(1)}, bf16[8,32,512]{2,1,0:T(8,128)(2,1)S(1)}, u32[]{:S(2)}, u32[]{:S(2)}) collective-permute-start(bf16[8,32,512]{2,1,0:T(8,128)(2,1)S(1)} %get-tuple-element.26), channel_id=1, source_target_pairs={{1,0},{2,1},{3,2},{4,3},{5,4},{6,5},{7,6},{8,7},{9,8},{10,9},{11,1... | collective-permute-start | bytes 786440 | tf_op jit(solution)/shard_map/ppermute | solution.py:10
  10.9 14.5 %copy-start = (bf16[512,16,32]{0,2,1:T(8,128)(2,1)S(1)}, bf16[512,16,32]{0,2,1:T(8,128)(2,1)}, u32[]{:S(2)}) copy-start(bf16[512,16,32]{0,2,1:T(8,128)(2,1)} %param.7) | copy-start | bytes 1572868
  16.8 26.4 %copy-start.1 = (bf16[512,512]{1,0:T(8,128)(2,1)}, bf16[512,512]{1,0:T(8,128)(2,1)S(1)}, u32[]{:S(2)}) copy-start(bf16[512,512]{1,0:T(8,128)(2,1)S(1)} %fusion.2) | copy-start | bytes 1572868
  16.8 26.4 %collective-permute-start.4 = (bf16[16,32,512]{2,1,0:T(8,128)(2,1)S(1)}, bf16[16,32,512]{2,1,0:T(8,128)(2,1)S(1)}, u32[]{:S(2)}, u32[]{:S(2)}) collective-permute-start(bf16[16,32,512]{2,1,0:T(8,128)(2,1)S(1)} %bitcast.58), channel_id=1, source_target_pairs={{0,1},{1,2},{2,3},{3,4},{4,5},{5,6},{6,7},{7,8},{8,9},{9,10},{10,1... | collective-permute-start | bytes 1572872 | tf_op jit(solution)/shard_map/ppermute | solution.py:10
  18.7 24.5 %collective-permute-start.5 = (bf16[16,32,512]{2,1,0:T(8,128)(2,1)S(1)}, bf16[16,32,512]{2,1,0:T(8,128)(2,1)S(1)}, u32[]{:S(2)}, u32[]{:S(2)}) collective-permute-start(bf16[16,32,512]{2,1,0:T(8,128)(2,1)S(1)} %bitcast.59), channel_id=1, source_target_pairs={{1,0},{2,1},{3,2},{4,3},{5,4},{6,5},{7,6},{8,7},{9,8},{10,9},{11,1... | collective-permute-start | bytes 1572872 | tf_op jit(solution)/shard_map/ppermute | solution.py:10
  25.5 8.3 %collective-permute-start.2 = (bf16[32,8,512]{2,1,0:T(8,128)(2,1)S(1)}, bf16[32,8,512]{2,1,0:T(8,128)(2,1)S(1)}, u32[]{:S(2)}, u32[]{:S(2)}) collective-permute-start(bf16[32,8,512]{2,1,0:T(8,128)(2,1)S(1)} %get-tuple-element.23), channel_id=1, source_target_pairs={{0,32},{32,64},{64,96},{96,128},{128,160},{160,192},{192,224},{1,3... | collective-permute-start | bytes 786440 | tf_op jit(solution)/shard_map/ppermute | solution.py:10
  28.1 15.0 %collective-permute-start.3 = (bf16[32,8,512]{2,1,0:T(8,128)(2,1)S(1)}, bf16[32,8,512]{2,1,0:T(8,128)(2,1)S(1)}, u32[]{:S(2)}, u32[]{:S(2)}) collective-permute-start(bf16[32,8,512]{2,1,0:T(8,128)(2,1)S(1)} %get-tuple-element.24), channel_id=1, source_target_pairs={{32,0},{64,32},{96,64},{128,96},{160,128},{192,160},{224,192},{33,... | collective-permute-start | bytes 786440 | tf_op jit(solution)/shard_map/ppermute | solution.py:10
  43.4 3.2 %copy-start.3 = (bf16[17,17]{1,0:T(8,128)(2,1)S(1)}, bf16[17,17]{1,0:T(8,128)(2,1)}, u32[]{:S(2)}) copy-start(bf16[17,17]{1,0:T(8,128)(2,1)} %param.6) | copy-start | bytes 1738
  44.7 19.1 %collective-permute-start.6 = (bf16[48,16,512]{2,1,0:T(8,128)(2,1)}, bf16[48,16,512]{2,1,0:T(8,128)(2,1)}, u32[]{:S(2)}, u32[]{:S(2)}) collective-permute-start(bf16[48,16,512]{2,1,0:T(8,128)(2,1)} %get-tuple-element.22), channel_id=1, source_target_pairs={{0,32},{32,64},{64,96},{96,128},{128,160},{160,192},{192,224},{1,3... | collective-permute-start | bytes 2359304 | tf_op jit(solution)/shard_map/ppermute | solution.py:10
  47.0 21.2 %collective-permute-start.7 = (bf16[48,16,512]{2,1,0:T(8,128)(2,1)}, bf16[48,16,512]{2,1,0:T(8,128)(2,1)}, u32[]{:S(2)}, u32[]{:S(2)}) collective-permute-start(bf16[48,16,512]{2,1,0:T(8,128)(2,1)} %get-tuple-element.21), channel_id=1, source_target_pairs={{32,0},{64,32},{96,64},{128,96},{160,128},{192,160},{224,192},{33,... | collective-permute-start | bytes 2359304 | tf_op jit(solution)/shard_map/ppermute | solution.py:10
  76.1 2.2 %copy-start.4 = (bf16[4096,512]{1,0:T(8,128)(2,1)S(1)}, bf16[4096,512]{1,0:T(8,128)(2,1)}, u32[]{:S(2)}) copy-start(bf16[4096,512]{1,0:T(8,128)(2,1)} %param.5) | copy-start | bytes 12582916
  76.5 2.0 %copy-start.2 = (bf16[512,512]{1,0:T(8,128)(2,1)S(1)}, bf16[512,512]{1,0:T(8,128)(2,1)}, u32[]{:S(2)}) copy-start(bf16[512,512]{1,0:T(8,128)(2,1)} %copy-done.1) | copy-start | bytes 1572868

commit v14 on v3

--- a/solution.py
+++ b/solution.py
@@ -70,13 +70,13 @@
     spectra = jnp.exp(-opacity).astype(jnp.bfloat16)
     group = 4 if rows % 4 == 0 else rows
     forward = blur_mat(point_spread, group, cols + 2 * h, h)
-    adjoint = blur_mat(point_spread[::-1, ::-1], group, cols, h)
+    adjoint = blur_mat(point_spread[::-1, ::-1], rows, cols, h)
     near = window(spectra.reshape(rows, cols, waves), 2 * h)
     blurred = blur(near, forward, group, rows + 2 * h, cols + 2 * h, h)
     blurred = blurred.reshape(rows + 2 * h, cols + 2 * h, waves)
     residual = (blurred - measured.astype(jnp.float32)).astype(jnp.bfloat16)
     residual = jnp.where(inside(rows, cols, h), residual, jnp.zeros_like(residual))
-    adjoint_field = blur(residual, adjoint, group, rows, cols, h)
+    adjoint_field = blur(residual, adjoint, rows, rows, cols, h)
     tau_grad = (-spectra.astype(jnp.float32) * adjoint_field).astype(jnp.bfloat16)
     coef_grad = lax.dot_general(
         tau_grad, profile_basis, (((1,), (1,)), ((), ())), preferred_element_type=jnp.float32

time: 74.7 us -> 91.5 us (1.22)
  the two profiles are of different devices: /device:TPU:29 before, /device:TPU:30 now
where the time goes in v14:
time: 91.5 us; the launch traced here: 90.6 us
  starting transfers between devices  30.8 us (34%)
  matrix products  25.7 us (28%)
  local copies, waits for them, and re-layouts  17.6 us (19%)
  waiting for transfers between devices  11.6 us (13%)
  other arithmetic  4.72 us (5%)
    ppermute x8, starting transfers between devices, send(): return lax.ppermute(block, axis, pairs)  30.8 us
    ppermute x8, waiting for transfers between devices, send(): return lax.ppermute(block, axis, pairs)  11.6 us
    unnamed x23, local copies, waits for them, and re-layouts  10.9 us
    dot_general x8, matrix products, blur(): jnp.dot(mat, flat[g * win_cols:g * win_cols + span], preferred_element_ty...  9.7 us
    dot_general x1, matrix products, shards(): lax.dot_general(tau_grad, profile_basis, (((1,), (1,)), ((), ())), prefer...  8.95 us
    dot_general x1, matrix products, shards(): jnp.dot(coefficients.reshape(rows * cols, profiles), profile_basis, prefe...  5.84 us
    concatenate x2, other arithmetic, window(): return jnp.concatenate([left, band, right], axis=1)  3.66 us
    reshape x2, local copies, waits for them, and re-layouts, blur_mat(): strip = strip.astype(psf.dtype).reshape(cols, k * win_cols)  1.96 us
  transfers between devices with their start and end apart: 8, of which 2 were waited for; matrix products, arithmetic and copies ran while one was open for 23% of the time, Pallas kernels for 0%

profile of v14, /device:TPU:30, one launch (start us, length us, event | category | flops | bytes accessed | tf_op | source)
XLA Modules:
  0.0 90.6 jit_solution(9509858823041710009)
XLA Ops:
  0.0 5.8 %fusion.9 = bf16[512,512]{1,0:T(8,128)(2,1)S(1)} fusion(bf16[512,4096]{1,0:T(8,128)(2,1)} %bitcast.56, bf16[4096,512]{1,0:T(8,128)(2,1)} %param.5), kind=kOutput, calls=%fused_computation.16 | convolution fusion | flops 2148007936 | bytes 8912896 | tf_op jit(solution)/shard_map/dot_general | solution.py:67
  5.9 1.9 %collective-permute-start = (bf16[16,32,512]{2,1,0:T(8,128)(2,1)S(1)}, bf16[16,32,512]{2,1,0:T(8,128)(2,1)S(1)}, u32[]{:S(2)}, u32[]{:S(2)}) collective-permute-start(bf16[16,32,512]{2,1,0:T(8,128)(2,1)S(1)} %bitcast.43), channel_id=1, source_target_pairs={{0,1},{1,2},{2,3},{3,4},{4,5},{5,6},{6,7},{7,8},{8,9},{9,10},{10,1... | collective-permute-start | bytes 1572872 | tf_op jit(solution)/shard_map/ppermute | solution.py:10
  7.8 7.9 %collective-permute-start.1 = (bf16[16,32,512]{2,1,0:T(8,128)(2,1)S(1)}, bf16[16,32,512]{2,1,0:T(8,128)(2,1)S(1)}, u32[]{:S(2)}, u32[]{:S(2)}) collective-permute-start(bf16[16,32,512]{2,1,0:T(8,128)(2,1)S(1)} %bitcast.44), channel_id=1, source_target_pairs={{1,0},{2,1},{3,2},{4,3},{5,4},{6,5},{7,6},{8,7},{9,8},{10,9},{11,1... | collective-permute-start | bytes 1572872 | tf_op jit(solution)/shard_map/ppermute | solution.py:10
  15.7 0.9 fusion.43
  16.6 1.9 %collective-permute-start.4 = (bf16[8,32,512]{2,1,0:T(8,128)(2,1)}, bf16[8,32,512]{2,1,0:T(8,128)(2,1)S(1)}, u32[]{:S(2)}, u32[]{:S(2)}) collective-permute-start(bf16[8,32,512]{2,1,0:T(8,128)(2,1)} %get-tuple-element.17), channel_id=1, source_target_pairs={{0,1},{1,2},{2,3},{3,4},{4,5},{5,6},{6,7},{7,8},{8,9},{9,10},{10,1... | collective-permute-start | bytes 786440 | tf_op jit(solution)/shard_map/ppermute | solution.py:10
  18.5 6.7 %collective-permute-start.5 = (bf16[8,32,512]{2,1,0:T(8,128)(2,1)}, bf16[8,32,512]{2,1,0:T(8,128)(2,1)S(1)}, u32[]{:S(2)}, u32[]{:S(2)}) collective-permute-start(bf16[8,32,512]{2,1,0:T(8,128)(2,1)} %get-tuple-element.18), channel_id=1, source_target_pairs={{1,0},{2,1},{3,2},{4,3},{5,4},{6,5},{7,6},{8,7},{9,8},{10,9},{11,1... | collective-permute-start | bytes 786440 | tf_op jit(solution)/shard_map/ppermute | solution.py:10
  27.7 0.7 pad_dynamic-update-slice_fusion.12
  29.9 0.7 pad_dynamic-update-slice_fusion.9
  34.2 0.7 pad_dynamic-update-slice_fusion.3
  34.9 0.7 pad_dynamic-update-slice_fusion.2
  36.4 1.0 %fusion.13 = bf16[48,17,64]{2,1,0:T(8,128)(2,1)} fusion(bf16[17,17]{1,0:T(8,128)(2,1)S(1)} %copy-done.3), kind=kOutput, calls=%fused_computation.27 | convolution fusion | flops 1932288 | bytes 105026 | tf_op jit(solution)/shard_map/ab,xbX->xaX/dot_general | solution.py:29
  37.5 1.3 %fusion.42 = (bf16[48,16,512]{2,1,0:T(8,128)(2,1)}, bf16[48,16,512]{2,1,0:T(8,128)(2,1)}) fusion(bf16[48,32,512]{2,1,0:T(8,128)(2,1)S(1)} %pad_maximum_fusion.1), kind=kLoop, calls=%fused_computation.72 | loop fusion | bytes 3145728 | tf_op jit(solution)/shard_map/slice | solution.py:18
  38.8 2.6 %collective-permute-start.2 = (bf16[48,16,512]{2,1,0:T(8,128)(2,1)}, bf16[48,16,512]{2,1,0:T(8,128)(2,1)S(1)}, u32[]{:S(2)}, u32[]{:S(2)}) collective-permute-start(bf16[48,16,512]{2,1,0:T(8,128)(2,1)} %get-tuple-element.13), channel_id=1, source_target_pairs={{0,32},{32,64},{64,96},{96,128},{128,160},{160,192},{192,224},{1,3... | collective-permute-start | bytes 2359304 | tf_op jit(solution)/shard_map/ppermute | solution.py:10
  41.4 3.3 %collective-permute-start.3 = (bf16[48,16,512]{2,1,0:T(8,128)(2,1)}, bf16[48,16,512]{2,1,0:T(8,128)(2,1)}, u32[]{:S(2)}, u32[]{:S(2)}) collective-permute-start(bf16[48,16,512]{2,1,0:T(8,128)(2,1)} %get-tuple-element.14), channel_id=1, source_target_pairs={{32,0},{64,32},{96,64},{128,96},{160,128},{192,160},{224,192},{33,... | collective-permute-start | bytes 2359304 | tf_op jit(solution)/shard_map/ppermute | solution.py:10
  45.1 0.9 pad_maximum_fusion.5
  45.9 4.7 %collective-permute-start.6 = (bf16[32,8,512]{2,1,0:T(8,128)(2,1)}, bf16[32,8,512]{2,1,0:T(8,128)(2,1)}, u32[]{:S(2)}, u32[]{:S(2)}) collective-permute-start(bf16[32,8,512]{2,1,0:T(8,128)(2,1)} %get-tuple-element.15), channel_id=1, source_target_pairs={{0,32},{32,64},{64,96},{96,128},{128,160},{160,192},{192,224},{1,3... | collective-permute-start | bytes 786440 | tf_op jit(solution)/shard_map/ppermute | solution.py:10
  50.6 1.9 %collective-permute-start.7 = (bf16[32,8,512]{2,1,0:T(8,128)(2,1)}, bf16[32,8,512]{2,1,0:T(8,128)(2,1)}, u32[]{:S(2)}, u32[]{:S(2)}) collective-permute-start(bf16[32,8,512]{2,1,0:T(8,128)(2,1)} %get-tuple-element.16), channel_id=1, source_target_pairs={{32,0},{64,32},{96,64},{128,96},{160,128},{192,160},{224,192},{33,... | collective-permute-start | bytes 786440 | tf_op jit(solution)/shard_map/ppermute | solution.py:10
  52.6 1.8 %reshape.69 = bf16[48,1088]{1,0:T(8,128)(2,1)} reshape(bf16[48,17,64]{2,1,0:T(8,128)(2,1)} %fusion.13) | data formatting | bytes 208896 | tf_op jit(solution)/shard_map/reshape | solution.py:30
  55.1 6.8 %collective-permute-done.6 = bf16[32,8,512]{2,1,0:T(8,128)(2,1)} collective-permute-done((bf16[32,8,512]{2,1,0:T(8,128)(2,1)}, bf16[32,8,512]{2,1,0:T(8,128)(2,1)}, u32[]{:S(2)}, u32[]{:S(2)}) %collective-permute-start.6) | collective-permute-done | bytes 262176 | tf_op jit(solution)/shard_map/ppermute | solution.py:10
  61.9 4.8 %collective-permute-done.7 = bf16[32,8,512]{2,1,0:T(8,128)(2,1)} collective-permute-done((bf16[32,8,512]{2,1,0:T(8,128)(2,1)}, bf16[32,8,512]{2,1,0:T(8,128)(2,1)}, u32[]{:S(2)}, u32[]{:S(2)}) %collective-permute-start.7) | collective-permute-done | bytes 262176 | tf_op jit(solution)/shard_map/ppermute | solution.py:10
  66.7 2.3 %pad_maximum_fusion.2 = bf16[32,48,512]{2,1,0:T(8,128)(2,1)} fusion(bf16[32,8,512]{2,1,0:T(8,128)(2,1)} %collective-permute-done.7, bf16[8,32,512]{2,1,0:T(8,128)(2,1)S(1)} %collective-permute-done.5, bf16[16,32,512]{2,1,0:T(8,128)(2,1)S(1)} %bitcast.42, bf16[8,32,512]{2,1,0:T(8,128)(2,1)S(1)} %collective-permute-done.4, ...), kind=kLoop, calls=%fused_computation.7 | loop fusion | flops 7864320 | bytes 3145728 | tf_op jit(solution)/shard_map/concatenate | solution.py:20
  69.0 1.3 %pad_maximum_fusion = bf16[48,64,512]{2,1,0:T(8,128)(2,1)S(1)} fusion(bf16[48,16,512]{2,1,0:T(8,128)(2,1)} %collective-permute-done.3, bf16[16,32,512]{2,1,0:T(8,128)(2,1)S(1)} %collective-permute-done.1, bf16[16,32,512]{2,1,0:T(8,128)(2,1)S(1)} %bitcast.46, bf16[16,32,512]{2,1,0:T(8,128)(2,1)S(1)} %collective-permute-done, ...), kind=kLoop, calls=%fused_computation.1 | loop fusion | flops 15728640 | bytes 6291456 | tf_op jit(solution)/shard_map/concatenate | solution.py:20
  70.4 1.4 %fusion.41 = (bf16[20,64,512]{2,1,0:T(8,128)(2,1)S(1)}, bf16[20,64,512]{2,1,0:T(8,128)(2,1)S(1)}, bf16[20,64,512]{2,1,0:T(8,128)(2,1)S(1)}, bf16[20,64,512]{2,1,...) fusion(bf16[48,64,512]{2,1,0:T(8,128)(2,1)S(1)} %pad_maximum_fusion), kind=kLoop, calls=%fused_computation.71 | loop fusion | bytes 20971520 | tf_op jit(solution)/shard_map/slice | solution.py:45
  71.8 1.2 %convolution_dynamic-update-slice_fusion.7 = f32[1536,512]{1,0:T(8,128)} fusion(bf16[1280,512]{1,0:T(8,128)(2,1)S(1)} %bitcast.55, bf16[48,1088]{1,0:T(8,128)(2,1)S(1)} %copy-done.2), kind=kOutput, calls=%fused_computation.25 | convolution fusion | flops 256573440 | bytes 1808384 | tf_op jit(solution)/shard_map/dot_general | solution.py:45
  73.0 1.2 %convolution_dynamic-update-slice_fusion.6 = f32[1536,512]{1,0:T(8,128)} fusion(f32[1536,512]{1,0:T(8,128)} %convolution_dynamic-update-slice_fusion.7, bf16[1280,512]{1,0:T(8,128)(2,1)S(1)} %bitcast.54, bf16[48,1088]{1,0:T(8,128)(2,1)S(1)} %copy-done.2), kind=kOutput, calls=%fused_computation.24 | convolution fusion | flops 256573440 | bytes 1808384 | tf_op jit(solution)/shard_map/dot_general | solution.py:45
  74.2 1.2 %convolution_dynamic-update-slice_fusion.5 = f32[1536,512]{1,0:T(8,128)} fusion(f32[1536,512]{1,0:T(8,128)} %convolution_dynamic-update-slice_fusion.6, bf16[1280,512]{1,0:T(8,128)(2,1)S(1)} %bitcast.53, bf16[48,1088]{1,0:T(8,128)(2,1)S(1)} %copy-done.2), kind=kOutput, calls=%fused_computation.23 | convolution fusion | flops 256573440 | bytes 1808384 | tf_op jit(solution)/shard_map/dot_general | solution.py:45
  75.4 1.2 %convolution_dynamic-update-slice_fusion.4 = f32[1536,512]{1,0:T(8,128)} fusion(f32[1536,512]{1,0:T(8,128)} %convolution_dynamic-update-slice_fusion.5, bf16[1280,512]{1,0:T(8,128)(2,1)S(1)} %bitcast.52, bf16[48,1088]{1,0:T(8,128)(2,1)S(1)} %copy-done.2), kind=kOutput, calls=%fused_computation.22 | convolution fusion | flops 256573440 | bytes 1808384 | tf_op jit(solution)/shard_map/dot_general | solution.py:45
  76.6 1.2 %convolution_dynamic-update-slice_fusion.3 = f32[1536,512]{1,0:T(8,128)} fusion(f32[1536,512]{1,0:T(8,128)} %convolution_dynamic-update-slice_fusion.4, bf16[1280,512]{1,0:T(8,128)(2,1)S(1)} %bitcast.51, bf16[48,1088]{1,0:T(8,128)(2,1)S(1)} %copy-done.2), kind=kOutput, calls=%fused_computation.21 | convolution fusion | flops 256573440 | bytes 1808384 | tf_op jit(solution)/shard_map/dot_general | solution.py:45
  77.8 1.2 %convolution_dynamic-update-slice_fusion.2 = f32[1536,512]{1,0:T(8,128)} fusion(f32[1536,512]{1,0:T(8,128)} %convolution_dynamic-update-slice_fusion.3, bf16[1280,512]{1,0:T(8,128)(2,1)S(1)} %bitcast.50, bf16[48,1088]{1,0:T(8,128)(2,1)S(1)} %copy-done.2), kind=kOutput, calls=%fused_computation.20 | convolution fusion | flops 256573440 | bytes 1808384 | tf_op jit(solution)/shard_map/dot_general | solution.py:45
  79.0 1.2 %convolution_dynamic-update-slice_fusion.1 = f32[1536,512]{1,0:T(8,128)} fusion(f32[1536,512]{1,0:T(8,128)} %convolution_dynamic-update-slice_fusion.2, bf16[1280,512]{1,0:T(8,128)(2,1)S(1)} %bitcast.49, bf16[48,1088]{1,0:T(8,128)(2,1)S(1)} %copy-done.2), kind=kOutput, calls=%fused_computation.19 | convolution fusion | flops 256573440 | bytes 1808384 | tf_op jit(solution)/shard_map/dot_general | solution.py:45
  80.3 1.2 %convolution_dynamic-update-slice_fusion = f32[1536,512]{1,0:T(8,128)} fusion(f32[1536,512]{1,0:T(8,128)} %convolution_dynamic-update-slice_fusion.1, bf16[1280,512]{1,0:T(8,128)(2,1)S(1)} %bitcast.48, bf16[48,1088]{1,0:T(8,128)(2,1)S(1)} %copy-done.2), kind=kOutput, calls=%fused_computation.18 | convolution fusion | flops 256573440 | bytes 1808384 | tf_op jit(solution)/shard_map/dot_general | solution.py:45
  81.7 9.0 %convolution_convert_fusion = bf16[512,4096]{1,0:T(8,128)(2,1)} fusion(bf16[4096,512]{1,0:T(8,128)(2,1)} %param.5, bf16[512,1536]{1,0:T(8,128)(2,1)} %pad_dynamic-update-slice_fusion, f32[1536,512]{1,0:T(8,128)} %convolution_dynamic-update-slice_fusion, bf16[1536,512]{1,0:T(8,128)(2,1)S(1)} %bitcast.47, pred[1536]{0:T(1024)(128)(4,1)S(1)} %and_and_fusion, ...), kind=kOutput, calls=%fused_computation | convolution fusion | flops 2959081472 | bytes 15205888 | tf_op jit(solution)/shard_map/dot_general | solution.py:81
  (39 shorter events, 9.7 us)
Async XLA Ops:
  0.0 15.7 %copy-start = (bf16[512,16,32]{0,2,1:T(8,128)(2,1)S(1)}, bf16[512,16,32]{0,2,1:T(8,128)(2,1)}, u32[]{:S(2)}) copy-start(bf16[512,16,32]{0,2,1:T(8,128)(2,1)} %param.7) | copy-start | bytes 1572868
  0.0 25.1 %copy-start.3 = (bf16[17,17]{1,0:T(8,128)(2,1)S(1)}, bf16[17,17]{1,0:T(8,128)(2,1)}, u32[]{:S(2)}) copy-start(bf16[17,17]{1,0:T(8,128)(2,1)} %param.6) | copy-start | bytes 1738
  5.9 31.5 %collective-permute-start = (bf16[16,32,512]{2,1,0:T(8,128)(2,1)S(1)}, bf16[16,32,512]{2,1,0:T(8,128)(2,1)S(1)}, u32[]{:S(2)}, u32[]{:S(2)}) collective-permute-start(bf16[16,32,512]{2,1,0:T(8,128)(2,1)S(1)} %bitcast.43), channel_id=1, source_target_pairs={{0,1},{1,2},{2,3},{3,4},{4,5},{5,6},{6,7},{7,8},{8,9},{9,10},{10,1... | collective-permute-start | bytes 1572872 | tf_op jit(solution)/shard_map/ppermute | solution.py:10
  7.8 29.6 %collective-permute-start.1 = (bf16[16,32,512]{2,1,0:T(8,128)(2,1)S(1)}, bf16[16,32,512]{2,1,0:T(8,128)(2,1)S(1)}, u32[]{:S(2)}, u32[]{:S(2)}) collective-permute-start(bf16[16,32,512]{2,1,0:T(8,128)(2,1)S(1)} %bitcast.44), channel_id=1, source_target_pairs={{1,0},{2,1},{3,2},{4,3},{5,4},{6,5},{7,6},{8,7},{9,8},{10,9},{11,1... | collective-permute-start | bytes 1572872 | tf_op jit(solution)/shard_map/ppermute | solution.py:10
  16.6 28.5 %collective-permute-start.4 = (bf16[8,32,512]{2,1,0:T(8,128)(2,1)}, bf16[8,32,512]{2,1,0:T(8,128)(2,1)S(1)}, u32[]{:S(2)}, u32[]{:S(2)}) collective-permute-start(bf16[8,32,512]{2,1,0:T(8,128)(2,1)} %get-tuple-element.17), channel_id=1, source_target_pairs={{0,1},{1,2},{2,3},{3,4},{4,5},{5,6},{6,7},{7,8},{8,9},{9,10},{10,1... | collective-permute-start | bytes 786440 | tf_op jit(solution)/shard_map/ppermute | solution.py:10
  18.5 26.6 %collective-permute-start.5 = (bf16[8,32,512]{2,1,0:T(8,128)(2,1)}, bf16[8,32,512]{2,1,0:T(8,128)(2,1)S(1)}, u32[]{:S(2)}, u32[]{:S(2)}) collective-permute-start(bf16[8,32,512]{2,1,0:T(8,128)(2,1)} %get-tuple-element.18), channel_id=1, source_target_pairs={{1,0},{2,1},{3,2},{4,3},{5,4},{6,5},{7,6},{8,7},{9,8},{10,9},{11,1... | collective-permute-start | bytes 786440 | tf_op jit(solution)/shard_map/ppermute | solution.py:10
  38.8 30.2 %collective-permute-start.2 = (bf16[48,16,512]{2,1,0:T(8,128)(2,1)}, bf16[48,16,512]{2,1,0:T(8,128)(2,1)S(1)}, u32[]{:S(2)}, u32[]{:S(2)}) collective-permute-start(bf16[48,16,512]{2,1,0:T(8,128)(2,1)} %get-tuple-element.13), channel_id=1, source_target_pairs={{0,32},{32,64},{64,96},{96,128},{128,160},{160,192},{192,224},{1,3... | collective-permute-start | bytes 2359304 | tf_op jit(solution)/shard_map/ppermute | solution.py:10
  41.4 27.6 %collective-permute-start.3 = (bf16[48,16,512]{2,1,0:T(8,128)(2,1)}, bf16[48,16,512]{2,1,0:T(8,128)(2,1)}, u32[]{:S(2)}, u32[]{:S(2)}) collective-permute-start(bf16[48,16,512]{2,1,0:T(8,128)(2,1)} %get-tuple-element.14), channel_id=1, source_target_pairs={{32,0},{64,32},{96,64},{128,96},{160,128},{192,160},{224,192},{33,... | collective-permute-start | bytes 2359304 | tf_op jit(solution)/shard_map/ppermute | solution.py:10
  45.9 15.9 %collective-permute-start.6 = (bf16[32,8,512]{2,1,0:T(8,128)(2,1)}, bf16[32,8,512]{2,1,0:T(8,128)(2,1)}, u32[]{:S(2)}, u32[]{:S(2)}) collective-permute-start(bf16[32,8,512]{2,1,0:T(8,128)(2,1)} %get-tuple-element.15), channel_id=1, source_target_pairs={{0,32},{32,64},{64,96},{96,128},{128,160},{160,192},{192,224},{1,3... | collective-permute-start | bytes 786440 | tf_op jit(solution)/shard_map/ppermute | solution.py:10
  50.6 16.1 %collective-permute-start.7 = (bf16[32,8,512]{2,1,0:T(8,128)(2,1)}, bf16[32,8,512]{2,1,0:T(8,128)(2,1)}, u32[]{:S(2)}, u32[]{:S(2)}) collective-permute-start(bf16[32,8,512]{2,1,0:T(8,128)(2,1)} %get-tuple-element.16), channel_id=1, source_target_pairs={{32,0},{64,32},{96,64},{128,96},{160,128},{192,160},{224,192},{33,... | collective-permute-start | bytes 786440 | tf_op jit(solution)/shard_map/ppermute | solution.py:10
  70.4 1.4 %copy-start.2 = (bf16[48,1088]{1,0:T(8,128)(2,1)S(1)}, bf16[48,1088]{1,0:T(8,128)(2,1)}, u32[]{:S(2)}) copy-start(bf16[48,1088]{1,0:T(8,128)(2,1)} %reshape.69) | copy-start | bytes 313348
  80.3 1.4 %copy-start.1 = (bf16[32,48,512]{2,1,0:T(8,128)(2,1)S(1)}, bf16[32,48,512]{2,1,0:T(8,128)(2,1)}, u32[]{:S(2)}) copy-start(bf16[32,48,512]{2,1,0:T(8,128)(2,1)} %pad_maximum_fusion.2) | copy-start | bytes 4718596
